TPU v7x, 256 devices: a whole 4x4x8 slice. The times are simulated.
256 devices in a mesh: layer: 2 (over core), feat: 4 (over x), tok: 32 (over z, y).
Axes of the slice: x: 4, y: 4, z: 8, core: 2. Of those that a mesh axis runs over, the one named last changes fastest.
Arguments:
- resid_in: bfloat16 [8192, 2304], P('tok', 'feat'), may hold values from -6 to 6
- attn_out: bfloat16 [2, 8192, 2304], P('layer', 'tok', 'feat'), may hold values from -4 to 4
- carry_in: bfloat16 [8192, 2304], P('tok', 'feat'), may hold values from -4 to 4
- enc_weight: bfloat16 [2, 2304, 8192], P('layer', None, 'feat'), may hold values from -0.125 to 0.125
- enc_bias: float32 [2, 8192], P('layer', 'feat'), may hold values from -3 to 3
- dec_own: bfloat16 [2, 8192, 2304], P('layer', 'feat', 'tok'), may hold values from -0.125 to 0.125
- dec_next: bfloat16 [2, 8192, 2304], P('layer', 'feat', 'tok'), may hold values from -0.125 to 0.125
- block_list: int32 [2, 64, 32], P('layer', 'tok'), may hold values from 0 to 63, all different within a row
- block_count: int32 [2, 64], P('layer', 'tok'), may hold values from 8 to 32, as said below
Outputs:
- reconstruction: bfloat16 [2, 8192, 2304], P('layer', 'tok', 'feat')
- outgoing: bfloat16 [2, 8192, 2304], P('layer', 'tok', 'feat')
Inputs may be any that keep to these rules, and one draw needn't show every extreme that they name: Each row of block_list names 32 different blocks; only its first block_count entries are in use. `block_count`: some entry equals 32.
All inputs are finite; a program needn't handle non-finite values.
Results may differ from a plain program's by a relative error of at most 0.015.
Values may be sent and summed in bfloat16 or wider, within the bound.
No kernel may reach another device: no remote copies, remote signals or barrier semaphores. Data moves between devices by JAX's collectives and lax.ppermute only.
A program may use at most 128 MiB of HBM per device.

v0:
```python
import jax
import jax.numpy as jnp
from jax import lax
from jax.sharding import PartitionSpec as P

BLOCK = 128
TILE = 128


def from_behind(shard, axis, by):
    length = lax.axis_size(axis)
    pairs = [(i, i + by) for i in range(length) if 0 <= i + by < length]
    return lax.ppermute(shard, axis, pairs)


def block_mask(block_list, block_count, tile_index, feat_index, blocks_dev):
    listed = lax.dynamic_index_in_dim(block_list[0], tile_index, 0, keepdims=False)
    count_now = lax.dynamic_index_in_dim(block_count[0], tile_index, 0, keepdims=False)
    in_use = jnp.arange(listed.shape[0], dtype=jnp.int32) < count_now
    own_blocks = feat_index * blocks_dev + jnp.arange(blocks_dev, dtype=jnp.int32)
    matches = (listed[None, :] == own_blocks[:, None]) & in_use[None, :]
    return jnp.any(matches, axis=1)


def decode_every(gathered, enc_weight, enc_bias, decoders, active):
    preact = (
        jnp.dot(gathered, enc_weight[0], preferred_element_type=jnp.float32) + enc_bias[0][None, :]
    )
    feat_mask = jnp.repeat(active.astype(jnp.float32), BLOCK)
    features = (jax.nn.relu(preact) * feat_mask[None, :]).astype(jnp.bfloat16)
    own_part = jnp.dot(features, decoders[0], preferred_element_type=jnp.float32)
    next_part = jnp.dot(features, decoders[1], preferred_element_type=jnp.float32)
    return jnp.stack([own_part, next_part])


def store_rows(holder, values, row_start, is_valid):
    previous = lax.dynamic_slice_in_dim(holder, row_start, values.shape[0], 0)
    return lax.dynamic_update_slice_in_dim(
        holder, jnp.where(is_valid, values, previous), row_start, 0
    )


def shards(
    resid_in, attn_out, carry_in, enc_weight, enc_bias, dec_own, dec_next, block_list, block_count
):
    layer_count = lax.axis_size("layer")
    section_index = lax.axis_index("layer")
    feat_index = lax.axis_index("feat")
    tile_count = block_count.shape[1]
    columns = resid_in.shape[1]
    blocks_dev = enc_weight.shape[2] // BLOCK
    decoders = (
        lax.all_gather(dec_own[0], "tok", axis=1, tiled=True),
        lax.all_gather(dec_next[0], "tok", axis=1, tiled=True),
    )
    empty_rows = jnp.zeros((resid_in.shape[0], columns), jnp.bfloat16)
    nothing_yet = jnp.zeros((2, TILE, columns), jnp.bfloat16)

    def advance(step_index, state_tuple):
        arrived, recon_holder, outgoing_holder = state_tuple
        tile_index = step_index - section_index
        is_valid = (tile_index >= 0) & (tile_index < tile_count)
        tile_index = jnp.clip(tile_index, 0, tile_count - 1)
        row_start = tile_index * TILE
        first_section = section_index == 0
        residual = jnp.where(
            first_section, lax.dynamic_slice_in_dim(resid_in, row_start, TILE, 0), arrived[0]
        )
        incoming = jnp.where(
            first_section, lax.dynamic_slice_in_dim(carry_in, row_start, TILE, 0), arrived[1]
        )
        gathered = lax.all_gather(residual, "feat", axis=1, tiled=True)
        active = block_mask(block_list, block_count, tile_index, feat_index, blocks_dev)
        zero_terms = jnp.zeros((2, TILE, gathered.shape[1]), jnp.float32)
        terms = lax.cond(
            is_valid,
            lambda source: decode_every(source, enc_weight, enc_bias, decoders, active),
            lambda source: zero_terms,
            gathered,
        )
        summed = lax.psum_scatter(
            terms.astype(jnp.bfloat16), "feat", scatter_dimension=2, tiled=True
        ).astype(jnp.float32)
        attention = lax.dynamic_slice_in_dim(attn_out[0], row_start, TILE, 0)
        recon_now = summed[0] + incoming.astype(jnp.float32)
        new_residual = (
            residual.astype(jnp.float32) + attention.astype(jnp.float32) + recon_now
        ).astype(jnp.bfloat16)
        outgoing_now = summed[1].astype(jnp.bfloat16)
        recon_holder = store_rows(recon_holder, recon_now.astype(jnp.bfloat16), row_start, is_valid)
        outgoing_holder = store_rows(outgoing_holder, outgoing_now, row_start, is_valid)
        arrived = from_behind(jnp.stack([new_residual, outgoing_now]), "layer", 1)
        return (arrived, recon_holder, outgoing_holder)

    finished = lax.fori_loop(
        0, tile_count + layer_count - 1, advance, (nothing_yet, empty_rows, empty_rows)
    )
    return (finished[1][None], finished[2][None])


def solution(mesh):
    return jax.shard_map(
        shards,
        mesh=mesh,
        in_specs=(
            P("tok", "feat"),
            P("layer", "tok", "feat"),
            P("tok", "feat"),
            P("layer", None, "feat"),
            P("layer", "feat"),
            P("layer", "feat", "tok"),
            P("layer", "feat", "tok"),
            P("layer", "tok", None),
            P("layer", "tok"),
        ),
        out_specs=(P("layer", "tok", "feat"), P("layer", "tok", "feat")),
        check_vma=False,
    )
```

profile of v0, /device:TPU:1, one launch (start us, length us, event | category | flops | bytes accessed | tf_op | source)
XLA Modules:
  0.0 485.6 jit_solution(13964440871166911584)
XLA Ops:
  7.2 0.7 all-gather.5.cloned.1.call-update
  7.9 0.7 all-gather.7.cloned.1.call-update
  8.7 108.2 %all-gather.5.cloned.1.call-done = bf16[1,2048,2304]{1,2,0:T(8,128)(2,1)} async-done(((bf16[1,2048,72]{1,2,0:T(8,128)(2,1)}), bf16[1,2048,2304]{1,2,0:T(8,128)(2,1)}) %all-gather.5.cloned.1.call-update) | async-done | bytes 9437200 | tf_op jit(solution)/shard_map/all_gather | solution.py:53
  116.8 12.4 %copy.26 = bf16[2048,2304]{1,0:T(8,128)(2,1)} copy(bf16[2048,2304]{0,1:T(8,128)(2,1)} %bitcast.82) | data formatting | bytes 18874368 | tf_op jit(solution)/shard_map/while | solution.py:95
  129.2 90.5 %all-gather.7.cloned.1.call-done = bf16[1,2048,2304]{1,2,0:T(8,128)(2,1)} async-done(((bf16[1,2048,72]{1,2,0:T(8,128)(2,1)}), bf16[1,2048,2304]{1,2,0:T(8,128)(2,1)}) %all-gather.7.cloned.1.call-update) | async-done | bytes 9437200 | tf_op jit(solution)/shard_map/all_gather | solution.py:54
  219.8 12.8 %copy.27 = bf16[2048,2304]{1,0:T(8,128)(2,1)} copy(bf16[2048,2304]{0,1:T(8,128)(2,1)} %bitcast.83) | data formatting | bytes 18874368 | tf_op jit(solution)/shard_map/while | solution.py:95
  232.7 245.5 %while.19 = (s32[]{:T(128)}, bf16[2,128,576]{1,2,0:T(8,128)(2,1)S(1)}, bf16[256,576]{0,1:T(8,128)(2,1)S(1)}, bf16[256,576]{0,1:T(8,128)(2,1)S(1)}, pred[]{:T(512...) while((s32[]{:T(128)}, ...), condition=%wide.region_5.6_spmd, body=%wide.region_0.5_spmd.sunk | while | flops 3627509248 | bytes 116467488 | solution.py:95
  232.9 11.7 %all_gather.18 = bf16[128,2304]{0,1:T(8,128)(2,1)S(1)} all-gather(bf16[128,576]{0,1:T(8,128)(2,1)S(1)} %bitcast_select_fusion.4), channel_id=1, replica_groups=mesh['layer'=2,'feat'=4,'tok'=32] {'feat'}, dimensions={1}, use_global_device_ids=true | all-gather | bytes 737280 | tf_op jit(solution)/shard_map/while/body/eval_jaxpr/all_gather | solution.py:72
  244.7 2.7 copy.33
  247.4 0.6 dynamic-slice.29
  248.7 59.4 %all-reduce.5.cloned.1.call-done = bf16[2,128,2304]{1,0,2:T(2,128)(2,1)} async-done(((bf16[2,128,2304]{1,0,2:T(2,128)(2,1)}), bf16[2,128,2304]{1,0,2:T(2,128)(2,1)}) %all-reduce.5.cloned.1.call-update) | async-done | bytes 1179664 | tf_op jit(solution)/shard_map/while
  308.0 1.2 constant_dynamic-slice_fusion.4
  309.4 0.2 fusion.30
  309.6 1.3 collective-permute-start
  310.9 2.9 collective-permute-done
  313.8 10.9 %all_gather.18 = bf16[128,2304]{0,1:T(8,128)(2,1)S(1)} all-gather(bf16[128,576]{0,1:T(8,128)(2,1)S(1)} %bitcast_select_fusion.4), channel_id=1, replica_groups=mesh['layer'=2,'feat'=4,'tok'=32] {'feat'}, dimensions={1}, use_global_device_ids=true | all-gather | bytes 737280 | tf_op jit(solution)/shard_map/while/body/eval_jaxpr/all_gather | solution.py:72
  324.8 10.8 %conditional.2 = (bf16[2,128,2304]{2,1,0:T(8,128)(2,1)S(1)}) conditional(s32[]{:T(128)} %convert_element_type.137, () %tuple.76, (bf16[1,2304,2048]{2,1,0:T(8,128)(2,1)}, bf16[128,2304]{0,1:T(8,128)(2,1)S(1)}, f32[1,2048]{1,0:T(1,128)S(1)}, s32[1,2,32]{2,1,0:T(2,128)S(1)}, s32[]{:T(128)}, /*index=5*/s32[]{:T(128)}, s32[16,1]{0,1:T(1,128)S(1)}, ...), branch_computations={%region_1.1_spmd, %region_2.3_spmd} | conditional | flops 3625518592 | bytes 100099104 | solution.py:75
  324.8 0.6 constant_dynamic-slice_fusion
  325.4 0.9 compare_bitcast_fusion
  326.3 0.2 and_reduce_fusion
  326.6 5.8 %fusion.11 = bf16[128,2048]{1,0:T(8,128)(2,1)S(1)} fusion(bf16[128,2304]{0,1:T(8,128)(2,1)S(1)} %get-tuple-element.503, bf16[1,2304,2048]{2,1,0:T(8,128)(2,1)} %get-tuple-element.426, f32[2048]{0:T(1024)S(1)} %broadcast_bitcast_fusion, f32[2048]{0:T(1024)S(1)} %bitcast.86), kind=kOutput, calls=%fused_computation.7 | convolution fusion | flops 1209008128 | bytes 10567680 | tf_op jit(solution)/shard_map/while/body/eval_jaxpr/cond/branch_1_fun/dot_general | solution.py:27
  332.5 1.4 convolution_bitcast_fusion
  334.0 1.4 convolution_bitcast_fusion.1
  335.4 0.1 pad_maximum_fusion
  335.6 2.7 copy.33
  338.3 0.6 dynamic-slice.29
  339.5 52.4 %all-reduce.5.cloned.1.call-done = bf16[2,128,2304]{1,0,2:T(2,128)(2,1)} async-done(((bf16[2,128,2304]{1,0,2:T(2,128)(2,1)}), bf16[2,128,2304]{1,0,2:T(2,128)(2,1)}) %all-reduce.5.cloned.1.call-update) | async-done | bytes 1179664 | tf_op jit(solution)/shard_map/while
  391.9 1.2 constant_dynamic-slice_fusion.4
  393.3 0.2 fusion.30
  393.5 1.3 collective-permute-start
  394.8 2.9 collective-permute-done
  397.7 10.9 %all_gather.18 = bf16[128,2304]{0,1:T(8,128)(2,1)S(1)} all-gather(bf16[128,576]{0,1:T(8,128)(2,1)S(1)} %bitcast_select_fusion.4), channel_id=1, replica_groups=mesh['layer'=2,'feat'=4,'tok'=32] {'feat'}, dimensions={1}, use_global_device_ids=true | all-gather | bytes 737280 | tf_op jit(solution)/shard_map/while/body/eval_jaxpr/all_gather | solution.py:72
  408.7 10.8 %conditional.2 = (bf16[2,128,2304]{2,1,0:T(8,128)(2,1)S(1)}) conditional(s32[]{:T(128)} %convert_element_type.137, () %tuple.76, (bf16[1,2304,2048]{2,1,0:T(8,128)(2,1)}, bf16[128,2304]{0,1:T(8,128)(2,1)S(1)}, f32[1,2048]{1,0:T(1,128)S(1)}, s32[1,2,32]{2,1,0:T(2,128)S(1)}, s32[]{:T(128)}, /*index=5*/s32[]{:T(128)}, s32[16,1]{0,1:T(1,128)S(1)}, ...), branch_computations={%region_1.1_spmd, %region_2.3_spmd} | conditional | flops 3625518592 | bytes 100099104 | solution.py:75
  408.7 0.6 constant_dynamic-slice_fusion
  409.3 0.9 compare_bitcast_fusion
  410.2 0.2 and_reduce_fusion
  410.5 5.8 %fusion.11 = bf16[128,2048]{1,0:T(8,128)(2,1)S(1)} fusion(bf16[128,2304]{0,1:T(8,128)(2,1)S(1)} %get-tuple-element.503, bf16[1,2304,2048]{2,1,0:T(8,128)(2,1)} %get-tuple-element.426, f32[2048]{0:T(1024)S(1)} %broadcast_bitcast_fusion, f32[2048]{0:T(1024)S(1)} %bitcast.86), kind=kOutput, calls=%fused_computation.7 | convolution fusion | flops 1209008128 | bytes 10567680 | tf_op jit(solution)/shard_map/while/body/eval_jaxpr/cond/branch_1_fun/dot_general | solution.py:27
  416.4 1.4 convolution_bitcast_fusion
  417.9 1.4 convolution_bitcast_fusion.1
  419.3 0.1 pad_maximum_fusion
  419.5 2.7 copy.33
  422.2 0.6 dynamic-slice.29
  423.4 49.1 %all-reduce.5.cloned.1.call-done = bf16[2,128,2304]{1,0,2:T(2,128)(2,1)} async-done(((bf16[2,128,2304]{1,0,2:T(2,128)(2,1)}), bf16[2,128,2304]{1,0,2:T(2,128)(2,1)}) %all-reduce.5.cloned.1.call-update) | async-done | bytes 1179664 | tf_op jit(solution)/shard_map/while
  472.5 1.2 constant_dynamic-slice_fusion.4
  473.8 0.2 fusion.30
  474.0 1.3 collective-permute-start
  475.3 2.9 collective-permute-done
  478.3 0.7 copy-done.2
  (74 shorter events, 1.6 us)
Async XLA Ops:
  7.2 109.7 %all-gather.5.cloned.1.call-start = ((), (), s32[]{:S(2)}) async-start(), calls=%async_computation | async-start | bytes 9732096 | tf_op jit(solution)/shard_map/all_gather | solution.py:53
  7.9 211.8 %all-gather.7.cloned.1.call-start = ((), (), s32[]{:S(2)}) async-start(), calls=%async_computation.1 | async-start | bytes 9732096 | tf_op jit(solution)/shard_map/all_gather | solution.py:54
  219.7 12.9 %copy-start.1 = (bf16[256,576]{0,1:T(8,128)(2,1)S(1)}, bf16[256,576]{0,1:T(8,128)(2,1)}, u32[]{:S(2)}) copy-start(bf16[256,576]{0,1:T(8,128)(2,1)} %param.15) | copy-start | bytes 884740
  219.7 13.0 %copy-start.4 = (bf16[1,256,576]{1,2,0:T(8,128)(2,1)S(1)}, bf16[1,256,576]{1,2,0:T(8,128)(2,1)}, u32[]{:S(2)}) copy-start(bf16[1,256,576]{1,2,0:T(8,128)(2,1)} %param.14) | copy-start | bytes 884740
  219.7 13.0 %copy-start.5 = (bf16[256,576]{0,1:T(8,128)(2,1)S(1)}, bf16[256,576]{0,1:T(8,128)(2,1)}, u32[]{:S(2)}) copy-start(bf16[256,576]{0,1:T(8,128)(2,1)} %param.13) | copy-start | bytes 884740
  219.7 13.0 %copy-start.6 = (f32[1,2048]{1,0:T(1,128)S(1)}, f32[1,2048]{1,0:T(1,128)}, u32[]{:S(2)}) copy-start(f32[1,2048]{1,0:T(1,128)} %param.17) | copy-start | bytes 24580
  219.7 13.0 %copy-start.7 = (s32[1,2,32]{2,1,0:T(2,128)S(1)}, s32[1,2,32]{2,1,0:T(2,128)}, u32[]{:S(2)}) copy-start(s32[1,2,32]{2,1,0:T(2,128)} %param.20) | copy-start | bytes 772
  219.7 13.0 %copy-start.8 = (s32[1,2]{1,0:T(1,128)S(1)}, s32[1,2]{1,0:T(1,128)}, u32[]{:S(2)}) copy-start(s32[1,2]{1,0:T(1,128)} %param.21) | copy-start | bytes 28
  219.7 13.0 %copy-start.9 = (u32[256]{0:T(256)S(1)}, u32[256]{0:T(256)}, u32[]{:S(2)}) copy-start(u32[256]{0:T(256)} %constant.151) | copy-start | bytes 3076
  232.7 75.3 %all-reduce.5.cloned.1.call-start = ((), (), s32[]{:S(2)}) async-start(), calls=%async_computation.2 | async-start | bytes 2359296 | tf_op jit(solution)/shard_map/while
  309.6 4.2 collective-permute-start
  313.8 78.2 %all-reduce.5.cloned.1.call-start = ((), (), s32[]{:S(2)}) async-start(), calls=%async_computation.2 | async-start | bytes 2359296 | tf_op jit(solution)/shard_map/while
  324.8 7.7 %copy-start = (bf16[2048,2304]{1,0:T(8,128)(2,1)S(1)}, bf16[2048,2304]{1,0:T(8,128)(2,1)}, u32[]{:S(2)}) copy-start(bf16[2048,2304]{1,0:T(8,128)(2,1)} %get-tuple-element.435) | copy-start | bytes 28311556 | tf_op jit(solution)/shard_map/while/body/eval_jaxpr/cond
  326.6 7.3 %slice-start = ((s8[9437184]{0:T(1024)(128)(4,1)}), s8[4194304]{0:T(1024)(128)(4,1)S(1)}, s32[]{:S(2)}) async-start(s8[9437184]{0:T(1024)(128)(4,1)} %bitcast.80), calls=%async_computation.3 | async-start | bytes 8388608 | tf_op jit(solution)/shard_map/while/body/eval_jaxpr/cond
  326.6 7.3 %slice-start.1 = ((s8[9437184]{0:T(1024)(128)(4,1)}), s8[4194304]{0:T(1024)(128)(4,1)S(1)}, s32[]{:S(2)}) async-start(s8[9437184]{0:T(1024)(128)(4,1)} %bitcast.80), calls=%async_computation.4 | async-start | bytes 8388608 | tf_op jit(solution)/shard_map/while/body/eval_jaxpr/cond
  332.5 1.5 slice-start.2
  393.5 4.2 collective-permute-start
  397.7 74.8 %all-reduce.5.cloned.1.call-start = ((), (), s32[]{:S(2)}) async-start(), calls=%async_computation.2 | async-start | bytes 2359296 | tf_op jit(solution)/shard_map/while
  408.7 7.7 %copy-start = (bf16[2048,2304]{1,0:T(8,128)(2,1)S(1)}, bf16[2048,2304]{1,0:T(8,128)(2,1)}, u32[]{:S(2)}) copy-start(bf16[2048,2304]{1,0:T(8,128)(2,1)} %get-tuple-element.435) | copy-start | bytes 28311556 | tf_op jit(solution)/shard_map/while/body/eval_jaxpr/cond
  410.5 7.3 %slice-start = ((s8[9437184]{0:T(1024)(128)(4,1)}), s8[4194304]{0:T(1024)(128)(4,1)S(1)}, s32[]{:S(2)}) async-start(s8[9437184]{0:T(1024)(128)(4,1)} %bitcast.80), calls=%async_computation.3 | async-start | bytes 8388608 | tf_op jit(solution)/shard_map/while/body/eval_jaxpr/cond
  410.5 7.3 %slice-start.1 = ((s8[9437184]{0:T(1024)(128)(4,1)}), s8[4194304]{0:T(1024)(128)(4,1)S(1)}, s32[]{:S(2)}) async-start(s8[9437184]{0:T(1024)(128)(4,1)} %bitcast.80), calls=%async_computation.4 | async-start | bytes 8388608 | tf_op jit(solution)/shard_map/while/body/eval_jaxpr/cond
  416.4 1.5 slice-start.2
  474.0 4.2 collective-permute-start
  478.3 0.7 copy-start.2
  478.3 0.8 copy-start.3
Sparse Core Ops, SparseCore 0:
  10.5 106.2 all-gather.4
  119.4 100.2 all-gather.6
  247.5 60.4 all-reduce.4
  338.4 53.4 all-reduce.4
  422.3 50.1 all-reduce.4
where the time goes:
time: 486 us
  waiting for transfers between devices  370 us (76%)
  local copies, waits for them, and re-layouts  41.3 us (8%)
  blocking collectives  33.6 us (7%)
  matrix products  17.4 us (4%)
  between operations  13.8 us (3%)
    while x6, waiting for transfers between devices  161 us
    all_gather x1, waiting for transfers between devices, shards(): lax.all_gather(dec_own[0], 'tok', axis=1, tiled=True)  108 us
    all_gather x1, waiting for transfers between devices, shards(): lax.all_gather(dec_next[0], 'tok', axis=1, tiled=True)  90.5 us
    all_gather x3, blocking collectives, advance(): gathered = lax.all_gather(residual, 'feat', axis=1, tiled=True)  33.6 us
    while x2, local copies, waits for them, and re-layouts, shards(): lax.fori_loop(0, tile_count + layer_count - 1, advance, (nothing_yet, emp...  25.2 us
    dot_general x2, matrix products, decode_every(): jnp.dot(gathered, enc_weight[0], preferred_element_type=jnp.float32)  11.7 us
  transfers between devices with their start and end apart: 8, of which 8 were waited for; matrix products, arithmetic and copies ran while one was open for 3% of the time, Pallas kernels for 0%

commit v1 on v0

v1 whole, which is shorter than its diff:
```python
import jax
import jax.numpy as jnp
from jax import lax
from jax.sharding import PartitionSpec as P

BLOCK = 128
TILE = 128
GROUP = ("layer", "feat")


def within_layer(shard, section, shift, n_feat):
    pairs = [
        (section * n_feat + i, section * n_feat + (i + shift) % n_feat) for i in range(n_feat)
    ]
    return lax.ppermute(shard, GROUP, pairs)


def feat_gather(part, section, feat_index, n_feat):
    received = [part] + [within_layer(part, section, k, n_feat) for k in range(1, n_feat)]
    blocks = []
    for j in range(n_feat):
        block = jnp.zeros_like(part)
        for k in range(n_feat):
            block = jnp.where((feat_index - k) % n_feat == j, received[k], block)
        blocks.append(block)
    return jnp.concatenate(blocks, axis=-1)


def feat_reduce_scatter(terms, section, feat_index, n_feat):
    cols = terms.shape[-1] // n_feat
    total = lax.dynamic_slice_in_dim(terms, feat_index * cols, cols, terms.ndim - 1).astype(
        jnp.float32
    )
    for k in range(1, n_feat):
        target = (feat_index + k) % n_feat
        piece = lax.dynamic_slice_in_dim(terms, target * cols, cols, terms.ndim - 1)
        total = total + within_layer(piece, section, k, n_feat).astype(jnp.float32)
    return total


def feature_mask(block_list, block_count, feat_index, blocks_dev):
    listed = block_list[0]
    in_use = jnp.arange(listed.shape[1], dtype=jnp.int32)[None, :] < block_count[0][:, None]
    own_blocks = feat_index * blocks_dev + jnp.arange(blocks_dev, dtype=jnp.int32)
    matches = (listed[:, None, :] == own_blocks[None, :, None]) & in_use[:, None, :]
    active = jnp.any(matches, axis=2).astype(jnp.float32)
    return jnp.repeat(jnp.repeat(active, TILE, axis=0), BLOCK, axis=1)


def decode_every(gathered, enc_weight, enc_bias, decoders, mask):
    preact = (
        jnp.dot(gathered, enc_weight[0], preferred_element_type=jnp.float32) + enc_bias[0][None, :]
    )
    features = (jax.nn.relu(preact) * mask).astype(jnp.bfloat16)
    own_part = jnp.dot(features, decoders[0], preferred_element_type=jnp.float32)
    next_part = jnp.dot(features, decoders[1], preferred_element_type=jnp.float32)
    return jnp.stack([own_part, next_part]).astype(jnp.bfloat16)


def shards(
    resid_in, attn_out, carry_in, enc_weight, enc_bias, dec_own, dec_next, block_list, block_count
):
    layer_count = lax.axis_size("layer")
    n_feat = lax.axis_size("feat")
    section_index = lax.axis_index("layer")
    feat_index = lax.axis_index("feat")
    blocks_dev = enc_weight.shape[2] // BLOCK
    decoders = (
        lax.all_gather(dec_own[0], "tok", axis=1, tiled=True),
        lax.all_gather(dec_next[0], "tok", axis=1, tiled=True),
    )
    mask = feature_mask(block_list, block_count, feat_index, blocks_dev)
    attention = attn_out[0].astype(jnp.float32)

    residual = resid_in
    incoming = carry_in
    recon_out = jnp.zeros_like(resid_in)
    outgoing_out = jnp.zeros_like(resid_in)
    for section in range(layer_count):
        gathered = feat_gather(residual, section, feat_index, n_feat)
        terms = lax.cond(
            section_index == section,
            lambda source: decode_every(source, enc_weight, enc_bias, decoders, mask),
            lambda source: jnp.zeros((2,) + source.shape, jnp.bfloat16),
            gathered,
        )
        summed = feat_reduce_scatter(terms, section, feat_index, n_feat)
        recon_now = summed[0] + incoming.astype(jnp.float32)
        new_residual = (residual.astype(jnp.float32) + attention + recon_now).astype(jnp.bfloat16)
        outgoing_now = summed[1].astype(jnp.bfloat16)
        here = section_index == section
        recon_out = jnp.where(here, recon_now.astype(jnp.bfloat16), recon_out)
        outgoing_out = jnp.where(here, outgoing_now, outgoing_out)
        if section + 1 < layer_count:
            arrived = lax.ppermute(
                jnp.stack([new_residual, outgoing_now]), "layer", [(section, section + 1)]
            )
            residual = arrived[0]
            incoming = arrived[1]
    return (recon_out[None], outgoing_out[None])


def solution(mesh):
    return jax.shard_map(
        shards,
        mesh=mesh,
        in_specs=(
            P("tok", "feat"),
            P("layer", "tok", "feat"),
            P("tok", "feat"),
            P("layer", None, "feat"),
            P("layer", "feat"),
            P("layer", "feat", "tok"),
            P("layer", "feat", "tok"),
            P("layer", "tok", None),
            P("layer", "tok"),
        ),
        out_specs=(P("layer", "tok", "feat"), P("layer", "tok", "feat")),
        check_vma=False,
    )
```

time: 486 us -> 344 us (0.71)
  waiting for transfers between devices: 370 us -> 263 us
  blocking collectives: 33.6 us -> 0 us
  local copies, waits for them, and re-layouts: 41.3 us -> 11.2 us
  starting transfers between devices: 4 us -> 27.2 us
  other arithmetic: 3.52 us -> 11.8 us
    while x6 -> x0, waiting for transfers between devices: 161 us -> none
    ppermute x3 -> x13, waiting for transfers between devices: 8.75 us -> 55.8 us  [the longest x1 39.3 us: shards(): lax.ppermute(jnp.stack([new_residual, outgoing_now]), 'layer', [(section,...]
    all_gather x3 -> x0, blocking collectives: 33.6 us -> none  [advance(): gathered = lax.all_gather(residual, 'feat', axis=1, tiled=True)]
    while x8 -> x0, local copies, waits for them, and re-layouts: 30.6 us -> none  [the longest x2 25.2 us: shards(): lax.fori_loop(0, tile_count + layer_count - 1, advance, (nothing_yet, emp...]
    ppermute x3 -> x13, starting transfers between devices: 3.88 us -> 27.1 us  [the longest x12 25.8 us: within_layer(): return lax.ppermute(shard, GROUP, pairs)]
    all_gather x1, waiting for transfers between devices: 90.5 us -> 103 us  [shards(): lax.all_gather(dec_next[0], 'tok', axis=1, tiled=True)]
    cond x19 -> x7, local copies, waits for them, and re-layouts: 8.28 us -> 2.46 us  [the longest x1 2.45 us: shards(): lax.cond(section_index == section, lambda source: decode_every(source, en...]
    all_gather x1, waiting for transfers between devices: 108 us -> 103 us  [shards(): lax.all_gather(dec_own[0], 'tok', axis=1, tiled=True)]
  transfers between devices with their start and end apart: 8 -> 15, of which waited for: 8 -> 7; matrix products, arithmetic and copies ran while one was open for 3% -> 1% of each run, Pallas kernels for 0% -> 0%
where the time goes in v1:
time: 344 us; the launch traced here: 343 us
  waiting for transfers between devices  263 us (76%)
  starting transfers between devices  27.2 us (8%)
  matrix products  15.5 us (5%)
  between operations  14.4 us (4%)
  other arithmetic  11.8 us (3%)
  local copies, waits for them, and re-layouts  11.2 us (3%)
    all_gather x1, waiting for transfers between devices, shards(): lax.all_gather(dec_next[0], 'tok', axis=1, tiled=True)  103 us
    all_gather x1, waiting for transfers between devices, shards(): lax.all_gather(dec_own[0], 'tok', axis=1, tiled=True)  103 us
    ppermute x1, waiting for transfers between devices, shards(): lax.ppermute(jnp.stack([new_residual, outgoing_now]), 'layer', [(section,...  39.3 us
    ppermute x12, starting transfers between devices, within_layer(): return lax.ppermute(shard, GROUP, pairs)  25.8 us
    ppermute x12, waiting for transfers between devices, within_layer(): return lax.ppermute(shard, GROUP, pairs)  16.5 us
  transfers between devices with their start and end apart: 15, of which 7 were waited for; matrix products, arithmetic and copies ran while one was open for 1% of the time, Pallas kernels for 0%

profile of v1, /device:TPU:1, one launch (start us, length us, event | category | flops | bytes accessed | tf_op | source)
XLA Modules:
  0.0 343.0 jit_solution(14870867963671778885)
XLA Ops:
  7.2 0.7 all-gather.5.cloned.1.call-update
  7.9 0.7 all-gather.7.cloned.1.call-update
  8.6 0.7 collective-permute-start.2
  9.3 0.7 collective-permute-start.1
  10.0 0.7 collective-permute-start
  10.9 0.7 iota_compare_fusion
  11.6 0.9 and_reduce_fusion
  12.5 0.6 broadcast_in_dim.14
  13.1 0.9 copy.63
  14.1 0.1 select_select_fusion.7
  14.2 0.1 pad_maximum_fusion.2
  14.3 102.5 %all-gather.5.cloned.1.call-done = bf16[1,2048,2304]{1,2,0:T(8,128)(2,1)} async-done(((bf16[1,2048,72]{1,2,0:T(8,128)(2,1)}), bf16[1,2048,2304]{1,2,0:T(8,128)(2,1)}) %all-gather.5.cloned.1.call-update) | async-done | bytes 9437200 | tf_op jit(solution)/shard_map/all_gather | solution.py:69
  116.8 102.9 %all-gather.7.cloned.1.call-done = bf16[1,2048,2304]{1,2,0:T(8,128)(2,1)} async-done(((bf16[1,2048,72]{1,2,0:T(8,128)(2,1)}), bf16[1,2048,2304]{1,2,0:T(8,128)(2,1)}) %all-gather.7.cloned.1.call-update) | async-done | bytes 9437200 | tf_op jit(solution)/shard_map/all_gather | solution.py:70
  219.7 1.6 conditional.2
  219.7 1.6 broadcast.29.clone
  221.3 2.4 constant_dynamic-slice_fusion.5
  223.7 1.5 collective-permute-start.3
  225.1 1.5 collective-permute-start.5
  226.6 1.5 collective-permute-start.4
  228.1 1.9 convert_add_fusion.1
  230.1 1.2 fusion.40
  231.3 0.1 pad_maximum_fusion.4
  231.3 1.3 collective-permute-start.6
  232.6 39.3 %collective-permute-done.6 = bf16[2,256,576]{1,2,0:T(8,128)(2,1)} collective-permute-done((bf16[2,256,576]{1,2,0:T(8,128)(2,1)S(1)}, bf16[2,256,576]{1,2,0:T(8,128)(2,1)}, u32[]{:S(2)}, u32[]{:S(2)}) %collective-permute-start.6) | collective-permute-done | bytes 589856 | tf_op jit(solution)/shard_map/ppermute | solution.py:95
  271.9 1.7 slice_bitcast_fusion.1
  273.6 4.5 %collective-permute-start.9 = (bf16[256,576]{0,1:T(8,128)(2,1)}, bf16[256,576]{0,1:T(8,128)(2,1)}, u32[]{:S(2)}, u32[]{:S(2)}) collective-permute-start(bf16[256,576]{0,1:T(8,128)(2,1)} %slice_bitcast_fusion.1), channel_id=1, source_target_pairs={{128,160},{160,192},{192,224},{224,128},{129,161},{161,193},{193,2... | collective-permute-start | bytes 884744 | tf_op jit(solution)/shard_map/ppermute | solution.py:15
  278.1 4.0 %collective-permute-start.8 = (bf16[256,576]{0,1:T(8,128)(2,1)}, bf16[256,576]{0,1:T(8,128)(2,1)}, u32[]{:S(2)}, u32[]{:S(2)}) collective-permute-start(bf16[256,576]{0,1:T(8,128)(2,1)} %slice_bitcast_fusion.1), channel_id=1, source_target_pairs={{128,192},{160,224},{192,128},{224,160},{129,193},{161,225},{193,1... | collective-permute-start | bytes 884744 | tf_op jit(solution)/shard_map/ppermute | solution.py:15
  282.1 2.2 collective-permute-start.7
  284.3 3.4 collective-permute-done.8
  287.7 2.1 collective-permute-done.7
  289.9 1.1 select_select_fusion.2
  291.0 1.4 select_select_fusion.3
  292.4 0.1 pad_maximum_fusion.3
  292.4 18.5 %conditional.3 = (bf16[2,256,2304]{1,2,0:T(8,128)(2,1)}) conditional(s32[]{:T(128)} %convert_element_type.74, () %tuple.20, (bf16[1,2304,2048]{2,1,0:T(8,128)(2,1)}, bf16[256,2304]{0,1:T(8,128)(2,1)S(1)}, f32[1,2048]{1,0:T(1,128)S(1)}, f32[256,2048]{1,0:T(8,128)S(1)}, bf16[2048,2304]{0,1:T(8,128)(2,1)}, /*index=5*/bf16[2048,2304]{0,1:T(8,128)(2,1)}) %tuple.58), branch_computations={%region_3.4_spmd, %region_4.5_spmd} | conditional | flops 7252213760 | bytes 74850384 | solution.py:81
  292.7 6.5 %fusion.29 = bf16[256,2048]{1,0:T(8,128)(2,1)S(1)} fusion(f32[256,2048]{1,0:T(8,128)S(1)} %get-tuple-element.39, bf16[256,2304]{0,1:T(8,128)(2,1)S(1)} %get-tuple-element.75, bf16[1,2304,2048]{2,1,0:T(8,128)(2,1)} %get-tuple-element.37, f32[2048]{0:T(1024)S(1)} %bitcast.93), kind=kOutput, calls=%fused_computation.20 | convolution fusion | flops 2418016256 | bytes 13770752 | tf_op jit(solution)/shard_map/cond/branch_1_fun/dot_general | solution.py:52
  299.1 6.4 %fusion.19 = bf16[1,256,2304]{2,1,0:T(8,128)(2,1)S(1)} fusion(bf16[256,2048]{1,0:T(8,128)(2,1)S(1)} %fusion.29, bf16[2048,2304]{0,1:T(8,128)(2,1)} %get-tuple-element.79), kind=kOutput, calls=%fused_computation.16 | convolution fusion | flops 2416508928 | bytes 11665408 | tf_op jit(solution)/shard_map/cond/branch_1_fun/dot_general | solution.py:56
  305.6 2.7 fusion.18
  308.3 0.2 pad_maximum_fusion.1
  308.5 2.4 copy.60
  310.9 1.5 constant_dynamic-slice_fusion.2
  312.5 2.5 collective-permute-start.10
  315.0 4.0 %collective-permute-start.12 = (bf16[2,256,576]{1,2,0:T(8,128)(2,1)S(1)}, bf16[2,256,576]{1,2,0:T(8,128)(2,1)S(1)}, u32[]{:S(2)}, u32[]{:S(2)}) collective-permute-start(bf16[2,256,576]{1,2,0:T(8,128)(2,1)S(1)} %get-tuple-element.83), channel_id=1, source_target_pairs={{128,224},{160,128},{192,160},{224,192},{129,225},{161,129},{193,1... | collective-permute-start | bytes 1769480 | tf_op jit(solution)/shard_map/ppermute | solution.py:15
  319.0 2.1 collective-permute-start.11
  321.1 3.2 collective-permute-done.10
  324.3 7.8 %collective-permute-done.12 = bf16[2,256,576]{1,2,0:T(8,128)(2,1)S(1)} collective-permute-done((bf16[2,256,576]{1,2,0:T(8,128)(2,1)S(1)}, bf16[2,256,576]{1,2,0:T(8,128)(2,1)S(1)}, u32[]{:S(2)}, u32[]{:S(2)}) %collective-permute-start.12) | collective-permute-done | bytes 589856 | tf_op jit(solution)/shard_map/ppermute | solution.py:15
  332.1 1.4 convert_add_fusion
  333.5 0.8 fusion.42
  334.3 1.8 fusion.39
  (30 shorter events, 0.3 us)
Async XLA Ops:
  7.2 109.7 %all-gather.5.cloned.1.call-start = ((), (), s32[]{:S(2)}) async-start(), calls=%async_computation | async-start | bytes 9732096 | tf_op jit(solution)/shard_map/all_gather | solution.py:69
  7.9 211.8 %all-gather.7.cloned.1.call-start = ((), (), s32[]{:S(2)}) async-start(), calls=%async_computation.1 | async-start | bytes 9732096 | tf_op jit(solution)/shard_map/all_gather | solution.py:70
  8.6 5.3 %collective-permute-start.2 = (bf16[256,576]{0,1:T(8,128)(2,1)}, bf16[256,576]{0,1:T(8,128)(2,1)S(1)}, u32[]{:S(2)}, u32[]{:S(2)}) collective-permute-start(bf16[256,576]{0,1:T(8,128)(2,1)} %param.13), channel_id=1, source_target_pairs={{0,32},{32,64},{64,96},{96,0},{1,33},{33,65},{65,97},{97,1},{2,34}... | collective-permute-start | bytes 884744 | tf_op jit(solution)/shard_map/ppermute | solution.py:15
  9.3 4.7 %collective-permute-start.1 = (bf16[256,576]{0,1:T(8,128)(2,1)}, bf16[256,576]{0,1:T(8,128)(2,1)S(1)}, u32[]{:S(2)}, u32[]{:S(2)}) collective-permute-start(bf16[256,576]{0,1:T(8,128)(2,1)} %param.13), channel_id=1, source_target_pairs={{0,64},{32,96},{64,0},{96,32},{1,65},{33,97},{65,1},{97,33},{2,66}... | collective-permute-start | bytes 884744 | tf_op jit(solution)/shard_map/ppermute | solution.py:15
  10.0 4.0 %collective-permute-start = (bf16[256,576]{0,1:T(8,128)(2,1)}, bf16[256,576]{0,1:T(8,128)(2,1)S(1)}, u32[]{:S(2)}, u32[]{:S(2)}) collective-permute-start(bf16[256,576]{0,1:T(8,128)(2,1)} %param.13), channel_id=1, source_target_pairs={{0,96},{32,0},{64,32},{96,64},{1,97},{33,1},{65,33},{97,65},{2,98}... | collective-permute-start | bytes 884744 | tf_op jit(solution)/shard_map/ppermute | solution.py:15
  13.1 1.0 copy-start
  14.1 205.6 %copy-start.3 = (f32[1,2048]{1,0:T(1,128)S(1)}, f32[1,2048]{1,0:T(1,128)}, u32[]{:S(2)}) copy-start(f32[1,2048]{1,0:T(1,128)} %param.17) | copy-start | bytes 24580
  223.7 4.4 %collective-permute-start.3 = (bf16[2,256,576]{1,2,0:T(8,128)(2,1)}, bf16[2,256,576]{1,2,0:T(8,128)(2,1)}, u32[]{:S(2)}, u32[]{:S(2)}) collective-permute-start(bf16[2,256,576]{1,2,0:T(8,128)(2,1)} %get-tuple-element.85), channel_id=1, source_target_pairs={{0,32},{32,64},{64,96},{96,0},{1,33},{33,65},{65,97},{97,1},{2,34}... | collective-permute-start | bytes 1769480 | tf_op jit(solution)/shard_map/ppermute | solution.py:15
  225.1 3.0 collective-permute-start.5
  226.6 1.5 collective-permute-start.4
  228.1 2.0 copy-start.2
  231.3 40.6 %collective-permute-start.6 = (bf16[2,256,576]{1,2,0:T(8,128)(2,1)S(1)}, bf16[2,256,576]{1,2,0:T(8,128)(2,1)}, u32[]{:S(2)}, u32[]{:S(2)}) collective-permute-start(bf16[2,256,576]{1,2,0:T(8,128)(2,1)S(1)} %pad_maximum_fusion.4), channel_id=1, source_target_pairs={{0,128},{1,129},{2,130},{3,131},{4,132},{5,133},{6,134},{7,135},{8... | collective-permute-start | bytes 1769480 | tf_op jit(solution)/shard_map/ppermute | solution.py:95
  273.6 10.7 %collective-permute-start.9 = (bf16[256,576]{0,1:T(8,128)(2,1)}, bf16[256,576]{0,1:T(8,128)(2,1)}, u32[]{:S(2)}, u32[]{:S(2)}) collective-permute-start(bf16[256,576]{0,1:T(8,128)(2,1)} %slice_bitcast_fusion.1), channel_id=1, source_target_pairs={{128,160},{160,192},{192,224},{224,128},{129,161},{161,193},{193,2... | collective-permute-start | bytes 884744 | tf_op jit(solution)/shard_map/ppermute | solution.py:15
  278.1 9.6 %collective-permute-start.8 = (bf16[256,576]{0,1:T(8,128)(2,1)}, bf16[256,576]{0,1:T(8,128)(2,1)}, u32[]{:S(2)}, u32[]{:S(2)}) collective-permute-start(bf16[256,576]{0,1:T(8,128)(2,1)} %slice_bitcast_fusion.1), channel_id=1, source_target_pairs={{128,192},{160,224},{192,128},{224,160},{129,193},{161,225},{193,1... | collective-permute-start | bytes 884744 | tf_op jit(solution)/shard_map/ppermute | solution.py:15
  282.1 7.8 %collective-permute-start.7 = (bf16[256,576]{0,1:T(8,128)(2,1)}, bf16[256,576]{0,1:T(8,128)(2,1)}, u32[]{:S(2)}, u32[]{:S(2)}) collective-permute-start(bf16[256,576]{0,1:T(8,128)(2,1)} %slice_bitcast_fusion.1), channel_id=1, source_target_pairs={{128,224},{160,128},{192,160},{224,192},{129,225},{161,129},{193,1... | collective-permute-start | bytes 884744 | tf_op jit(solution)/shard_map/ppermute | solution.py:15
  292.6 12.9 %slice-start.3 = ((s8[9437184]{0:T(1024)(128)(4,1)}), s8[4194304]{0:T(1024)(128)(4,1)S(1)}, s32[]{:S(2)}) async-start(s8[9437184]{0:T(1024)(128)(4,1)} %bitcast.99), calls=%async_computation.5 | async-start | bytes 8388608 | tf_op jit(solution)/shard_map/cond
  292.7 12.9 %slice-start.4 = ((s8[9437184]{0:T(1024)(128)(4,1)}), s8[4194304]{0:T(1024)(128)(4,1)S(1)}, s32[]{:S(2)}) async-start(s8[9437184]{0:T(1024)(128)(4,1)} %bitcast.99), calls=%async_computation.6 | async-start | bytes 8388608 | tf_op jit(solution)/shard_map/cond
  299.1 6.4 %slice-start.5 = ((s8[9437184]{0:T(1024)(128)(4,1)}), s8[1048576]{0:T(1024)(128)(4,1)S(1)}, s32[]{:S(2)}) async-start(s8[9437184]{0:T(1024)(128)(4,1)} %bitcast.99), calls=%async_computation.7 | async-start | bytes 2097152 | tf_op jit(solution)/shard_map/cond
  312.5 11.8 %collective-permute-start.10 = (bf16[2,256,576]{1,2,0:T(8,128)(2,1)S(1)}, bf16[2,256,576]{1,2,0:T(8,128)(2,1)S(1)}, u32[]{:S(2)}, u32[]{:S(2)}) collective-permute-start(bf16[2,256,576]{1,2,0:T(8,128)(2,1)S(1)} %get-tuple-element.82), channel_id=1, source_target_pairs={{128,160},{160,192},{192,224},{224,128},{129,161},{161,193},{193,2... | collective-permute-start | bytes 1769480 | tf_op jit(solution)/shard_map/ppermute | solution.py:15
  315.0 17.1 %collective-permute-start.12 = (bf16[2,256,576]{1,2,0:T(8,128)(2,1)S(1)}, bf16[2,256,576]{1,2,0:T(8,128)(2,1)S(1)}, u32[]{:S(2)}, u32[]{:S(2)}) collective-permute-start(bf16[2,256,576]{1,2,0:T(8,128)(2,1)S(1)} %get-tuple-element.83), channel_id=1, source_target_pairs={{128,224},{160,128},{192,160},{224,192},{129,225},{161,129},{193,1... | collective-permute-start | bytes 1769480 | tf_op jit(solution)/shard_map/ppermute | solution.py:15
  319.0 15.3 %copy-start.1 = (bf16[256,576]{0,1:T(8,128)(2,1)S(1)}, bf16[256,576]{0,1:T(8,128)(2,1)}, u32[]{:S(2)}) copy-start(bf16[256,576]{0,1:T(8,128)(2,1)} %param.15) | copy-start | bytes 884740
  319.0 13.1 %collective-permute-start.11 = (bf16[2,256,576]{1,2,0:T(8,128)(2,1)S(1)}, bf16[2,256,576]{1,2,0:T(8,128)(2,1)S(1)}, u32[]{:S(2)}, u32[]{:S(2)}) collective-permute-start(bf16[2,256,576]{1,2,0:T(8,128)(2,1)S(1)} %get-tuple-element.84), channel_id=1, source_target_pairs={{128,192},{160,224},{192,128},{224,160},{129,193},{161,225},{193,1... | collective-permute-start | bytes 1769480 | tf_op jit(solution)/shard_map/ppermute | solution.py:15
Sparse Core Ops, SparseCore 0:
  10.5 106.2 all-gather.4
  119.4 100.2 all-gather.6

commit v2 on v1

--- a/solution.py
+++ b/solution.py
@@ -9,6 +9,8 @@
 
 
 def within_layer(shard, section, shift, n_feat):
+    if section is None:
+        return lax.ppermute(shard, "feat", [(i, (i + shift) % n_feat) for i in range(n_feat)])
     pairs = [
         (section * n_feat + i, section * n_feat + (i + shift) % n_feat) for i in range(n_feat)
     ]
@@ -47,56 +49,60 @@
     return jnp.repeat(jnp.repeat(active, TILE, axis=0), BLOCK, axis=1)
 
 
-def decode_every(gathered, enc_weight, enc_bias, decoders, mask):
+def encode(gathered, enc_weight, enc_bias, mask):
     preact = (
         jnp.dot(gathered, enc_weight[0], preferred_element_type=jnp.float32) + enc_bias[0][None, :]
     )
-    features = (jax.nn.relu(preact) * mask).astype(jnp.bfloat16)
-    own_part = jnp.dot(features, decoders[0], preferred_element_type=jnp.float32)
-    next_part = jnp.dot(features, decoders[1], preferred_element_type=jnp.float32)
-    return jnp.stack([own_part, next_part]).astype(jnp.bfloat16)
+    return (jax.nn.relu(preact) * mask).astype(jnp.bfloat16)
 
 
 def shards(
     resid_in, attn_out, carry_in, enc_weight, enc_bias, dec_own, dec_next, block_list, block_count
 ):
-    layer_count = lax.axis_size("layer")
     n_feat = lax.axis_size("feat")
     section_index = lax.axis_index("layer")
     feat_index = lax.axis_index("feat")
     blocks_dev = enc_weight.shape[2] // BLOCK
-    decoders = (
-        lax.all_gather(dec_own[0], "tok", axis=1, tiled=True),
-        lax.all_gather(dec_next[0], "tok", axis=1, tiled=True),
-    )
+    first_core = section_index == 0
+    first_dec = jnp.where(first_core, dec_own[0], lax.ppermute(dec_next[0], "layer", [(0, 1)]))
+    second_dec = jnp.where(first_core, lax.ppermute(dec_next[0], "layer", [(1, 0)]), dec_own[0])
+    first_full = lax.all_gather(first_dec, "tok", axis=1, tiled=True)
+    second_full = lax.all_gather(second_dec, "tok", axis=1, tiled=True)
     mask = feature_mask(block_list, block_count, feat_index, blocks_dev)
     attention = attn_out[0].astype(jnp.float32)
 
-    residual = resid_in
-    incoming = carry_in
-    recon_out = jnp.zeros_like(resid_in)
-    outgoing_out = jnp.zeros_like(resid_in)
-    for section in range(layer_count):
-        gathered = feat_gather(residual, section, feat_index, n_feat)
-        terms = lax.cond(
-            section_index == section,
-            lambda source: decode_every(source, enc_weight, enc_bias, decoders, mask),
-            lambda source: jnp.zeros((2,) + source.shape, jnp.bfloat16),
-            gathered,
-        )
-        summed = feat_reduce_scatter(terms, section, feat_index, n_feat)
-        recon_now = summed[0] + incoming.astype(jnp.float32)
-        new_residual = (residual.astype(jnp.float32) + attention + recon_now).astype(jnp.bfloat16)
-        outgoing_now = summed[1].astype(jnp.bfloat16)
-        here = section_index == section
-        recon_out = jnp.where(here, recon_now.astype(jnp.bfloat16), recon_out)
-        outgoing_out = jnp.where(here, outgoing_now, outgoing_out)
-        if section + 1 < layer_count:
-            arrived = lax.ppermute(
-                jnp.stack([new_residual, outgoing_now]), "layer", [(section, section + 1)]
-            )
-            residual = arrived[0]
-            incoming = arrived[1]
+    gathered = feat_gather(resid_in, 0, feat_index, n_feat)
+    features = lax.cond(
+        first_core,
+        lambda source: encode(source, enc_weight, enc_bias, mask),
+        lambda source: jnp.zeros((source.shape[0], enc_weight.shape[2]), jnp.bfloat16),
+        gathered,
+    )
+    features = jnp.where(first_core, features, lax.ppermute(features, "layer", [(0, 1)]))
+    part = jnp.dot(features, first_full, preferred_element_type=jnp.float32).astype(jnp.bfloat16)
+    summed = feat_reduce_scatter(part, None, feat_index, n_feat)
+    recon_first = summed + carry_in.astype(jnp.float32)
+    residual_next = (resid_in.astype(jnp.float32) + attention + recon_first).astype(jnp.bfloat16)
+    outgoing_first = summed.astype(jnp.bfloat16)
+    swapped = lax.ppermute(
+        jnp.where(first_core, residual_next, outgoing_first), "layer", [(0, 1), (1, 0)]
+    )
+
+    gathered = feat_gather(swapped, 1, feat_index, n_feat)
+    features = lax.cond(
+        first_core,
+        lambda source: jnp.zeros((source.shape[0], enc_weight.shape[2]), jnp.bfloat16),
+        lambda source: encode(source, enc_weight, enc_bias, mask),
+        gathered,
+    )
+    features = jnp.where(first_core, lax.ppermute(features, "layer", [(1, 0)]), features)
+    part = jnp.dot(features, second_full, preferred_element_type=jnp.float32).astype(jnp.bfloat16)
+    summed = feat_reduce_scatter(part, None, feat_index, n_feat)
+    recon_second = summed + outgoing_first.astype(jnp.float32)
+    outgoing_second = lax.ppermute(summed.astype(jnp.bfloat16), "layer", [(0, 1)])
+
+    recon_out = jnp.where(first_core, recon_first, recon_second).astype(jnp.bfloat16)
+    outgoing_out = jnp.where(first_core, swapped, outgoing_second)
     return (recon_out[None], outgoing_out[None])
 
 

time: 344 us -> 263 us (0.76)
  waiting for transfers between devices: 263 us -> 167 us
  starting transfers between devices: 27.2 us -> 36.8 us
  matrix products: 15.5 us -> 22.2 us
  other arithmetic: 11.8 us -> 6.34 us
  local copies, waits for them, and re-layouts: 11.2 us -> 15 us
    all_gather x2, waiting for transfers between devices: 205 us -> 112 us  [the longest x1 68.7 us: shards(): first_full = lax.all_gather(first_dec, 'tok', axis=1, tiled=True)]
    ppermute x1 -> x12, starting transfers between devices: 1.29 us -> 23 us  [the longest x6 9.61 us: within_layer(): lax.ppermute(shard, 'feat', [(i, (i + shift) % n_feat) for i in range(n_f...]
    ppermute x12 -> x6, waiting for transfers between devices: 16.5 us -> 4 us  [within_layer(): return lax.ppermute(shard, GROUP, pairs)]
    ppermute x12 -> x6, starting transfers between devices: 25.8 us -> 13.8 us  [within_layer(): return lax.ppermute(shard, GROUP, pairs)]
    ppermute x1 -> x12, waiting for transfers between devices: 39.3 us -> 50.3 us  [the longest x6 24.1 us: within_layer(): lax.ppermute(shard, 'feat', [(i, (i + shift) % n_feat) for i in range(n_f...]
    dot_general x3, matrix products: 15.5 us -> 22.2 us  [the longest x1 8.8 us: encode(): jnp.dot(gathered, enc_weight[0], preferred_element_type=jnp.float32)]
    concatenate x0 -> x2, local copies, waits for them, and re-layouts: none -> 6.35 us  [feat_gather(): return jnp.concatenate(blocks, axis=-1)]
    unnamed x9 -> x24, local copies, waits for them, and re-layouts: 0.92 us -> 6.11 us
  transfers between devices with their start and end apart: 15 -> 20, of which waited for: 7 -> 15; matrix products, arithmetic and copies ran while one was open for 1% -> 12% of each run, Pallas kernels for 0% -> 0%
where the time goes in v2:
time: 263 us; the launch traced here: 262 us
  waiting for transfers between devices  167 us (63%)
  starting transfers between devices  36.8 us (14%)
  matrix products  22.2 us (8%)
  local copies, waits for them, and re-layouts  15 us (6%)
  between operations  14.3 us (5%)
  other arithmetic  6.34 us (2%)
    all_gather x1, waiting for transfers between devices, shards(): first_full = lax.all_gather(first_dec, 'tok', axis=1, tiled=True)  68.7 us
    all_gather x1, waiting for transfers between devices, shards(): second_full = lax.all_gather(second_dec, 'tok', axis=1, tiled=True)  43.7 us
    ppermute x6, waiting for transfers between devices, within_layer(): lax.ppermute(shard, 'feat', [(i, (i + shift) % n_feat) for i in range(n_f...  24.1 us
    ppermute x1, waiting for transfers between devices, shards(): lax.ppermute(features, 'layer', [(0, 1)])  20.4 us
    ppermute x6, starting transfers between devices, within_layer(): return lax.ppermute(shard, GROUP, pairs)  13.8 us
    ppermute x6, starting transfers between devices, within_layer(): lax.ppermute(shard, 'feat', [(i, (i + shift) % n_feat) for i in range(n_f...  9.61 us
    dot_general x1, matrix products, encode(): jnp.dot(gathered, enc_weight[0], preferred_element_type=jnp.float32)  8.8 us
    dot_general x1, matrix products, shards(): jnp.dot(features, second_full, preferred_element_type=jnp.float32)  6.72 us
  transfers between devices with their start and end apart: 20, of which 15 were waited for; matrix products, arithmetic and copies ran while one was open for 12% of the time, Pallas kernels for 0%

profile of v2, /device:TPU:1, one launch (start us, length us, event | category | flops | bytes accessed | tf_op | source)
XLA Modules:
  0.0 262.1 jit_solution(61151270122451124)
XLA Ops:
  7.2 5.3 %collective-permute-start.13 = (bf16[2048,72]{0,1:T(8,128)(2,1)}, bf16[2048,72]{0,1:T(8,128)(2,1)S(1)}, u32[]{:S(2)}, u32[]{:S(2)}) collective-permute-start(bf16[2048,72]{0,1:T(8,128)(2,1)} %bitcast.51), channel_id=1, source_target_pairs={{128,0},{129,1},{130,2},{131,3},{132,4},{133,5},{134,6},{135,7},{1... | collective-permute-start | bytes 884744 | tf_op jit(solution)/shard_map/ppermute | solution.py:68
  12.5 1.3 collective-permute-start.4
  13.9 2.3 collective-permute-done.4
  16.2 1.8 bitcast_select_fusion.1
  18.1 0.7 all-gather.5.cloned.1.call-update
  19.0 0.7 collective-permute-start
  19.7 0.7 collective-permute-start.1
  20.4 1.4 collective-permute-start.2
  22.1 0.6 broadcast_in_dim.16
  22.7 0.9 copy.37
  23.7 0.7 copy-done.1
  24.6 2.1 select_select_fusion.4
  26.7 3.1 %concatenate.6 = bf16[256,2304]{1,0:T(8,128)(2,1)} concatenate(bf16[256,576]{1,0:T(8,128)(2,1)S(1)} %select_select_fusion.7, bf16[256,576]{1,0:T(8,128)(2,1)} %get-tuple-element.43, bf16[256,576]{1,0:T(8,128)(2,1)S(1)} %get-tuple-element.42, bf16[256,576]{1,0:T(8,128)(2,1)S(1)} %get-tuple-element.41), dimensions={1} | concatenate | bytes 2359296 | tf_op jit(solution)/shard_map/concatenate | solution.py:28
  29.9 1.3 collective-permute-start.3
  31.3 20.4 %collective-permute-done.3 = bf16[256,2048]{1,0:T(8,128)(2,1)S(1)} collective-permute-done((bf16[256,2048]{1,0:T(8,128)(2,1)S(1)}, bf16[256,2048]{1,0:T(8,128)(2,1)S(1)}, u32[]{:S(2)}, u32[]{:S(2)}) %collective-permute-start.3) | collective-permute-done | bytes 1048608 | tf_op jit(solution)/shard_map/ppermute | solution.py:81
  51.7 1.0 copy-done.6
  52.7 68.7 %all-gather.3.cloned.1.call-done = bf16[2048,2304]{0,1:T(8,128)(2,1)} async-done(((bf16[2048,72]{0,1:T(8,128)(2,1)}), bf16[2048,2304]{0,1:T(8,128)(2,1)}) %all-gather.3.cloned.1.call-update) | async-done | bytes 9437200 | tf_op jit(solution)/shard_map/all_gather | solution.py:69
  121.4 6.7 %convolution_convert_fusion.1 = bf16[256,2304]{1,0:T(8,128)(2,1)S(1)} fusion(bf16[2048,2304]{0,1:T(8,128)(2,1)} %all-gather.3.cloned.1.call-done, bf16[256,2048]{1,0:T(8,128)(2,1)S(1)} %get-tuple-element.52, bf16[256,2048]{1,0:T(8,128)(2,1)} %copy-done.6, pred[]{:T(512)S(6)} %eq.121), kind=kOutput, calls=%fused_computation.13 | convolution fusion | flops 2417033216 | bytes 12713985 | tf_op jit(solution)/shard_map/dot_general | solution.py:82
  128.1 1.3 constant_dynamic-slice_fusion.5
  129.5 1.2 collective-permute-start.5
  130.6 2.4 collective-permute-start.6
  133.0 1.2 collective-permute-start.7
  134.4 1.2 copy.32
  135.6 3.5 %collective-permute-done.5 = bf16[256,576]{1,0:T(8,128)(2,1)S(1)} collective-permute-done((bf16[256,576]{1,0:T(8,128)(2,1)}, bf16[256,576]{1,0:T(8,128)(2,1)S(1)}, u32[]{:S(2)}, u32[]{:S(2)}) %collective-permute-start.5) | collective-permute-done | bytes 294944 | tf_op jit(solution)/shard_map/ppermute | solution.py:13
  139.1 7.9 %collective-permute-done.6 = bf16[256,576]{1,0:T(8,128)(2,1)S(1)} collective-permute-done((bf16[256,576]{1,0:T(8,128)(2,1)}, bf16[256,576]{1,0:T(8,128)(2,1)S(1)}, u32[]{:S(2)}, u32[]{:S(2)}) %collective-permute-start.6) | collective-permute-done | bytes 294944 | tf_op jit(solution)/shard_map/ppermute | solution.py:13
  147.5 1.9 collective-permute-start.8
  149.4 1.3 collective-permute-done.8
  150.7 4.5 %collective-permute-start.10 = (bf16[256,576]{1,0:T(8,128)(2,1)S(1)}, bf16[256,576]{1,0:T(8,128)(2,1)S(1)}, u32[]{:S(2)}, u32[]{:S(2)}) collective-permute-start(bf16[256,576]{1,0:T(8,128)(2,1)S(1)} %collective-permute-done.8), channel_id=1, source_target_pairs={{128,192},{160,224},{192,128},{224,160},{129,193},{161,225},{193,1... | collective-permute-start | bytes 884744 | tf_op jit(solution)/shard_map/ppermute | solution.py:17
  155.1 2.1 collective-permute-start.11
  157.3 4.4 %collective-permute-start.9 = (bf16[256,576]{1,0:T(8,128)(2,1)S(1)}, bf16[256,576]{1,0:T(8,128)(2,1)S(1)}, u32[]{:S(2)}, u32[]{:S(2)}) collective-permute-start(bf16[256,576]{1,0:T(8,128)(2,1)S(1)} %collective-permute-done.8), channel_id=1, source_target_pairs={{128,224},{160,128},{192,160},{224,192},{129,225},{161,129},{193,1... | collective-permute-start | bytes 884744 | tf_op jit(solution)/shard_map/ppermute | solution.py:17
  161.7 2.8 %collective-permute-done.11 = bf16[256,576]{1,0:T(8,128)(2,1)S(1)} collective-permute-done((bf16[256,576]{1,0:T(8,128)(2,1)S(1)}, bf16[256,576]{1,0:T(8,128)(2,1)S(1)}, u32[]{:S(2)}, u32[]{:S(2)}) %collective-permute-start.11) | collective-permute-done | bytes 294944 | tf_op jit(solution)/shard_map/ppermute | solution.py:17
  164.4 1.2 collective-permute-done.9
  165.7 1.0 select_select_fusion
  166.7 3.2 %concatenate.7 = bf16[256,2304]{1,0:T(8,128)(2,1)} concatenate(bf16[256,576]{1,0:T(8,128)(2,1)S(1)} %select_select_fusion.3, bf16[256,576]{1,0:T(8,128)(2,1)} %get-tuple-element.40, bf16[256,576]{1,0:T(8,128)(2,1)} %get-tuple-element.39, bf16[256,576]{1,0:T(8,128)(2,1)S(1)} %get-tuple-element.38), dimensions={1} | concatenate | bytes 2359296 | tf_op jit(solution)/shard_map/concatenate | solution.py:28
  170.0 8.8 %conditional.3 = (bf16[256,2048]{1,0:T(8,128)(2,1)}) conditional(s32[]{:T(128)} %convert_element_type.70, (bf16[1,2304,2048]{2,1,0:T(8,128)(2,1)}, bf16[256,2304]{1,0:T(8,128)(2,1)}, f32[1,2048]{1,0:T(1,128)S(1)}, f32[256,2048]{1,0:T(8,128)}) %tuple.48, () %tuple.23), branch_computations={%region_3.4_spmd, %region_4.5_spmd} | conditional | flops 2418016256 | bytes 13770760 | solution.py:92
  170.0 8.8 %fusion.25 = bf16[256,2048]{1,0:T(8,128)(2,1)} fusion(f32[256,2048]{1,0:T(8,128)} %get-tuple-element.29, bf16[256,2304]{1,0:T(8,128)(2,1)} %get-tuple-element.26, bf16[1,2304,2048]{2,1,0:T(8,128)(2,1)} %get-tuple-element.27, f32[2048]{0:T(1024)S(1)} %bitcast.54), kind=kOutput, calls=%fused_computation.11 | convolution fusion | flops 2418016256 | bytes 13770752 | tf_op jit(solution)/shard_map/cond/branch_0_fun/dot_general | solution.py:54
  178.8 2.3 collective-permute-start.12
  181.1 43.7 %all-gather.5.cloned.1.call-done = bf16[2048,2304]{0,1:T(8,128)(2,1)} async-done(((bf16[2048,72]{0,1:T(8,128)(2,1)}), bf16[2048,2304]{0,1:T(8,128)(2,1)}) %all-gather.5.cloned.1.call-update) | async-done | bytes 9437200 | tf_op jit(solution)/shard_map/all_gather | solution.py:70
  224.8 6.7 %convolution_convert_fusion = bf16[256,2304]{1,0:T(8,128)(2,1)S(1)} fusion(bf16[2048,2304]{0,1:T(8,128)(2,1)} %all-gather.5.cloned.1.call-done, bf16[256,2048]{1,0:T(8,128)(2,1)} %collective-permute-done.12, bf16[256,2048]{1,0:T(8,128)(2,1)} %get-tuple-element.53, pred[]{:T(512)S(6)} %eq.121), kind=kOutput, calls=%fused_computation.12 | convolution fusion | flops 2417033216 | bytes 12713985 | tf_op jit(solution)/shard_map/dot_general | solution.py:99
  232.0 1.3 collective-permute-start.14
  233.3 2.4 collective-permute-start.15
  235.7 1.2 collective-permute-start.16
  236.8 4.3 %collective-permute-done.14 = bf16[256,576]{1,0:T(8,128)(2,1)S(1)} collective-permute-done((bf16[256,576]{1,0:T(8,128)(2,1)S(1)}, bf16[256,576]{1,0:T(8,128)(2,1)S(1)}, u32[]{:S(2)}, u32[]{:S(2)}) %collective-permute-start.14) | collective-permute-done | bytes 294944 | tf_op jit(solution)/shard_map/ppermute | solution.py:13
  241.2 7.9 %collective-permute-done.15 = bf16[256,576]{1,0:T(8,128)(2,1)S(1)} collective-permute-done((bf16[256,576]{1,0:T(8,128)(2,1)S(1)}, bf16[256,576]{1,0:T(8,128)(2,1)S(1)}, u32[]{:S(2)}, u32[]{:S(2)}) %collective-permute-start.15) | collective-permute-done | bytes 294944 | tf_op jit(solution)/shard_map/ppermute | solution.py:13
  250.1 1.3 collective-permute-start.17
  251.4 0.9 copy.33
  252.3 2.1 collective-permute-done.17
  254.4 0.9 copy.34
  (42 shorter events, 3.4 us)
Async XLA Ops:
  7.2 11.6 %copy-start.3 = (bf16[256,576]{0,1:T(8,128)(2,1)S(1)}, bf16[256,576]{0,1:T(8,128)(2,1)}, u32[]{:S(2)}) copy-start(bf16[256,576]{0,1:T(8,128)(2,1)} %param.13) | copy-start | bytes 884740
  7.2 14.7 %copy-start.8 = (s32[1,2]{1,0:T(1,128)S(1)}, s32[1,2]{1,0:T(1,128)}, u32[]{:S(2)}) copy-start(s32[1,2]{1,0:T(1,128)} %param.21) | copy-start | bytes 28
  7.2 14.7 %copy-start.5 = (s32[1,2,32]{2,1,0:T(2,128)S(1)}, s32[1,2,32]{2,1,0:T(2,128)}, u32[]{:S(2)}) copy-start(s32[1,2,32]{2,1,0:T(2,128)} %param.20) | copy-start | bytes 772
  7.2 114.2 %all-gather.3.cloned.1.call-start = ((), (), s32[]{:S(2)}) async-start(), calls=%async_computation | async-start | bytes 9732096 | tf_op jit(solution)/shard_map/all_gather | solution.py:69
  7.2 6.6 %collective-permute-start.13 = (bf16[2048,72]{0,1:T(8,128)(2,1)}, bf16[2048,72]{0,1:T(8,128)(2,1)S(1)}, u32[]{:S(2)}, u32[]{:S(2)}) collective-permute-start(bf16[2048,72]{0,1:T(8,128)(2,1)} %bitcast.51), channel_id=1, source_target_pairs={{128,0},{129,1},{130,2},{131,3},{132,4},{133,5},{134,6},{135,7},{1... | collective-permute-start | bytes 884744 | tf_op jit(solution)/shard_map/ppermute | solution.py:68
  12.5 3.7 %collective-permute-start.4 = (bf16[2048,72]{0,1:T(8,128)(2,1)}, bf16[2048,72]{0,1:T(8,128)(2,1)S(1)}, u32[]{:S(2)}, u32[]{:S(2)}) collective-permute-start(bf16[2048,72]{0,1:T(8,128)(2,1)} %bitcast.52), channel_id=1, source_target_pairs={{0,128},{1,129},{2,130},{3,131},{4,132},{5,133},{6,134},{7,135},{8... | collective-permute-start | bytes 884744 | tf_op jit(solution)/shard_map/ppermute | solution.py:67
  18.0 206.8 %all-gather.5.cloned.1.call-start = ((), (), s32[]{:S(2)}) async-start(), calls=%async_computation.1 | async-start | bytes 9732096 | tf_op jit(solution)/shard_map/all_gather | solution.py:70
  19.0 4.6 %collective-permute-start = (bf16[256,576]{1,0:T(8,128)(2,1)S(1)}, bf16[256,576]{1,0:T(8,128)(2,1)S(1)}, u32[]{:S(2)}, u32[]{:S(2)}) collective-permute-start(bf16[256,576]{1,0:T(8,128)(2,1)S(1)} %copy.23), channel_id=1, source_target_pairs={{0,96},{32,0},{64,32},{96,64},{1,97},{33,1},{65,33},{97,65},{2,98}... | collective-permute-start | bytes 884744 | tf_op jit(solution)/shard_map/ppermute | solution.py:17
  19.7 3.9 %collective-permute-start.1 = (bf16[256,576]{1,0:T(8,128)(2,1)S(1)}, bf16[256,576]{1,0:T(8,128)(2,1)S(1)}, u32[]{:S(2)}, u32[]{:S(2)}) collective-permute-start(bf16[256,576]{1,0:T(8,128)(2,1)S(1)} %copy.23), channel_id=1, source_target_pairs={{0,64},{32,96},{64,0},{96,32},{1,65},{33,97},{65,1},{97,33},{2,66}... | collective-permute-start | bytes 884744 | tf_op jit(solution)/shard_map/ppermute | solution.py:17
  20.4 3.3 %collective-permute-start.2 = (bf16[256,576]{1,0:T(8,128)(2,1)S(1)}, bf16[256,576]{1,0:T(8,128)(2,1)}, u32[]{:S(2)}, u32[]{:S(2)}) collective-permute-start(bf16[256,576]{1,0:T(8,128)(2,1)S(1)} %copy.23), channel_id=1, source_target_pairs={{0,32},{32,64},{64,96},{96,0},{1,33},{33,65},{65,97},{97,1},{2,34}... | collective-permute-start | bytes 884744 | tf_op jit(solution)/shard_map/ppermute | solution.py:17
  23.6 6.2 %copy-start = (f32[32,8,16,128]{3,1,2,0:T(8,128)}, f32[32,8,16,128]{3,1,2,0:T(8,128)S(1)}, u32[]{:S(2)}) copy-start(f32[32,8,16,128]{3,1,2,0:T(8,128)S(1)} %copy.37) | copy-start | bytes 6291460
  23.6 0.8 copy-start.1
  23.6 0.9 copy-start.2
  24.6 5.2 %copy-start.7 = (f32[1,2048]{1,0:T(1,128)S(1)}, f32[1,2048]{1,0:T(1,128)}, u32[]{:S(2)}) copy-start(f32[1,2048]{1,0:T(1,128)} %param.17) | copy-start | bytes 24580
  29.9 21.8 %collective-permute-start.3 = (bf16[256,2048]{1,0:T(8,128)(2,1)S(1)}, bf16[256,2048]{1,0:T(8,128)(2,1)S(1)}, u32[]{:S(2)}, u32[]{:S(2)}) collective-permute-start(bf16[256,2048]{1,0:T(8,128)(2,1)S(1)} %get-tuple-element.52), channel_id=1, source_target_pairs={{0,128},{1,129},{2,130},{3,131},{4,132},{5,133},{6,134},{7,135},{8... | collective-permute-start | bytes 3145736 | tf_op jit(solution)/shard_map/ppermute | solution.py:81
  51.7 1.0 copy-start.6
  128.1 6.1 %copy-start.4 = (bf16[256,576]{0,1:T(8,128)(2,1)S(1)}, bf16[256,576]{0,1:T(8,128)(2,1)}, u32[]{:S(2)}) copy-start(bf16[256,576]{0,1:T(8,128)(2,1)} %param.15) | copy-start | bytes 884740
  129.5 9.6 %collective-permute-start.5 = (bf16[256,576]{1,0:T(8,128)(2,1)}, bf16[256,576]{1,0:T(8,128)(2,1)S(1)}, u32[]{:S(2)}, u32[]{:S(2)}) collective-permute-start(bf16[256,576]{1,0:T(8,128)(2,1)} %get-tuple-element.47), channel_id=1, source_target_pairs={{0,32},{32,64},{64,96},{96,0},{1,33},{33,65},{65,97},{97,1},{2,34}... | collective-permute-start | bytes 884744 | tf_op jit(solution)/shard_map/ppermute | solution.py:13
  130.6 16.4 %collective-permute-start.6 = (bf16[256,576]{1,0:T(8,128)(2,1)}, bf16[256,576]{1,0:T(8,128)(2,1)S(1)}, u32[]{:S(2)}, u32[]{:S(2)}) collective-permute-start(bf16[256,576]{1,0:T(8,128)(2,1)} %get-tuple-element.49), channel_id=1, source_target_pairs={{0,64},{32,96},{64,0},{96,32},{1,65},{33,97},{65,1},{97,33},{2,66}... | collective-permute-start | bytes 884744 | tf_op jit(solution)/shard_map/ppermute | solution.py:13
  133.0 14.0 %collective-permute-start.7 = (bf16[256,576]{1,0:T(8,128)(2,1)S(1)}, bf16[256,576]{1,0:T(8,128)(2,1)S(1)}, u32[]{:S(2)}, u32[]{:S(2)}) collective-permute-start(bf16[256,576]{1,0:T(8,128)(2,1)S(1)} %get-tuple-element.48), channel_id=1, source_target_pairs={{0,96},{32,0},{64,32},{96,64},{1,97},{33,1},{65,33},{97,65},{2,98}... | collective-permute-start | bytes 884744 | tf_op jit(solution)/shard_map/ppermute | solution.py:13
  147.5 3.2 %collective-permute-start.8 = (bf16[256,576]{1,0:T(8,128)(2,1)S(1)}, bf16[256,576]{1,0:T(8,128)(2,1)S(1)}, u32[]{:S(2)}, u32[]{:S(2)}) collective-permute-start(bf16[256,576]{1,0:T(8,128)(2,1)S(1)} %fusion.35), channel_id=1, source_target_pairs={{0,128},{128,0},{1,129},{129,1},{2,130},{130,2},{3,131},{131,3},{4... | collective-permute-start | bytes 884744 | tf_op jit(solution)/shard_map/ppermute | solution.py:87
  150.7 11.0 %collective-permute-start.10 = (bf16[256,576]{1,0:T(8,128)(2,1)S(1)}, bf16[256,576]{1,0:T(8,128)(2,1)S(1)}, u32[]{:S(2)}, u32[]{:S(2)}) collective-permute-start(bf16[256,576]{1,0:T(8,128)(2,1)S(1)} %collective-permute-done.8), channel_id=1, source_target_pairs={{128,192},{160,224},{192,128},{224,160},{129,193},{161,225},{193,1... | collective-permute-start | bytes 884744 | tf_op jit(solution)/shard_map/ppermute | solution.py:17
  155.1 9.3 %collective-permute-start.11 = (bf16[256,576]{1,0:T(8,128)(2,1)S(1)}, bf16[256,576]{1,0:T(8,128)(2,1)S(1)}, u32[]{:S(2)}, u32[]{:S(2)}) collective-permute-start(bf16[256,576]{1,0:T(8,128)(2,1)S(1)} %collective-permute-done.8), channel_id=1, source_target_pairs={{128,160},{160,192},{192,224},{224,128},{129,161},{161,193},{193,2... | collective-permute-start | bytes 884744 | tf_op jit(solution)/shard_map/ppermute | solution.py:17
  157.3 8.4 %collective-permute-start.9 = (bf16[256,576]{1,0:T(8,128)(2,1)S(1)}, bf16[256,576]{1,0:T(8,128)(2,1)S(1)}, u32[]{:S(2)}, u32[]{:S(2)}) collective-permute-start(bf16[256,576]{1,0:T(8,128)(2,1)S(1)} %collective-permute-done.8), channel_id=1, source_target_pairs={{128,224},{160,128},{192,160},{224,192},{129,225},{161,129},{193,1... | collective-permute-start | bytes 884744 | tf_op jit(solution)/shard_map/ppermute | solution.py:17
  178.8 46.0 %collective-permute-start.12 = (bf16[256,2048]{1,0:T(8,128)(2,1)}, bf16[256,2048]{1,0:T(8,128)(2,1)}, u32[]{:S(2)}, u32[]{:S(2)}) collective-permute-start(bf16[256,2048]{1,0:T(8,128)(2,1)} %get-tuple-element.53), channel_id=1, source_target_pairs={{128,0},{129,1},{130,2},{131,3},{132,4},{133,5},{134,6},{135,7},{1... | collective-permute-start | bytes 3145736 | tf_op jit(solution)/shard_map/ppermute | solution.py:98
  232.0 9.2 %collective-permute-start.14 = (bf16[256,576]{1,0:T(8,128)(2,1)S(1)}, bf16[256,576]{1,0:T(8,128)(2,1)S(1)}, u32[]{:S(2)}, u32[]{:S(2)}) collective-permute-start(bf16[256,576]{1,0:T(8,128)(2,1)S(1)} %get-tuple-element.44), channel_id=1, source_target_pairs={{0,32},{32,64},{64,96},{96,0},{1,33},{33,65},{65,97},{97,1},{2,34}... | collective-permute-start | bytes 884744 | tf_op jit(solution)/shard_map/ppermute | solution.py:13
  233.3 15.8 %collective-permute-start.15 = (bf16[256,576]{1,0:T(8,128)(2,1)S(1)}, bf16[256,576]{1,0:T(8,128)(2,1)S(1)}, u32[]{:S(2)}, u32[]{:S(2)}) collective-permute-start(bf16[256,576]{1,0:T(8,128)(2,1)S(1)} %get-tuple-element.46), channel_id=1, source_target_pairs={{0,64},{32,96},{64,0},{96,32},{1,65},{33,97},{65,1},{97,33},{2,66}... | collective-permute-start | bytes 884744 | tf_op jit(solution)/shard_map/ppermute | solution.py:13
  235.7 13.8 %collective-permute-start.16 = (bf16[256,576]{1,0:T(8,128)(2,1)S(1)}, bf16[256,576]{1,0:T(8,128)(2,1)S(1)}, u32[]{:S(2)}, u32[]{:S(2)}) collective-permute-start(bf16[256,576]{1,0:T(8,128)(2,1)S(1)} %get-tuple-element.45), channel_id=1, source_target_pairs={{0,96},{32,0},{64,32},{96,64},{1,97},{33,1},{65,33},{97,65},{2,98}... | collective-permute-start | bytes 884744 | tf_op jit(solution)/shard_map/ppermute | solution.py:13
  250.1 4.2 %collective-permute-start.17 = (bf16[256,576]{1,0:T(8,128)(2,1)S(1)}, bf16[256,576]{1,0:T(8,128)(2,1)S(1)}, u32[]{:S(2)}, u32[]{:S(2)}) collective-permute-start(bf16[256,576]{1,0:T(8,128)(2,1)S(1)} %get-tuple-element.36), channel_id=1, source_target_pairs={{0,128},{1,129},{2,130},{3,131},{4,132},{5,133},{6,134},{7,135},{8... | collective-permute-start | bytes 884744 | tf_op jit(solution)/shard_map/ppermute | solution.py:102
Sparse Core Ops, SparseCore 0:
  18.2 103.2 all-gather.2
  124.6 100.1 all-gather.4

commit v3 on v2

--- a/solution.py
+++ b/solution.py
@@ -6,6 +6,7 @@
 BLOCK = 128
 TILE = 128
 GROUP = ("layer", "feat")
+SPLIT = 1024
 
 
 def within_layer(shard, section, shift, n_feat):
@@ -56,6 +57,23 @@
     return (jax.nn.relu(preact) * mask).astype(jnp.bfloat16)
 
 
+def gather_columns(shard):
+    n_tok = lax.axis_size("tok")
+    by_gather = lax.all_gather(shard[:SPLIT], "tok", axis=1, tiled=True)
+    rest = jnp.broadcast_to(shard[SPLIT:][None], (n_tok,) + shard[SPLIT:].shape)
+    by_all_to_all = lax.all_to_all(rest, "tok", 0, 0, tiled=True)
+    return by_gather, by_all_to_all
+
+
+def decode(features, full):
+    by_gather, by_all_to_all = full
+    first = jnp.dot(features[:, :SPLIT], by_gather, preferred_element_type=jnp.float32)
+    second = jnp.einsum(
+        "tf,jfc->tjc", features[:, SPLIT:], by_all_to_all, preferred_element_type=jnp.float32
+    )
+    return (first + second.reshape(first.shape)).astype(jnp.bfloat16)
+
+
 def shards(
     resid_in, attn_out, carry_in, enc_weight, enc_bias, dec_own, dec_next, block_list, block_count
 ):
@@ -66,8 +84,8 @@
     first_core = section_index == 0
     first_dec = jnp.where(first_core, dec_own[0], lax.ppermute(dec_next[0], "layer", [(0, 1)]))
     second_dec = jnp.where(first_core, lax.ppermute(dec_next[0], "layer", [(1, 0)]), dec_own[0])
-    first_full = lax.all_gather(first_dec, "tok", axis=1, tiled=True)
-    second_full = lax.all_gather(second_dec, "tok", axis=1, tiled=True)
+    first_full = gather_columns(first_dec)
+    second_full = gather_columns(second_dec)
     mask = feature_mask(block_list, block_count, feat_index, blocks_dev)
     attention = attn_out[0].astype(jnp.float32)
 
@@ -79,7 +97,7 @@
         gathered,
     )
     features = jnp.where(first_core, features, lax.ppermute(features, "layer", [(0, 1)]))
-    part = jnp.dot(features, first_full, preferred_element_type=jnp.float32).astype(jnp.bfloat16)
+    part = decode(features, first_full)
     summed = feat_reduce_scatter(part, None, feat_index, n_feat)
     recon_first = summed + carry_in.astype(jnp.float32)
     residual_next = (resid_in.astype(jnp.float32) + attention + recon_first).astype(jnp.bfloat16)
@@ -96,7 +114,7 @@
         gathered,
     )
     features = jnp.where(first_core, lax.ppermute(features, "layer", [(1, 0)]), features)
-    part = jnp.dot(features, second_full, preferred_element_type=jnp.float32).astype(jnp.bfloat16)
+    part = decode(features, second_full)
     summed = feat_reduce_scatter(part, None, feat_index, n_feat)
     recon_second = summed + outgoing_first.astype(jnp.float32)
     outgoing_second = lax.ppermute(summed.astype(jnp.bfloat16), "layer", [(0, 1)])

time: 263 us -> 342 us (1.30); the launches traced: 262 us -> 337 us
  waiting for transfers between devices: 167 us -> 215 us
  starting transfers between devices: 36.8 us -> 49.5 us
  local copies, waits for them, and re-layouts: 15 us -> 21.8 us
  matrix products: 22.2 us -> 28.1 us
    all_to_all x0 -> x2, waiting for transfers between devices: none -> 151 us  [gather_columns(): by_all_to_all = lax.all_to_all(rest, 'tok', 0, 0, tiled=True)]
    all_gather x2, waiting for transfers between devices: 112 us -> 0.01 us  [gather_columns(): by_gather = lax.all_gather(shard[:SPLIT], 'tok', axis=1, tiled=True)]
    all_to_all x0 -> x2, starting transfers between devices: none -> 18.4 us  [gather_columns(): by_all_to_all = lax.all_to_all(rest, 'tok', 0, 0, tiled=True)]
    reshape x0 -> x2, matrix products: none -> 10.6 us  [decode(): return (first + second.reshape(first.shape)).astype(jnp.bfloat16)]
    broadcast_in_dim x0 -> x2, local copies, waits for them, and re-layouts: none -> 5.55 us  [gather_columns(): rest = jnp.broadcast_to(shard[SPLIT:][None], (n_tok,) + shard[SPLIT:].shape)]
    ppermute x1, waiting for transfers between devices: 2.07 us -> 7.36 us  [shards(): lax.ppermute(summed.astype(jnp.bfloat16), 'layer', [(0, 1)])]
    dot_general x2, matrix products: 13.4 us -> 9.24 us  [decode(): jnp.dot(features[:, :SPLIT], by_gather, preferred_element_type=jnp.float32)]
    ppermute x6, waiting for transfers between devices: 24.1 us -> 20.5 us  [within_layer(): lax.ppermute(shard, 'feat', [(i, (i + shift) % n_feat) for i in range(n_f...]
  transfers between devices with their start and end apart: 20 -> 22, of which waited for: 15 -> 15; matrix products, arithmetic and copies ran while one was open for 12% -> 14% of each run, Pallas kernels for 0% -> 0%
where the time goes in v3:
time: 342 us; the launch traced here: 337 us
  waiting for transfers between devices  215 us (63%)
  starting transfers between devices  49.5 us (14%)
  matrix products  28.1 us (8%)
  local copies, waits for them, and re-layouts  21.8 us (6%)
  between operations  14.3 us (4%)
  other arithmetic  8.04 us (2%)
    all_to_all x2, waiting for transfers between devices, gather_columns(): by_all_to_all = lax.all_to_all(rest, 'tok', 0, 0, tiled=True)  151 us
    ppermute x1, waiting for transfers between devices, shards(): lax.ppermute(features, 'layer', [(0, 1)])  22.9 us
    ppermute x6, waiting for transfers between devices, within_layer(): lax.ppermute(shard, 'feat', [(i, (i + shift) % n_feat) for i in range(n_f...  20.5 us
    all_to_all x2, starting transfers between devices, gather_columns(): by_all_to_all = lax.all_to_all(rest, 'tok', 0, 0, tiled=True)  18.4 us
    ppermute x6, starting transfers between devices, within_layer(): return lax.ppermute(shard, GROUP, pairs)  11.7 us
    reshape x2, matrix products, decode(): return (first + second.reshape(first.shape)).astype(jnp.bfloat16)  10.6 us
    dot_general x2, matrix products, decode(): jnp.dot(features[:, :SPLIT], by_gather, preferred_element_type=jnp.float32)  9.24 us
    dot_general x1, matrix products, encode(): jnp.dot(gathered, enc_weight[0], preferred_element_type=jnp.float32)  8.24 us
  transfers between devices with their start and end apart: 22, of which 15 were waited for; matrix products, arithmetic and copies ran while one was open for 14% of the time, Pallas kernels for 0%

profile of v3, /device:TPU:1, one launch (start us, length us, event | category | flops | bytes accessed | tf_op | source)
XLA Modules:
  0.0 336.9 jit_solution(10206233065900570939)
XLA Ops:
  7.2 5.1 %collective-permute-start.13 = (bf16[2048,72]{0,1:T(8,128)(2,1)}, bf16[2048,72]{0,1:T(8,128)(2,1)S(1)}, u32[]{:S(2)}, u32[]{:S(2)}) collective-permute-start(bf16[2048,72]{0,1:T(8,128)(2,1)} %bitcast.65), channel_id=1, source_target_pairs={{128,0},{129,1},{130,2},{131,3},{132,4},{133,5},{134,6},{135,7},{1... | collective-permute-start | bytes 884744 | tf_op jit(solution)/shard_map/ppermute | solution.py:86
  12.3 1.3 collective-permute-start.4
  13.7 2.3 collective-permute-done.4
  16.0 1.0 bitcast_select_fusion.1
  17.7 2.7 broadcast_in_dim.14
  20.4 9.6 %all-to-all-start = ((bf16[32,1024,72]{1,2,0:T(8,128)(2,1)}), bf16[32,1024,72]{1,2,0:T(8,128)(2,1)}, u32[]{:S(2)}, u32[]{:S(2)}) async-start(bf16[32,1024,72]{1,2,0:T(8,128)(2,1)} %broadcast_in_dim.14), calls=%async_computation | async-start | bytes 9437184 | tf_op jit(solution)/shard_map/all_to_all | solution.py:64
  31.5 125.5 %all-to-all-done = bf16[32,1024,72]{1,2,0:T(8,128)(2,1)} async-done(((bf16[32,1024,72]{1,2,0:T(8,128)(2,1)}), bf16[32,1024,72]{1,2,0:T(8,128)(2,1)}, u32[]{:S(2)}, u32[]{:S(2)}) %all-to-all-start) | async-done | bytes 4718624 | tf_op jit(solution)/shard_map/all_to_all | solution.py:64
  156.9 2.8 broadcast_in_dim.30
  159.8 8.8 %all-to-all-start.1 = ((bf16[32,1024,72]{1,2,0:T(8,128)(2,1)}), bf16[32,1024,72]{1,2,0:T(8,128)(2,1)}, u32[]{:S(2)}, u32[]{:S(2)}) async-start(bf16[32,1024,72]{1,2,0:T(8,128)(2,1)} %broadcast_in_dim.30), calls=%async_computation.1 | async-start | bytes 9437184 | tf_op jit(solution)/shard_map/all_to_all | solution.py:64
  170.9 1.4 collective-permute-start.2
  173.2 0.9 copy.55
  175.1 2.1 select_select_fusion.4
  177.2 3.1 concatenate.6
  180.5 1.3 collective-permute-start.3
  181.9 22.9 %collective-permute-done.3 = bf16[256,2048]{1,0:T(8,128)(2,1)S(1)} collective-permute-done((bf16[256,2048]{1,0:T(8,128)(2,1)S(1)}, bf16[256,2048]{1,0:T(8,128)(2,1)S(1)}, u32[]{:S(2)}, u32[]{:S(2)}) %collective-permute-start.3) | collective-permute-done | bytes 1048608 | tf_op jit(solution)/shard_map/ppermute | solution.py:99
  204.9 5.3 %fusion.35 = f32[256,2304]{1,0:T(8,128)} fusion(bf16[1024,2304]{0,1:T(8,128)(2,1)} %bitcast.10, bf16[256,2048]{1,0:T(8,128)(2,1)S(1)} %broadcast_select_fusion.1), kind=kOutput, calls=%fused_computation.29 | convolution fusion | flops 1207959552 | bytes 7602176 | tf_op jit(solution)/shard_map/reshape | solution.py:74
  210.1 4.6 %fusion.28 = bf16[256,2304]{1,0:T(8,128)(2,1)S(1)} fusion(f32[256,2304]{1,0:T(8,128)} %fusion.35, bf16[1024,2304]{0,1:T(8,128)(2,1)} %all-gather.3.cloned.1.call-done, bf16[256,2048]{1,0:T(8,128)(2,1)S(1)} %broadcast_select_fusion.1), kind=kOutput, calls=%fused_computation.14 | convolution fusion | flops 1209139200 | bytes 8781824 | tf_op jit(solution)/shard_map/dot_general | solution.py:70
  214.7 1.3 constant_dynamic-slice_fusion.5
  216.0 1.5 collective-permute-start.6
  217.5 1.2 collective-permute-start.7
  218.7 1.2 copy.47
  219.8 1.2 copy.49
  221.0 12.7 %collective-permute-done.5 = bf16[256,576]{1,0:T(8,128)(2,1)S(1)} collective-permute-done((bf16[256,576]{1,0:T(8,128)(2,1)}, bf16[256,576]{1,0:T(8,128)(2,1)S(1)}, u32[]{:S(2)}, u32[]{:S(2)}) %collective-permute-start.5) | collective-permute-done | bytes 294944 | tf_op jit(solution)/shard_map/ppermute | solution.py:14
  234.4 1.2 collective-permute-start.8
  235.7 1.3 collective-permute-done.8
  236.9 2.5 collective-permute-start.10
  239.4 3.7 %collective-permute-start.11 = (bf16[256,576]{1,0:T(8,128)(2,1)S(1)}, bf16[256,576]{1,0:T(8,128)(2,1)S(1)}, u32[]{:S(2)}, u32[]{:S(2)}) collective-permute-start(bf16[256,576]{1,0:T(8,128)(2,1)S(1)} %collective-permute-done.8), channel_id=1, source_target_pairs={{128,160},{160,192},{192,224},{224,128},{129,161},{161,193},{193,2... | collective-permute-start | bytes 884744 | tf_op jit(solution)/shard_map/ppermute | solution.py:18
  243.2 2.8 collective-permute-start.9
  246.6 3.5 %collective-permute-done.11 = bf16[256,576]{1,0:T(8,128)(2,1)S(1)} collective-permute-done((bf16[256,576]{1,0:T(8,128)(2,1)S(1)}, bf16[256,576]{1,0:T(8,128)(2,1)S(1)}, u32[]{:S(2)}, u32[]{:S(2)}) %collective-permute-start.11) | collective-permute-done | bytes 294944 | tf_op jit(solution)/shard_map/ppermute | solution.py:18
  250.1 1.2 collective-permute-done.9
  251.4 1.1 select_select_fusion
  252.5 3.2 concatenate.7
  255.7 8.2 %conditional.3 = (bf16[256,2048]{1,0:T(8,128)(2,1)}) conditional(s32[]{:T(128)} %convert_element_type.70, (bf16[1,2304,2048]{2,1,0:T(8,128)(2,1)}, bf16[256,2304]{1,0:T(8,128)(2,1)}, f32[1,2048]{1,0:T(1,128)S(1)}, f32[256,2048]{1,0:T(8,128)}) %tuple.51, () %tuple.23), branch_computations={%region_3.4_spmd, %region_4.5_spmd} | conditional | flops 2418016256 | bytes 13770760 | solution.py:110
  255.7 8.2 %fusion.25 = bf16[256,2048]{1,0:T(8,128)(2,1)} fusion(f32[256,2048]{1,0:T(8,128)} %get-tuple-element.29, bf16[256,2304]{1,0:T(8,128)(2,1)} %get-tuple-element.26, bf16[1,2304,2048]{2,1,0:T(8,128)(2,1)} %get-tuple-element.27, f32[2048]{0:T(1024)S(1)} %bitcast.68), kind=kOutput, calls=%fused_computation.11 | convolution fusion | flops 2418016256 | bytes 13770752 | tf_op jit(solution)/shard_map/cond/branch_0_fun/dot_general | solution.py:55
  264.0 1.3 collective-permute-start.12
  265.3 2.4 collective-permute-done.12
  267.7 2.4 broadcast_select_fusion
  270.1 26.0 %all-to-all-done.1 = bf16[32,1024,72]{1,2,0:T(8,128)(2,1)} async-done(((bf16[32,1024,72]{1,2,0:T(8,128)(2,1)}), bf16[32,1024,72]{1,2,0:T(8,128)(2,1)}, u32[]{:S(2)}, u32[]{:S(2)}) %all-to-all-start.1) | async-done | bytes 4718624 | tf_op jit(solution)/shard_map/all_to_all | solution.py:64
  296.0 5.3 %fusion.32 = f32[256,2304]{1,0:T(8,128)} fusion(bf16[1024,2304]{0,1:T(8,128)(2,1)} %bitcast.15, bf16[256,2048]{1,0:T(8,128)(2,1)} %broadcast_select_fusion), kind=kOutput, calls=%fused_computation.26 | convolution fusion | flops 1207959552 | bytes 7602176 | tf_op jit(solution)/shard_map/reshape | solution.py:74
  301.4 4.7 %fusion.29 = bf16[256,2304]{1,0:T(8,128)(2,1)S(1)} fusion(f32[256,2304]{1,0:T(8,128)} %fusion.32, bf16[1024,2304]{0,1:T(8,128)(2,1)} %all-gather.5.cloned.1.call-done, bf16[256,2048]{1,0:T(8,128)(2,1)} %broadcast_select_fusion), kind=kOutput, calls=%fused_computation.15 | convolution fusion | flops 1209139200 | bytes 8781824 | tf_op jit(solution)/shard_map/dot_general | solution.py:70
  306.6 1.4 collective-permute-start.14
  307.9 2.5 collective-permute-start.15
  310.4 1.1 collective-permute-start.16
  311.5 2.2 collective-permute-done.14
  313.8 5.2 %collective-permute-done.15 = bf16[256,576]{1,0:T(8,128)(2,1)S(1)} collective-permute-done((bf16[256,576]{1,0:T(8,128)(2,1)S(1)}, bf16[256,576]{1,0:T(8,128)(2,1)S(1)}, u32[]{:S(2)}, u32[]{:S(2)}) %collective-permute-start.15) | collective-permute-done | bytes 294944 | tf_op jit(solution)/shard_map/ppermute | solution.py:14
  319.6 1.3 collective-permute-start.17
  320.9 0.9 copy.51
  321.7 7.4 %collective-permute-done.17 = bf16[256,576]{1,0:T(8,128)(2,1)S(1)} collective-permute-done((bf16[256,576]{1,0:T(8,128)(2,1)S(1)}, bf16[256,576]{1,0:T(8,128)(2,1)S(1)}, u32[]{:S(2)}, u32[]{:S(2)}) %collective-permute-start.17) | collective-permute-done | bytes 294944 | tf_op jit(solution)/shard_map/ppermute | solution.py:120
  (50 shorter events, 10.1 us)
Async XLA Ops:
  7.2 6.5 %collective-permute-start.13 = (bf16[2048,72]{0,1:T(8,128)(2,1)}, bf16[2048,72]{0,1:T(8,128)(2,1)S(1)}, u32[]{:S(2)}, u32[]{:S(2)}) collective-permute-start(bf16[2048,72]{0,1:T(8,128)(2,1)} %bitcast.65), channel_id=1, source_target_pairs={{128,0},{129,1},{130,2},{131,3},{132,4},{133,5},{134,6},{135,7},{1... | collective-permute-start | bytes 884744 | tf_op jit(solution)/shard_map/ppermute | solution.py:86
  12.3 3.7 %collective-permute-start.4 = (bf16[2048,72]{0,1:T(8,128)(2,1)}, bf16[2048,72]{0,1:T(8,128)(2,1)S(1)}, u32[]{:S(2)}, u32[]{:S(2)}) collective-permute-start(bf16[2048,72]{0,1:T(8,128)(2,1)} %bitcast.66), channel_id=1, source_target_pairs={{0,128},{1,129},{2,130},{3,131},{4,132},{5,133},{6,134},{7,135},{8... | collective-permute-start | bytes 884744 | tf_op jit(solution)/shard_map/ppermute | solution.py:85
  20.4 136.5 %all-to-all-start = ((bf16[32,1024,72]{1,2,0:T(8,128)(2,1)}), bf16[32,1024,72]{1,2,0:T(8,128)(2,1)}, u32[]{:S(2)}, u32[]{:S(2)}) async-start(bf16[32,1024,72]{1,2,0:T(8,128)(2,1)} %broadcast_in_dim.14), calls=%async_computation | async-start | bytes 9437184 | tf_op jit(solution)/shard_map/all_to_all | solution.py:64
  30.0 180.1 %all-gather.3.cloned.1.call-start = ((), (), s32[]{:S(2)}) async-start(), calls=%async_computation.2 | async-start | bytes 4866048 | tf_op jit(solution)/shard_map/all_gather | solution.py:62
  159.8 9.6 %copy-start.3 = (bf16[256,576]{0,1:T(8,128)(2,1)S(1)}, bf16[256,576]{0,1:T(8,128)(2,1)}, u32[]{:S(2)}) copy-start(bf16[256,576]{0,1:T(8,128)(2,1)} %param.13) | copy-start | bytes 884740
  159.8 12.6 %copy-start.6 = (s32[1,2]{1,0:T(1,128)S(1)}, s32[1,2]{1,0:T(1,128)}, u32[]{:S(2)}) copy-start(s32[1,2]{1,0:T(1,128)} %param.21) | copy-start | bytes 28
  159.8 12.7 %copy-start.4 = (s32[1,2,32]{2,1,0:T(2,128)S(1)}, s32[1,2,32]{2,1,0:T(2,128)}, u32[]{:S(2)}) copy-start(s32[1,2,32]{2,1,0:T(2,128)} %param.20) | copy-start | bytes 772
  159.8 136.3 %all-to-all-start.1 = ((bf16[32,1024,72]{1,2,0:T(8,128)(2,1)}), bf16[32,1024,72]{1,2,0:T(8,128)(2,1)}, u32[]{:S(2)}, u32[]{:S(2)}) async-start(bf16[32,1024,72]{1,2,0:T(8,128)(2,1)} %broadcast_in_dim.30), calls=%async_computation.1 | async-start | bytes 9437184 | tf_op jit(solution)/shard_map/all_to_all | solution.py:64
  168.6 132.8 %all-gather.5.cloned.1.call-start = ((), (), s32[]{:S(2)}) async-start(), calls=%async_computation.3 | async-start | bytes 4866048 | tf_op jit(solution)/shard_map/all_gather | solution.py:62
  169.6 4.6 %collective-permute-start = (bf16[256,576]{1,0:T(8,128)(2,1)S(1)}, bf16[256,576]{1,0:T(8,128)(2,1)S(1)}, u32[]{:S(2)}, u32[]{:S(2)}) collective-permute-start(bf16[256,576]{1,0:T(8,128)(2,1)S(1)} %copy.39), channel_id=1, source_target_pairs={{0,96},{32,0},{64,32},{96,64},{1,97},{33,1},{65,33},{97,65},{2,98}... | collective-permute-start | bytes 884744 | tf_op jit(solution)/shard_map/ppermute | solution.py:18
  170.3 3.9 %collective-permute-start.1 = (bf16[256,576]{1,0:T(8,128)(2,1)S(1)}, bf16[256,576]{1,0:T(8,128)(2,1)S(1)}, u32[]{:S(2)}, u32[]{:S(2)}) collective-permute-start(bf16[256,576]{1,0:T(8,128)(2,1)S(1)} %copy.39), channel_id=1, source_target_pairs={{0,64},{32,96},{64,0},{96,32},{1,65},{33,97},{65,1},{97,33},{2,66}... | collective-permute-start | bytes 884744 | tf_op jit(solution)/shard_map/ppermute | solution.py:18
  170.9 3.2 collective-permute-start.2
  174.1 6.3 %copy-start = (f32[32,8,16,128]{3,1,2,0:T(8,128)}, f32[32,8,16,128]{3,1,2,0:T(8,128)S(1)}, u32[]{:S(2)}) copy-start(f32[32,8,16,128]{3,1,2,0:T(8,128)S(1)} %copy.55) | copy-start | bytes 6291460
  174.1 0.8 copy-start.1
  174.2 0.9 copy-start.2
  175.1 5.2 %copy-start.5 = (f32[1,2048]{1,0:T(1,128)S(1)}, f32[1,2048]{1,0:T(1,128)}, u32[]{:S(2)}) copy-start(f32[1,2048]{1,0:T(1,128)} %param.17) | copy-start | bytes 24580
  180.5 24.2 %collective-permute-start.3 = (bf16[256,2048]{1,0:T(8,128)(2,1)S(1)}, bf16[256,2048]{1,0:T(8,128)(2,1)S(1)}, u32[]{:S(2)}, u32[]{:S(2)}) collective-permute-start(bf16[256,2048]{1,0:T(8,128)(2,1)S(1)} %get-tuple-element.58), channel_id=1, source_target_pairs={{0,128},{1,129},{2,130},{3,131},{4,132},{5,133},{6,134},{7,135},{8... | collective-permute-start | bytes 3145736 | tf_op jit(solution)/shard_map/ppermute | solution.py:99
  216.0 17.7 %collective-permute-start.5 = (bf16[256,576]{1,0:T(8,128)(2,1)}, bf16[256,576]{1,0:T(8,128)(2,1)S(1)}, u32[]{:S(2)}, u32[]{:S(2)}) collective-permute-start(bf16[256,576]{1,0:T(8,128)(2,1)} %get-tuple-element.49), channel_id=1, source_target_pairs={{0,32},{32,64},{64,96},{96,0},{1,33},{33,65},{65,97},{97,1},{2,34}... | collective-permute-start | bytes 884744 | tf_op jit(solution)/shard_map/ppermute | solution.py:14
  216.0 17.7 %collective-permute-start.6 = (bf16[256,576]{1,0:T(8,128)(2,1)}, bf16[256,576]{1,0:T(8,128)(2,1)S(1)}, u32[]{:S(2)}, u32[]{:S(2)}) collective-permute-start(bf16[256,576]{1,0:T(8,128)(2,1)} %get-tuple-element.51), channel_id=1, source_target_pairs={{0,64},{32,96},{64,0},{96,32},{1,65},{33,97},{65,1},{97,33},{2,66}... | collective-permute-start | bytes 884744 | tf_op jit(solution)/shard_map/ppermute | solution.py:14
  217.5 16.6 %collective-permute-start.7 = (bf16[256,576]{1,0:T(8,128)(2,1)S(1)}, bf16[256,576]{1,0:T(8,128)(2,1)S(1)}, u32[]{:S(2)}, u32[]{:S(2)}) collective-permute-start(bf16[256,576]{1,0:T(8,128)(2,1)S(1)} %get-tuple-element.50), channel_id=1, source_target_pairs={{0,96},{32,0},{64,32},{96,64},{1,97},{33,1},{65,33},{97,65},{2,98}... | collective-permute-start | bytes 884744 | tf_op jit(solution)/shard_map/ppermute | solution.py:14
  234.4 2.5 collective-permute-start.8
  236.9 9.7 %collective-permute-start.10 = (bf16[256,576]{1,0:T(8,128)(2,1)S(1)}, bf16[256,576]{1,0:T(8,128)(2,1)S(1)}, u32[]{:S(2)}, u32[]{:S(2)}) collective-permute-start(bf16[256,576]{1,0:T(8,128)(2,1)S(1)} %collective-permute-done.8), channel_id=1, source_target_pairs={{128,192},{160,224},{192,128},{224,160},{129,193},{161,225},{193,1... | collective-permute-start | bytes 884744 | tf_op jit(solution)/shard_map/ppermute | solution.py:18
  239.4 10.7 %collective-permute-start.11 = (bf16[256,576]{1,0:T(8,128)(2,1)S(1)}, bf16[256,576]{1,0:T(8,128)(2,1)S(1)}, u32[]{:S(2)}, u32[]{:S(2)}) collective-permute-start(bf16[256,576]{1,0:T(8,128)(2,1)S(1)} %collective-permute-done.8), channel_id=1, source_target_pairs={{128,160},{160,192},{192,224},{224,128},{129,161},{161,193},{193,2... | collective-permute-start | bytes 884744 | tf_op jit(solution)/shard_map/ppermute | solution.py:18
  243.2 8.2 %collective-permute-start.9 = (bf16[256,576]{1,0:T(8,128)(2,1)S(1)}, bf16[256,576]{1,0:T(8,128)(2,1)S(1)}, u32[]{:S(2)}, u32[]{:S(2)}) collective-permute-start(bf16[256,576]{1,0:T(8,128)(2,1)S(1)} %collective-permute-done.8), channel_id=1, source_target_pairs={{128,224},{160,128},{192,160},{224,192},{129,225},{161,129},{193,1... | collective-permute-start | bytes 884744 | tf_op jit(solution)/shard_map/ppermute | solution.py:18
  264.0 3.8 %collective-permute-start.12 = (bf16[256,2048]{1,0:T(8,128)(2,1)}, bf16[256,2048]{1,0:T(8,128)(2,1)S(1)}, u32[]{:S(2)}, u32[]{:S(2)}) collective-permute-start(bf16[256,2048]{1,0:T(8,128)(2,1)} %get-tuple-element.59), channel_id=1, source_target_pairs={{128,0},{129,1},{130,2},{131,3},{132,4},{133,5},{134,6},{135,7},{1... | collective-permute-start | bytes 3145736 | tf_op jit(solution)/shard_map/ppermute | solution.py:116
  306.6 7.2 %collective-permute-start.14 = (bf16[256,576]{1,0:T(8,128)(2,1)S(1)}, bf16[256,576]{1,0:T(8,128)(2,1)S(1)}, u32[]{:S(2)}, u32[]{:S(2)}) collective-permute-start(bf16[256,576]{1,0:T(8,128)(2,1)S(1)} %get-tuple-element.46), channel_id=1, source_target_pairs={{0,32},{32,64},{64,96},{96,0},{1,33},{33,65},{65,97},{97,1},{2,34}... | collective-permute-start | bytes 884744 | tf_op jit(solution)/shard_map/ppermute | solution.py:14
  307.9 11.1 %collective-permute-start.15 = (bf16[256,576]{1,0:T(8,128)(2,1)S(1)}, bf16[256,576]{1,0:T(8,128)(2,1)S(1)}, u32[]{:S(2)}, u32[]{:S(2)}) collective-permute-start(bf16[256,576]{1,0:T(8,128)(2,1)S(1)} %get-tuple-element.48), channel_id=1, source_target_pairs={{0,64},{32,96},{64,0},{96,32},{1,65},{33,97},{65,1},{97,33},{2,66}... | collective-permute-start | bytes 884744 | tf_op jit(solution)/shard_map/ppermute | solution.py:14
  310.4 8.5 %collective-permute-start.16 = (bf16[256,576]{1,0:T(8,128)(2,1)S(1)}, bf16[256,576]{1,0:T(8,128)(2,1)S(1)}, u32[]{:S(2)}, u32[]{:S(2)}) collective-permute-start(bf16[256,576]{1,0:T(8,128)(2,1)S(1)} %get-tuple-element.47), channel_id=1, source_target_pairs={{0,96},{32,0},{64,32},{96,64},{1,97},{33,1},{65,33},{97,65},{2,98}... | collective-permute-start | bytes 884744 | tf_op jit(solution)/shard_map/ppermute | solution.py:14
  319.6 9.5 %collective-permute-start.17 = (bf16[256,576]{1,0:T(8,128)(2,1)S(1)}, bf16[256,576]{1,0:T(8,128)(2,1)S(1)}, u32[]{:S(2)}, u32[]{:S(2)}) collective-permute-start(bf16[256,576]{1,0:T(8,128)(2,1)S(1)} %get-tuple-element.38), channel_id=1, source_target_pairs={{0,128},{1,129},{2,130},{3,131},{4,132},{5,133},{6,134},{7,135},{8... | collective-permute-start | bytes 884744 | tf_op jit(solution)/shard_map/ppermute | solution.py:120
Sparse Core Ops, SparseCore 0:
  34.0 128.7 all-gather.2
  172.6 128.7 all-gather.4

commit v4 on v3

v4 whole, which is shorter than its diff:
```python
import jax
import jax.numpy as jnp
from jax import lax
from jax.sharding import Mesh, PartitionSpec as P

BLOCK = 128
TILE = 128
GROUP = ("layer", "feat")
SPLIT = 1024
TOK = ("tz", "ty")


def within_layer(shard, section, shift, n_feat):
    if section is None:
        return lax.ppermute(shard, "feat", [(i, (i + shift) % n_feat) for i in range(n_feat)])
    pairs = [
        (section * n_feat + i, section * n_feat + (i + shift) % n_feat) for i in range(n_feat)
    ]
    return lax.ppermute(shard, GROUP, pairs)


def feat_gather(part, section, feat_index, n_feat):
    received = [part] + [within_layer(part, section, k, n_feat) for k in range(1, n_feat)]
    blocks = []
    for j in range(n_feat):
        block = jnp.zeros_like(part)
        for k in range(n_feat):
            block = jnp.where((feat_index - k) % n_feat == j, received[k], block)
        blocks.append(block)
    return jnp.concatenate(blocks, axis=-1)


def feat_reduce_scatter(terms, section, feat_index, n_feat):
    cols = terms.shape[-1] // n_feat
    total = lax.dynamic_slice_in_dim(terms, feat_index * cols, cols, terms.ndim - 1).astype(
        jnp.float32
    )
    for k in range(1, n_feat):
        target = (feat_index + k) % n_feat
        piece = lax.dynamic_slice_in_dim(terms, target * cols, cols, terms.ndim - 1)
        total = total + within_layer(piece, section, k, n_feat).astype(jnp.float32)
    return total


def feature_mask(block_list, block_count, feat_index, blocks_dev):
    listed = block_list[0]
    in_use = jnp.arange(listed.shape[1], dtype=jnp.int32)[None, :] < block_count[0][:, None]
    own_blocks = feat_index * blocks_dev + jnp.arange(blocks_dev, dtype=jnp.int32)
    matches = (listed[:, None, :] == own_blocks[None, :, None]) & in_use[:, None, :]
    active = jnp.any(matches, axis=2).astype(jnp.float32)
    return jnp.repeat(jnp.repeat(active, TILE, axis=0), BLOCK, axis=1)


def encode(gathered, enc_weight, enc_bias, mask):
    preact = (
        jnp.dot(gathered, enc_weight[0], preferred_element_type=jnp.float32) + enc_bias[0][None, :]
    )
    return (jax.nn.relu(preact) * mask).astype(jnp.bfloat16)


def gather_columns(shard):
    n_y = lax.axis_size("ty")
    y_index = lax.axis_index("ty")
    by_gather = lax.all_gather(shard[:SPLIT], TOK, axis=1, tiled=True)
    along_z = lax.all_gather(shard[SPLIT:], "tz", axis=0)
    received = [along_z] + [
        lax.ppermute(along_z, "ty", [(i, (i + k) % n_y) for i in range(n_y)]) for k in range(1, n_y)
    ]
    blocks = []
    for j in range(n_y):
        block = jnp.zeros_like(along_z)
        for k in range(n_y):
            block = jnp.where((y_index - k) % n_y == j, received[k], block)
        blocks.append(block)
    return by_gather, jnp.stack(blocks, axis=1)


def decode(features, full):
    by_gather, by_rest = full
    first = jnp.dot(features[:, :SPLIT], by_gather, preferred_element_type=jnp.float32)
    second = jnp.einsum(
        "tf,zyfc->tzyc", features[:, SPLIT:], by_rest, preferred_element_type=jnp.float32
    )
    return (first + second.reshape(first.shape)).astype(jnp.bfloat16)


def shards(
    resid_in, attn_out, carry_in, enc_weight, enc_bias, dec_own, dec_next, block_list, block_count
):
    n_feat = lax.axis_size("feat")
    section_index = lax.axis_index("layer")
    feat_index = lax.axis_index("feat")
    blocks_dev = enc_weight.shape[2] // BLOCK
    first_core = section_index == 0
    own_full = gather_columns(dec_own[0])
    next_full = gather_columns(dec_next[0])
    mask = feature_mask(block_list, block_count, feat_index, blocks_dev)
    attention = attn_out[0].astype(jnp.float32)

    def encoded(source, section):
        return lax.cond(
            section_index == section,
            lambda inner: encode(inner, enc_weight, enc_bias, mask),
            lambda inner: jnp.zeros((inner.shape[0], enc_weight.shape[2]), jnp.bfloat16),
            source,
        )

    features_first = encoded(feat_gather(resid_in, 0, feat_index, n_feat), 0)
    own_first = feat_reduce_scatter(decode(features_first, own_full), 0, feat_index, n_feat)
    recon_first = own_first + carry_in.astype(jnp.float32)
    residual_next = (resid_in.astype(jnp.float32) + attention + recon_first).astype(jnp.bfloat16)
    residual_next = lax.ppermute(residual_next, "layer", [(0, 1)])

    features_second = encoded(feat_gather(residual_next, 1, feat_index, n_feat), 1)
    own_second = feat_reduce_scatter(decode(features_second, own_full), 1, feat_index, n_feat)

    features = jnp.where(first_core, features_first, features_second)
    next_part = feat_reduce_scatter(decode(features, next_full), None, feat_index, n_feat)
    outgoing_now = next_part.astype(jnp.bfloat16)
    incoming = lax.ppermute(outgoing_now, "layer", [(0, 1)])
    recon_second = own_second + incoming.astype(jnp.float32)

    recon_out = jnp.where(first_core, recon_first, recon_second).astype(jnp.bfloat16)
    return (recon_out[None], outgoing_now[None])


def solution(mesh):
    devices = mesh.devices
    n_y = len({device.coords[1] for device in devices.reshape(-1)})
    split_mesh = Mesh(
        devices.reshape(devices.shape[:2] + (devices.shape[2] // n_y, n_y)),
        ("layer", "feat", "tz", "ty"),
    )
    return jax.shard_map(
        shards,
        mesh=split_mesh,
        in_specs=(
            P(TOK, "feat"),
            P("layer", TOK, "feat"),
            P(TOK, "feat"),
            P("layer", None, "feat"),
            P("layer", "feat"),
            P("layer", "feat", TOK),
            P("layer", "feat", TOK),
            P("layer", TOK, None),
            P("layer", TOK),
        ),
        out_specs=(P("layer", TOK, "feat"), P("layer", TOK, "feat")),
        check_vma=False,
    )
```

time: 342 us -> 326 us (0.953); the launches traced: 337 us -> 325 us
  waiting for transfers between devices: 215 us -> 196 us
  starting transfers between devices: 49.5 us -> 37 us
  local copies, waits for them, and re-layouts: 21.8 us -> 29.6 us
  other arithmetic: 8.04 us -> 15.3 us
  matrix products: 28.1 us -> 32.3 us
    all_to_all x2 -> x0, waiting for transfers between devices: 151 us -> none  [gather_columns(): by_all_to_all = lax.all_to_all(rest, 'tok', 0, 0, tiled=True)]
    all_gather x2 -> x4, waiting for transfers between devices: 0.01 us -> 145 us  [the longest x2 83.9 us: gather_columns(): by_gather = lax.all_gather(shard[:SPLIT], TOK, axis=1, tiled=True)]
    ppermute x6 -> x3, waiting for transfers between devices: 20.5 us -> 0.01 us  [within_layer(): lax.ppermute(shard, 'feat', [(i, (i + shift) % n_feat) for i in range(n_f...]
    all_to_all x2 -> x0, starting transfers between devices: 18.4 us -> none  [gather_columns(): by_all_to_all = lax.all_to_all(rest, 'tok', 0, 0, tiled=True)]
    dot_general x0 -> x3, matrix products: none -> 12 us  [decode(): jnp.einsum('tf,zyfc->tzyc', features[:, SPLIT:], by_rest, preferred_eleme...]
    ppermute x6 -> x12, starting transfers between devices: 11.7 us -> 22.6 us  [within_layer(): return lax.ppermute(shard, GROUP, pairs)]
    reshape x2 -> x0, matrix products: 10.6 us -> none  [decode(): return (first + second.reshape(first.shape)).astype(jnp.bfloat16)]
    reshape x0 -> x3, local copies, waits for them, and re-layouts: none -> 9.46 us  [decode(): return (first + second.reshape(first.shape)).astype(jnp.bfloat16)]
  transfers between devices with their start and end apart: 22 -> 27, of which waited for: 15 -> 12; matrix products, arithmetic and copies ran while one was open for 14% -> 20% of each run, Pallas kernels for 0% -> 0%
where the time goes in v4:
time: 326 us; the launch traced here: 325 us
  waiting for transfers between devices  196 us (60%)
  starting transfers between devices  37 us (11%)
  matrix products  32.3 us (10%)
  local copies, waits for them, and re-layouts  29.6 us (9%)
  other arithmetic  15.3 us (5%)
  between operations  14.4 us (4%)
    all_gather x2, waiting for transfers between devices, gather_columns(): by_gather = lax.all_gather(shard[:SPLIT], TOK, axis=1, tiled=True)  83.9 us
    all_gather x2, waiting for transfers between devices, gather_columns(): along_z = lax.all_gather(shard[SPLIT:], 'tz', axis=0)  61.5 us
    ppermute x12, starting transfers between devices, within_layer(): return lax.ppermute(shard, GROUP, pairs)  22.6 us
    ppermute x6, waiting for transfers between devices, gather_columns(): lax.ppermute(along_z, 'ty', [(i, (i + k) % n_y) for i in range(n_y)])  21 us
    ppermute x1, waiting for transfers between devices, shards(): residual_next = lax.ppermute(residual_next, 'layer', [(0, 1)])  15.8 us
    dot_general x3, matrix products, decode(): jnp.dot(features[:, :SPLIT], by_gather, preferred_element_type=jnp.float32)  13 us
    dot_general x3, matrix products, decode(): jnp.einsum('tf,zyfc->tzyc', features[:, SPLIT:], by_rest, preferred_eleme...  12 us
    ppermute x12, waiting for transfers between devices, within_layer(): return lax.ppermute(shard, GROUP, pairs)  11.6 us
  transfers between devices with their start and end apart: 27, of which 12 were waited for; matrix products, arithmetic and copies ran while one was open for 20% of the time, Pallas kernels for 0%

profile of v4, /device:TPU:1, one launch (start us, length us, event | category | flops | bytes accessed | tf_op | source)
XLA Modules:
  0.0 324.8 jit_solution(7871902711344026836)
XLA Ops:
  7.2 1.7 fusion.65
  9.0 1.7 fusion.64
  13.0 35.0 %all-gather.7.cloned.1.call-done = bf16[8,1024,72]{1,2,0:T(8,128)(2,1)} async-done(((bf16[1,1024,72]{1,2,0:T(8,128)(2,1)}), bf16[8,1024,72]{1,2,0:T(8,128)(2,1)}) %all-gather.7.cloned.1.call-update) | async-done | bytes 1179664 | tf_op jit(solution)/shard_map/all_gather | solution.py:65
  48.0 2.5 collective-permute-start.3
  54.1 2.2 copy.94
  57.1 1.2 select_select_fusion.4
  58.3 2.2 concatenate.6
  61.6 26.5 %all-gather.9.cloned.1.call-done = bf16[8,1024,72]{1,2,0:T(8,128)(2,1)} async-done(((bf16[1,1024,72]{1,2,0:T(8,128)(2,1)}), bf16[8,1024,72]{1,2,0:T(8,128)(2,1)}) %all-gather.9.cloned.1.call-update) | async-done | bytes 1179664 | tf_op jit(solution)/shard_map/all_gather | solution.py:65
  88.1 2.2 collective-permute-start.16
  91.3 21.0 %collective-permute-done.5 = bf16[8,1024,72]{1,2,0:T(8,128)(2,1)} collective-permute-done((bf16[8,1024,72]{1,2,0:T(8,128)(2,1)}, bf16[8,1024,72]{1,2,0:T(8,128)(2,1)}, u32[]{:S(2)}, u32[]{:S(2)}) %collective-permute-start.5) | collective-permute-done | bytes 1179680 | tf_op jit(solution)/shard_map/ppermute | solution.py:67
  112.5 2.5 select_bitcast_fusion.7
  115.1 2.7 fusion.55
  117.8 3.2 copy.78
  121.0 79.7 %all-gather.11.cloned.1.call-done = bf16[1,1024,2304]{1,2,0:T(8,128)(2,1)} async-done(((bf16[1,1024,72]{1,2,0:T(8,128)(2,1)}), bf16[1,1024,2304]{1,2,0:T(8,128)(2,1)}) %all-gather.11.cloned.1.call-update) | async-done | bytes 4718608 | tf_op jit(solution)/shard_map/all_gather | solution.py:64
  200.7 4.5 %fusion.51 = bf16[256,2304]{1,0:T(8,128)(2,1)S(1)} fusion(f32[256,2304]{1,0:T(8,128)} %copy.78, bf16[1,1024,2304]{1,2,0:T(8,128)(2,1)} %all-gather.11.cloned.1.call-done, bf16[256,2048]{1,0:T(8,128)(2,1)S(1)} %copy-done.3), kind=kOutput, calls=%fused_computation.27 | convolution fusion | flops 1209139200 | bytes 8781824 | tf_op jit(solution)/shard_map/dot_general | solution.py:80
  205.3 1.3 constant_dynamic-slice_fusion.8
  207.2 1.4 collective-permute-start.7
  208.6 1.4 collective-permute-start.8
  211.4 1.6 fusion.57
  213.1 1.3 collective-permute-start.9
  214.4 4.1 %select_bitcast_fusion.3 = (bf16[8,1,1024,72]{2,3,0,1:T(8,128)(2,1)}, bf16[8,1,1024,72]{2,3,0,1:T(8,128)(2,1)}, bf16[8,1,1024,72]{2,3,0,1:T(8,128)(2,1)}) fusion(bf16[8,1024,72]{1,2,0:T(8,128)(2,1)} %collective-permute-done.16, bf16[8,1024,72]{1,2,0:T(8,128)(2,1)} %collective-permute-done.17, bf16[8,1024,72]{1,2,0:T(8,128)(2,1)} %collective-permute-done.18, ...), kind=kLoop, calls=%fused_computation.32 | loop fusion | flops 7077888 | bytes 8257548 | tf_op jit(solution)/shard_map/stack | solution.py:75
  218.5 15.8 %collective-permute-done.9 = bf16[256,576]{1,0:T(8,128)(2,1)S(1)} collective-permute-done((bf16[256,576]{1,0:T(8,128)(2,1)S(1)}, bf16[256,576]{1,0:T(8,128)(2,1)S(1)}, u32[]{:S(2)}, u32[]{:S(2)}) %collective-permute-start.9) | collective-permute-done | bytes 294944 | tf_op jit(solution)/shard_map/ppermute | solution.py:112
  234.4 4.3 %collective-permute-start.10 = (bf16[256,576]{1,0:T(8,128)(2,1)S(1)}, bf16[256,576]{1,0:T(8,128)(2,1)S(1)}, u32[]{:S(2)}, u32[]{:S(2)}) collective-permute-start(bf16[256,576]{1,0:T(8,128)(2,1)S(1)} %collective-permute-done.9), channel_id=1, source_target_pairs={{128,224},{160,128},{192,160},{224,192},{129,225},{161,129},{193,1... | collective-permute-start | bytes 884744 | tf_op jit(solution)/shard_map/ppermute | solution.py:19
  238.6 1.9 collective-permute-start.11
  240.6 2.5 collective-permute-start.12
  243.1 2.5 select_bitcast_fusion.2
  246.1 1.9 collective-permute-done.11
  248.1 3.4 %collective-permute-done.12 = bf16[256,576]{1,0:T(8,128)(2,1)S(1)} collective-permute-done((bf16[256,576]{1,0:T(8,128)(2,1)S(1)}, bf16[256,576]{1,0:T(8,128)(2,1)S(1)}, u32[]{:S(2)}, u32[]{:S(2)}) %collective-permute-start.12) | collective-permute-done | bytes 294944 | tf_op jit(solution)/shard_map/ppermute | solution.py:19
  251.8 2.2 concatenate.7
  254.0 7.5 %conditional.3 = (bf16[256,2048]{1,0:T(8,128)(2,1)S(1)}) conditional(s32[]{:T(128)} %convert_element_type.92, () %tuple.22, (bf16[1,2304,2048]{2,1,0:T(8,128)(2,1)}, bf16[256,2304]{1,0:T(8,128)(2,1)}, f32[1,2048]{1,0:T(1,128)S(1)}, f32[256,2048]{1,0:T(8,128)}) %tuple.60), branch_computations={%region_3.4_spmd, %region_4.5_spmd} | conditional | flops 2418016256 | bytes 13770760 | solution.py:101
  254.0 7.2 %fusion.25 = bf16[256,2048]{1,0:T(8,128)(2,1)S(1)} fusion(f32[256,2048]{1,0:T(8,128)} %get-tuple-element.29, bf16[256,2304]{1,0:T(8,128)(2,1)} %get-tuple-element.26, bf16[1,2304,2048]{2,1,0:T(8,128)(2,1)} %get-tuple-element.27, f32[2048]{0:T(1024)S(1)} %bitcast.109), kind=kOutput, calls=%fused_computation.11 | convolution fusion | flops 2418016256 | bytes 13770752 | tf_op jit(solution)/shard_map/cond/branch_1_fun/dot_general | solution.py:56
  261.5 5.3 %fusion.54 = f32[256,8,4,72]{0,3,2,1:T(8,128)} fusion(bf16[8,1,1024,72]{2,3,1,0:T(8,128)(2,1)} %copy-done.10, bf16[8,1,1024,72]{2,3,1,0:T(8,128)(2,1)} %copy-done.11, bf16[8,1,1024,72]{2,3,1,0:T(8,128)(2,1)} %copy-done.8, bf16[8,1,1024,72]{2,3,1,0:T(8,128)(2,1)} %copy-done.9, bf16[256,2048]{1,0:T(8,128)(2,1)S(1)} %get-tuple-element.66), kind=kOutput, calls=%fused_computation.38 | convolution fusion | flops 1226833920 | bytes 7602176 | tf_op jit(solution)/shard_map/tf,zyfc->tzyc/dot_general | solution.py:81
  266.8 3.1 copy.82
  270.0 1.5 copy-done.12
  271.9 4.0 %fusion.34 = f32[256,8,4,72]{0,3,2,1:T(8,128)} fusion(bf16[256,2048]{1,0:T(8,128)(2,1)S(1)} %broadcast_select_fusion, bf16[8,1,1024,72]{2,3,0,1:T(8,128)(2,1)S(1)} %copy-done.13, bf16[8,1,1024,72]{2,3,0,1:T(8,128)(2,1)} %get-tuple-element.45, bf16[8,1,1024,72]{2,3,0,1:T(8,128)(2,1)} %select_bitcast_fusion.2, bf16[8,1,1024,72]{2,3,0,1:T(8,128)(2,1)S(1)} %copy-done.12), kind=kOutput, calls=%fused_computation.20 | convolution fusion | flops 1215037440 | bytes 7602176 | tf_op jit(solution)/shard_map/tf,zyfc->tzyc/dot_general | solution.py:81
  275.9 3.2 copy.84
  279.1 4.2 %all-gather.13.cloned.1.call-done = bf16[1,1024,2304]{1,2,0:T(8,128)(2,1)} async-done(((bf16[1,1024,72]{1,2,0:T(8,128)(2,1)}), bf16[1,1024,2304]{1,2,0:T(8,128)(2,1)}) %all-gather.13.cloned.1.call-update) | async-done | bytes 4718608 | tf_op jit(solution)/shard_map/all_gather | solution.py:64
  283.3 4.7 %fusion.45 = bf16[256,2304]{1,0:T(8,128)(2,1)S(1)} fusion(f32[256,2304]{1,0:T(8,128)} %copy.84, bf16[1,1024,2304]{1,2,0:T(8,128)(2,1)} %all-gather.13.cloned.1.call-done, bf16[256,2048]{1,0:T(8,128)(2,1)S(1)} %copy-done.15), kind=kOutput, calls=%fused_computation.25 | convolution fusion | flops 1209139200 | bytes 8781824 | tf_op jit(solution)/shard_map/dot_general | solution.py:80
  288.5 1.3 collective-permute-start.19
  289.7 2.4 collective-permute-start.20
  292.1 1.2 collective-permute-start.21
  293.3 3.8 %fusion.48 = bf16[256,2304]{1,0:T(8,128)(2,1)S(1)} fusion(f32[256,2304]{1,0:T(8,128)S(1)} %copy-done.4, bf16[1,1024,2304]{1,2,0:T(8,128)(2,1)} %all-gather.11.cloned.1.call-done, bf16[256,2048]{1,0:T(8,128)(2,1)S(1)} %get-tuple-element.66), kind=kOutput, calls=%fused_computation.26 | convolution fusion | flops 1209139200 | bytes 8781824 | tf_op jit(solution)/shard_map/dot_general | solution.py:80
  297.6 2.2 collective-permute-start.13
  299.8 2.8 collective-permute-start.14
  302.7 3.4 %collective-permute-start.15 = (bf16[256,576]{1,0:T(8,128)(2,1)S(1)}, bf16[256,576]{1,0:T(8,128)(2,1)}, u32[]{:S(2)}, u32[]{:S(2)}) collective-permute-start(bf16[256,576]{1,0:T(8,128)(2,1)S(1)} %get-tuple-element.53), channel_id=1, source_target_pairs={{128,224},{160,128},{192,160},{224,192},{129,225},{161,129},{193,1... | collective-permute-start | bytes 884744 | tf_op jit(solution)/shard_map/ppermute | solution.py:19
  306.4 1.3 collective-permute-start.22
  309.6 4.6 %collective-permute-done.14 = bf16[256,576]{1,0:T(8,128)(2,1)} collective-permute-done((bf16[256,576]{1,0:T(8,128)(2,1)S(1)}, bf16[256,576]{1,0:T(8,128)(2,1)}, u32[]{:S(2)}, u32[]{:S(2)}) %collective-permute-start.14) | collective-permute-done | bytes 294944 | tf_op jit(solution)/shard_map/ppermute | solution.py:19
  315.3 2.1 fusion.61
  (96 shorter events, 18.4 us)
Async XLA Ops:
  7.2 4.9 %copy-start.16 = (bf16[256,576]{0,1:T(8,128)(2,1)S(1)}, bf16[256,576]{0,1:T(8,128)(2,1)}, u32[]{:S(2)}) copy-start(bf16[256,576]{0,1:T(8,128)(2,1)} %param.13) | copy-start | bytes 884740
  7.2 40.8 %all-gather.7.cloned.1.call-start = ((), (), s32[]{:S(2)}) async-start(), calls=%async_computation | async-start | bytes 1327104 | tf_op jit(solution)/shard_map/all_gather | solution.py:65
  9.0 44.2 %copy-start.20 = (s32[1,2]{1,0:T(1,128)S(1)}, s32[1,2]{1,0:T(1,128)}, u32[]{:S(2)}) copy-start(s32[1,2]{1,0:T(1,128)} %param.21) | copy-start | bytes 28
  9.0 44.3 %copy-start.18 = (s32[1,2,32]{2,1,0:T(2,128)S(1)}, s32[1,2,32]{2,1,0:T(2,128)}, u32[]{:S(2)}) copy-start(s32[1,2,32]{2,1,0:T(2,128)} %param.20) | copy-start | bytes 772
  9.0 79.1 %all-gather.9.cloned.1.call-start = ((), (), s32[]{:S(2)}) async-start(), calls=%async_computation.1 | async-start | bytes 1327104 | tf_op jit(solution)/shard_map/all_gather | solution.py:65
  10.8 189.9 %all-gather.11.cloned.1.call-start = ((), (), s32[]{:S(2)}) async-start(), calls=%async_computation.2 | async-start | bytes 4866048 | tf_op jit(solution)/shard_map/all_gather | solution.py:64
  11.5 271.8 %all-gather.13.cloned.1.call-start = ((), (), s32[]{:S(2)}) async-start(), calls=%async_computation.3 | async-start | bytes 4866048 | tf_op jit(solution)/shard_map/all_gather | solution.py:64
  12.3 40.2 %collective-permute-start = (bf16[256,576]{1,0:T(8,128)(2,1)S(1)}, bf16[256,576]{1,0:T(8,128)(2,1)S(1)}, u32[]{:S(2)}, u32[]{:S(2)}) collective-permute-start(bf16[256,576]{1,0:T(8,128)(2,1)S(1)} %copy.68), channel_id=1, source_target_pairs={{0,96},{32,0},{64,32},{96,64},{1,97},{33,1},{65,33},{97,65},{2,98}... | collective-permute-start | bytes 884744 | tf_op jit(solution)/shard_map/ppermute | solution.py:19
  48.0 42.6 %collective-permute-start.3 = (bf16[8,1024,72]{1,2,0:T(8,128)(2,1)}, bf16[8,1024,72]{1,2,0:T(8,128)(2,1)S(1)}, u32[]{:S(2)}, u32[]{:S(2)}) collective-permute-start(bf16[8,1024,72]{1,2,0:T(8,128)(2,1)} %all-gather.7.cloned.1.call-done), channel_id=1, source_target_pairs={{0,3},{1,0},{2,1},{3,2},{4,7},{5,4},{6,5},{7,6},{8,11},{9,8},{10,9... | collective-permute-start | bytes 3538952 | tf_op jit(solution)/shard_map/ppermute | solution.py:67
  50.5 40.8 %collective-permute-start.4 = (bf16[8,1024,72]{1,2,0:T(8,128)(2,1)}, bf16[8,1024,72]{1,2,0:T(8,128)(2,1)}, u32[]{:S(2)}, u32[]{:S(2)}) collective-permute-start(bf16[8,1024,72]{1,2,0:T(8,128)(2,1)} %all-gather.7.cloned.1.call-done), channel_id=1, source_target_pairs={{0,2},{1,3},{2,0},{3,1},{4,6},{5,7},{6,4},{7,5},{8,10},{9,11},{10,... | collective-permute-start | bytes 3538952 | tf_op jit(solution)/shard_map/ppermute | solution.py:67
  51.0 61.3 %collective-permute-start.5 = (bf16[8,1024,72]{1,2,0:T(8,128)(2,1)}, bf16[8,1024,72]{1,2,0:T(8,128)(2,1)}, u32[]{:S(2)}, u32[]{:S(2)}) collective-permute-start(bf16[8,1024,72]{1,2,0:T(8,128)(2,1)} %all-gather.7.cloned.1.call-done), channel_id=1, source_target_pairs={{0,1},{1,2},{2,3},{3,0},{4,5},{5,6},{6,7},{7,4},{8,9},{9,10},{10,1... | collective-permute-start | bytes 3538952 | tf_op jit(solution)/shard_map/ppermute | solution.py:67
  51.6 4.7 %collective-permute-start.1 = (bf16[256,576]{1,0:T(8,128)(2,1)S(1)}, bf16[256,576]{1,0:T(8,128)(2,1)S(1)}, u32[]{:S(2)}, u32[]{:S(2)}) collective-permute-start(bf16[256,576]{1,0:T(8,128)(2,1)S(1)} %copy.68), channel_id=1, source_target_pairs={{0,64},{32,96},{64,0},{96,32},{1,65},{33,97},{65,1},{97,33},{2,66}... | collective-permute-start | bytes 884744 | tf_op jit(solution)/shard_map/ppermute | solution.py:19
  52.5 3.8 %collective-permute-start.2 = (bf16[256,576]{1,0:T(8,128)(2,1)S(1)}, bf16[256,576]{1,0:T(8,128)(2,1)S(1)}, u32[]{:S(2)}, u32[]{:S(2)}) collective-permute-start(bf16[256,576]{1,0:T(8,128)(2,1)S(1)} %copy.68), channel_id=1, source_target_pairs={{0,32},{32,64},{64,96},{96,0},{1,33},{33,65},{65,97},{97,1},{2,34}... | collective-permute-start | bytes 884744 | tf_op jit(solution)/shard_map/ppermute | solution.py:19
  56.3 0.7 copy-start.7
  58.3 2.2 copy-start.19
  60.5 51.8 %copy-start.1 = (bf16[8,1024,72]{1,2,0:T(8,128)(2,1)S(1)}, bf16[8,1024,72]{1,2,0:T(8,128)(2,1)}, u32[]{:S(2)}) copy-start(bf16[8,1024,72]{1,2,0:T(8,128)(2,1)} %all-gather.7.cloned.1.call-done) | copy-start | bytes 3538948
  88.1 126.3 %collective-permute-start.16 = (bf16[8,1024,72]{1,2,0:T(8,128)(2,1)}, bf16[8,1024,72]{1,2,0:T(8,128)(2,1)}, u32[]{:S(2)}, u32[]{:S(2)}) collective-permute-start(bf16[8,1024,72]{1,2,0:T(8,128)(2,1)} %all-gather.9.cloned.1.call-done), channel_id=1, source_target_pairs={{0,3},{1,0},{2,1},{3,2},{4,7},{5,4},{6,5},{7,6},{8,11},{9,8},{10,9... | collective-permute-start | bytes 3538952 | tf_op jit(solution)/shard_map/ppermute | solution.py:67
  90.3 124.1 %collective-permute-start.17 = (bf16[8,1024,72]{1,2,0:T(8,128)(2,1)}, bf16[8,1024,72]{1,2,0:T(8,128)(2,1)}, u32[]{:S(2)}, u32[]{:S(2)}) collective-permute-start(bf16[8,1024,72]{1,2,0:T(8,128)(2,1)} %all-gather.9.cloned.1.call-done), channel_id=1, source_target_pairs={{0,2},{1,3},{2,0},{3,1},{4,6},{5,7},{6,4},{7,5},{8,10},{9,11},{10,... | collective-permute-start | bytes 3538952 | tf_op jit(solution)/shard_map/ppermute | solution.py:67
  90.6 123.8 %collective-permute-start.18 = (bf16[8,1024,72]{1,2,0:T(8,128)(2,1)}, bf16[8,1024,72]{1,2,0:T(8,128)(2,1)}, u32[]{:S(2)}, u32[]{:S(2)}) collective-permute-start(bf16[8,1024,72]{1,2,0:T(8,128)(2,1)} %all-gather.9.cloned.1.call-done), channel_id=1, source_target_pairs={{0,1},{1,2},{2,3},{3,0},{4,5},{5,6},{6,7},{7,4},{8,9},{9,10},{10,1... | collective-permute-start | bytes 3538952 | tf_op jit(solution)/shard_map/ppermute | solution.py:67
  112.5 2.6 copy-start.8
  112.5 2.6 copy-start.2
  115.0 2.8 copy-start.9
  115.1 2.8 copy-start.10
  115.1 2.8 copy-start.11
  117.8 82.9 %copy-start.3 = (bf16[256,2048]{1,0:T(8,128)(2,1)S(1)}, bf16[256,2048]{1,0:T(8,128)(2,1)}, u32[]{:S(2)}) copy-start(bf16[256,2048]{1,0:T(8,128)(2,1)} %get-tuple-element.65) | copy-start | bytes 3145732
  205.2 5.0 %copy-start.5 = (bf16[256,2304]{1,0:T(8,128)(2,1)}, bf16[256,2304]{1,0:T(8,128)(2,1)S(1)}, u32[]{:S(2)}) copy-start(bf16[256,2304]{1,0:T(8,128)(2,1)S(1)} %fusion.51) | copy-start | bytes 3538948
  205.3 4.8 %copy-start.17 = (bf16[256,576]{0,1:T(8,128)(2,1)S(1)}, bf16[256,576]{0,1:T(8,128)(2,1)}, u32[]{:S(2)}) copy-start(bf16[256,576]{0,1:T(8,128)(2,1)} %param.15) | copy-start | bytes 884740
  206.6 2.1 collective-permute-start.6
  207.2 4.2 %collective-permute-start.7 = (bf16[256,576]{1,0:T(8,128)(2,1)}, bf16[256,576]{1,0:T(8,128)(2,1)}, u32[]{:S(2)}, u32[]{:S(2)}) collective-permute-start(bf16[256,576]{1,0:T(8,128)(2,1)} %get-tuple-element.60), channel_id=1, source_target_pairs={{0,64},{32,96},{64,0},{96,32},{1,65},{33,97},{65,1},{97,33},{2,66}... | collective-permute-start | bytes 884744 | tf_op jit(solution)/shard_map/ppermute | solution.py:19
  208.6 2.8 collective-permute-start.8
  211.4 3.0 copy-start
  213.1 21.3 %collective-permute-start.9 = (bf16[256,576]{1,0:T(8,128)(2,1)S(1)}, bf16[256,576]{1,0:T(8,128)(2,1)S(1)}, u32[]{:S(2)}, u32[]{:S(2)}) collective-permute-start(bf16[256,576]{1,0:T(8,128)(2,1)S(1)} %fusion.57), channel_id=1, source_target_pairs={{0,128},{1,129},{2,130},{3,131},{4,132},{5,133},{6,134},{7,135},{8... | collective-permute-start | bytes 884744 | tf_op jit(solution)/shard_map/ppermute | solution.py:112
  234.4 11.8 %collective-permute-start.10 = (bf16[256,576]{1,0:T(8,128)(2,1)S(1)}, bf16[256,576]{1,0:T(8,128)(2,1)S(1)}, u32[]{:S(2)}, u32[]{:S(2)}) collective-permute-start(bf16[256,576]{1,0:T(8,128)(2,1)S(1)} %collective-permute-done.9), channel_id=1, source_target_pairs={{128,224},{160,128},{192,160},{224,192},{129,225},{161,129},{193,1... | collective-permute-start | bytes 884744 | tf_op jit(solution)/shard_map/ppermute | solution.py:19
  238.6 9.4 %collective-permute-start.11 = (bf16[256,576]{1,0:T(8,128)(2,1)S(1)}, bf16[256,576]{1,0:T(8,128)(2,1)S(1)}, u32[]{:S(2)}, u32[]{:S(2)}) collective-permute-start(bf16[256,576]{1,0:T(8,128)(2,1)S(1)} %collective-permute-done.9), channel_id=1, source_target_pairs={{128,192},{160,224},{192,128},{224,160},{129,193},{161,225},{193,1... | collective-permute-start | bytes 884744 | tf_op jit(solution)/shard_map/ppermute | solution.py:19
  240.6 10.9 %collective-permute-start.12 = (bf16[256,576]{1,0:T(8,128)(2,1)S(1)}, bf16[256,576]{1,0:T(8,128)(2,1)S(1)}, u32[]{:S(2)}, u32[]{:S(2)}) collective-permute-start(bf16[256,576]{1,0:T(8,128)(2,1)S(1)} %collective-permute-done.9), channel_id=1, source_target_pairs={{128,160},{160,192},{192,224},{224,128},{129,161},{161,193},{193,2... | collective-permute-start | bytes 884744 | tf_op jit(solution)/shard_map/ppermute | solution.py:19
  269.8 1.7 copy-start.12
  269.8 2.0 copy-start.13
  270.0 5.9 %copy-start.14 = (bf16[256,2048]{1,0:T(8,128)(2,1)}, bf16[256,2048]{1,0:T(8,128)(2,1)S(1)}, u32[]{:S(2)}) copy-start(bf16[256,2048]{1,0:T(8,128)(2,1)S(1)} %broadcast_select_fusion) | copy-start | bytes 3145732
  275.9 7.4 %copy-start.15 = (bf16[256,2048]{1,0:T(8,128)(2,1)S(1)}, bf16[256,2048]{1,0:T(8,128)(2,1)}, u32[]{:S(2)}) copy-start(bf16[256,2048]{1,0:T(8,128)(2,1)} %copy-done.14) | copy-start | bytes 3145732
  283.3 10.0 %copy-start.4 = (f32[256,2304]{1,0:T(8,128)S(1)}, f32[256,2304]{1,0:T(8,128)}, u32[]{:S(2)}) copy-start(f32[256,2304]{1,0:T(8,128)} %copy.82) | copy-start | bytes 7077892
  288.5 14.2 %collective-permute-start.19 = (bf16[256,576]{1,0:T(8,128)(2,1)S(1)}, bf16[256,576]{1,0:T(8,128)(2,1)S(1)}, u32[]{:S(2)}, u32[]{:S(2)}) collective-permute-start(bf16[256,576]{1,0:T(8,128)(2,1)S(1)} %get-tuple-element.55), channel_id=1, source_target_pairs={{0,32},{32,64},{64,96},{96,0},{1,33},{33,65},{65,97},{97,1},{2,34}... | collective-permute-start | bytes 884744 | tf_op jit(solution)/shard_map/ppermute | solution.py:15
  289.7 16.4 %collective-permute-start.20 = (bf16[256,576]{1,0:T(8,128)(2,1)S(1)}, bf16[256,576]{1,0:T(8,128)(2,1)S(1)}, u32[]{:S(2)}, u32[]{:S(2)}) collective-permute-start(bf16[256,576]{1,0:T(8,128)(2,1)S(1)} %get-tuple-element.57), channel_id=1, source_target_pairs={{0,64},{32,96},{64,0},{96,32},{1,65},{33,97},{65,1},{97,33},{2,66}... | collective-permute-start | bytes 884744 | tf_op jit(solution)/shard_map/ppermute | solution.py:15
  292.1 14.0 %collective-permute-start.21 = (bf16[256,576]{1,0:T(8,128)(2,1)S(1)}, bf16[256,576]{1,0:T(8,128)(2,1)S(1)}, u32[]{:S(2)}, u32[]{:S(2)}) collective-permute-start(bf16[256,576]{1,0:T(8,128)(2,1)S(1)} %get-tuple-element.56), channel_id=1, source_target_pairs={{0,96},{32,0},{64,32},{96,64},{1,97},{33,1},{65,33},{97,65},{2,98}... | collective-permute-start | bytes 884744 | tf_op jit(solution)/shard_map/ppermute | solution.py:15
  297.1 9.2 %copy-start.6 = (bf16[256,2304]{1,0:T(8,128)(2,1)}, bf16[256,2304]{1,0:T(8,128)(2,1)S(1)}, u32[]{:S(2)}) copy-start(bf16[256,2304]{1,0:T(8,128)(2,1)S(1)} %fusion.48) | copy-start | bytes 3538948
  297.6 12.0 %collective-permute-start.13 = (bf16[256,576]{1,0:T(8,128)(2,1)S(1)}, bf16[256,576]{1,0:T(8,128)(2,1)S(1)}, u32[]{:S(2)}, u32[]{:S(2)}) collective-permute-start(bf16[256,576]{1,0:T(8,128)(2,1)S(1)} %get-tuple-element.52), channel_id=1, source_target_pairs={{128,160},{160,192},{192,224},{224,128},{129,161},{161,193},{193,2... | collective-permute-start | bytes 884744 | tf_op jit(solution)/shard_map/ppermute | solution.py:19
  299.8 14.4 %collective-permute-start.14 = (bf16[256,576]{1,0:T(8,128)(2,1)S(1)}, bf16[256,576]{1,0:T(8,128)(2,1)}, u32[]{:S(2)}, u32[]{:S(2)}) collective-permute-start(bf16[256,576]{1,0:T(8,128)(2,1)S(1)} %get-tuple-element.54), channel_id=1, source_target_pairs={{128,192},{160,224},{192,128},{224,160},{129,193},{161,225},{193,1... | collective-permute-start | bytes 884744 | tf_op jit(solution)/shard_map/ppermute | solution.py:19
  302.7 11.6 %collective-permute-start.15 = (bf16[256,576]{1,0:T(8,128)(2,1)S(1)}, bf16[256,576]{1,0:T(8,128)(2,1)}, u32[]{:S(2)}, u32[]{:S(2)}) collective-permute-start(bf16[256,576]{1,0:T(8,128)(2,1)S(1)} %get-tuple-element.53), channel_id=1, source_target_pairs={{128,224},{160,128},{192,160},{224,192},{129,225},{161,129},{193,1... | collective-permute-start | bytes 884744 | tf_op jit(solution)/shard_map/ppermute | solution.py:19
  306.4 8.9 %collective-permute-start.22 = (bf16[256,576]{1,0:T(8,128)(2,1)S(1)}, bf16[256,576]{1,0:T(8,128)(2,1)S(1)}, u32[]{:S(2)}, u32[]{:S(2)}) collective-permute-start(bf16[256,576]{1,0:T(8,128)(2,1)S(1)} %add_convert_fusion), channel_id=1, source_target_pairs={{0,128},{1,129},{2,130},{3,131},{4,132},{5,133},{6,134},{7,135},{8... | collective-permute-start | bytes 884744 | tf_op jit(solution)/shard_map/ppermute | solution.py:120
Sparse Core Ops, SparseCore 0:
  10.3 37.6 all-gather.6
  49.8 38.2 all-gather.8
  91.2 109.4 all-gather.10
  203.1 80.1 all-gather.12

commit v5 on v4

--- a/solution.py
+++ b/solution.py
@@ -6,7 +6,6 @@
 BLOCK = 128
 TILE = 128
 GROUP = ("layer", "feat")
-SPLIT = 1024
 TOK = ("tz", "ty")
 
 
@@ -58,30 +57,8 @@
     return (jax.nn.relu(preact) * mask).astype(jnp.bfloat16)
 
 
-def gather_columns(shard):
-    n_y = lax.axis_size("ty")
-    y_index = lax.axis_index("ty")
-    by_gather = lax.all_gather(shard[:SPLIT], TOK, axis=1, tiled=True)
-    along_z = lax.all_gather(shard[SPLIT:], "tz", axis=0)
-    received = [along_z] + [
-        lax.ppermute(along_z, "ty", [(i, (i + k) % n_y) for i in range(n_y)]) for k in range(1, n_y)
-    ]
-    blocks = []
-    for j in range(n_y):
-        block = jnp.zeros_like(along_z)
-        for k in range(n_y):
-            block = jnp.where((y_index - k) % n_y == j, received[k], block)
-        blocks.append(block)
-    return by_gather, jnp.stack(blocks, axis=1)
-
-
 def decode(features, full):
-    by_gather, by_rest = full
-    first = jnp.dot(features[:, :SPLIT], by_gather, preferred_element_type=jnp.float32)
-    second = jnp.einsum(
-        "tf,zyfc->tzyc", features[:, SPLIT:], by_rest, preferred_element_type=jnp.float32
-    )
-    return (first + second.reshape(first.shape)).astype(jnp.bfloat16)
+    return jnp.dot(features, full, preferred_element_type=jnp.float32).astype(jnp.bfloat16)
 
 
 def shards(
@@ -92,8 +69,8 @@
     feat_index = lax.axis_index("feat")
     blocks_dev = enc_weight.shape[2] // BLOCK
     first_core = section_index == 0
-    own_full = gather_columns(dec_own[0])
-    next_full = gather_columns(dec_next[0])
+    own_full = lax.all_gather(dec_own[0], TOK, axis=1, tiled=True)
+    next_full = lax.all_gather(dec_next[0], TOK, axis=1, tiled=True)
     mask = feature_mask(block_list, block_count, feat_index, blocks_dev)
     attention = attn_out[0].astype(jnp.float32)
 

time: 326 us -> 265 us (0.81)
  waiting for transfers between devices: 196 us -> 167 us
  local copies, waits for them, and re-layouts: 29.6 us -> 17.8 us
  other arithmetic: 15.3 us -> 7.73 us
  starting transfers between devices: 37 us -> 30.1 us
  matrix products: 32.3 us -> 27.2 us
    ppermute x6 -> x0, waiting for transfers between devices: 21 us -> none  [gather_columns(): lax.ppermute(along_z, 'ty', [(i, (i + k) % n_y) for i in range(n_y)])]
    reshape x3 -> x0, local copies, waits for them, and re-layouts: 9.46 us -> none  [decode(): return (first + second.reshape(first.shape)).astype(jnp.bfloat16)]
    another operation x4 -> x0, other arithmetic: 9.38 us -> none  [gather_columns(): return (by_gather, jnp.stack(blocks, axis=1))]
    all_gather x4 -> x2, waiting for transfers between devices: 145 us -> 138 us  [the longest x1 93.8 us: shards(): own_full = lax.all_gather(dec_own[0], TOK, axis=1, tiled=True)]
    ppermute x6 -> x0, starting transfers between devices: 6.8 us -> none  [gather_columns(): lax.ppermute(along_z, 'ty', [(i, (i + k) % n_y) for i in range(n_y)])]
    dot_general x6 -> x3, matrix products: 25 us -> 19.7 us  [decode(): jnp.dot(features, full, preferred_element_type=jnp.float32)]
    slice x2 -> x0, local copies, waits for them, and re-layouts: 3.46 us -> none  [gather_columns(): by_gather = lax.all_gather(shard[:SPLIT], TOK, axis=1, tiled=True)]
    unnamed x48 -> x30, local copies, waits for them, and re-layouts: 8.24 us -> 7.59 us
  transfers between devices with their start and end apart: 27 -> 19, of which waited for: 12 -> 8; matrix products, arithmetic and copies ran while one was open for 20% -> 15% of each run, Pallas kernels for 0% -> 0%
where the time goes in v5:
time: 265 us
  waiting for transfers between devices  167 us (63%)
  starting transfers between devices  30.1 us (11%)
  matrix products  27.2 us (10%)
  local copies, waits for them, and re-layouts  17.8 us (7%)
  between operations  14.4 us (5%)
  other arithmetic  7.73 us (3%)
    all_gather x1, waiting for transfers between devices, shards(): own_full = lax.all_gather(dec_own[0], TOK, axis=1, tiled=True)  93.8 us
    all_gather x1, waiting for transfers between devices, shards(): next_full = lax.all_gather(dec_next[0], TOK, axis=1, tiled=True)  44 us
    ppermute x12, starting transfers between devices, within_layer(): return lax.ppermute(shard, GROUP, pairs)  22.6 us
    dot_general x3, matrix products, decode(): jnp.dot(features, full, preferred_element_type=jnp.float32)  19.7 us
    ppermute x1, waiting for transfers between devices, shards(): residual_next = lax.ppermute(residual_next, 'layer', [(0, 1)])  15.9 us
    ppermute x12, waiting for transfers between devices, within_layer(): return lax.ppermute(shard, GROUP, pairs)  12.2 us
    unnamed x30, local copies, waits for them, and re-layouts  7.59 us
    dot_general x1, matrix products, encode(): jnp.dot(gathered, enc_weight[0], preferred_element_type=jnp.float32)  7.53 us
  transfers between devices with their start and end apart: 19, of which 8 were waited for; matrix products, arithmetic and copies ran while one was open for 15% of the time, Pallas kernels for 0%

profile of v5, /device:TPU:1, one launch (start us, length us, event | category | flops | bytes accessed | tf_op | source)
XLA Modules:
  0.0 264.6 jit_solution(4357151651610894616)
XLA Ops:
  7.9 0.7 all-gather.7.cloned.1.call-update
  8.6 1.2 copy.23
  9.8 0.7 collective-permute-start
  11.2 1.4 collective-permute-start.2
  12.6 0.7 iota_compare_fusion
  13.3 0.9 and_reduce_fusion
  14.8 0.9 copy.37
  15.8 0.8 copy-done.1
  16.8 2.1 select_select_fusion.4
  18.8 3.1 %concatenate.6 = bf16[256,2304]{1,0:T(8,128)(2,1)} concatenate(bf16[256,576]{1,0:T(8,128)(2,1)S(1)} %select_select_fusion.7, bf16[256,576]{1,0:T(8,128)(2,1)} %get-tuple-element.41, bf16[256,576]{1,0:T(8,128)(2,1)S(1)} %get-tuple-element.40, bf16[256,576]{1,0:T(8,128)(2,1)S(1)} %get-tuple-element.39), dimensions={1} | concatenate | bytes 2359296 | tf_op jit(solution)/shard_map/concatenate | solution.py:29
  22.0 1.1 conditional.2
  22.0 1.1 broadcast.25
  23.1 93.8 %all-gather.5.cloned.1.call-done = bf16[1,2048,2304]{1,2,0:T(8,128)(2,1)} async-done(((bf16[1,2048,72]{1,2,0:T(8,128)(2,1)}), bf16[1,2048,2304]{1,2,0:T(8,128)(2,1)}) %all-gather.5.cloned.1.call-update) | async-done | bytes 9437200 | tf_op jit(solution)/shard_map/all_gather | solution.py:72
  116.8 6.7 %fusion.34 = bf16[256,2304]{1,0:T(8,128)(2,1)S(1)} fusion(bf16[256,2048]{1,0:T(8,128)(2,1)} %get-tuple-element.51, bf16[1,2048,2304]{1,2,0:T(8,128)(2,1)} %all-gather.5.cloned.1.call-done), kind=kOutput, calls=%fused_computation.18 | convolution fusion | flops 2416508928 | bytes 11665408 | tf_op jit(solution)/shard_map/dot_general | solution.py:61
  123.5 1.3 constant_dynamic-slice_fusion.8
  125.5 0.7 collective-permute-start.4
  126.2 0.7 collective-permute-start.5
  127.1 1.2 copy.32
  128.3 0.8 copy-done.8
  129.5 1.3 collective-permute-start.6
  130.8 15.9 %collective-permute-done.6 = bf16[256,576]{1,0:T(8,128)(2,1)S(1)} collective-permute-done((bf16[256,576]{1,0:T(8,128)(2,1)S(1)}, bf16[256,576]{1,0:T(8,128)(2,1)S(1)}, u32[]{:S(2)}, u32[]{:S(2)}) %collective-permute-start.6) | collective-permute-done | bytes 294944 | tf_op jit(solution)/shard_map/ppermute | solution.py:89
  146.6 4.3 %collective-permute-start.7 = (bf16[256,576]{1,0:T(8,128)(2,1)S(1)}, bf16[256,576]{1,0:T(8,128)(2,1)S(1)}, u32[]{:S(2)}, u32[]{:S(2)}) collective-permute-start(bf16[256,576]{1,0:T(8,128)(2,1)S(1)} %collective-permute-done.6), channel_id=1, source_target_pairs={{128,224},{160,128},{192,160},{224,192},{129,225},{161,129},{193,1... | collective-permute-start | bytes 884744 | tf_op jit(solution)/shard_map/ppermute | solution.py:18
  150.9 3.1 %collective-permute-start.8 = (bf16[256,576]{1,0:T(8,128)(2,1)S(1)}, bf16[256,576]{1,0:T(8,128)(2,1)S(1)}, u32[]{:S(2)}, u32[]{:S(2)}) collective-permute-start(bf16[256,576]{1,0:T(8,128)(2,1)S(1)} %collective-permute-done.6), channel_id=1, source_target_pairs={{128,192},{160,224},{192,128},{224,160},{129,193},{161,225},{193,1... | collective-permute-start | bytes 884744 | tf_op jit(solution)/shard_map/ppermute | solution.py:18
  154.1 1.9 collective-permute-start.9
  156.0 2.4 collective-permute-done.7
  158.4 1.9 collective-permute-done.8
  160.3 3.4 %collective-permute-done.9 = bf16[256,576]{1,0:T(8,128)(2,1)S(1)} collective-permute-done((bf16[256,576]{1,0:T(8,128)(2,1)S(1)}, bf16[256,576]{1,0:T(8,128)(2,1)S(1)}, u32[]{:S(2)}, u32[]{:S(2)}) %collective-permute-start.9) | collective-permute-done | bytes 294944 | tf_op jit(solution)/shard_map/ppermute | solution.py:18
  163.8 0.7 copy-done.4
  164.6 1.3 select_select_fusion
  165.9 2.2 concatenate.7
  168.1 7.5 %conditional.3 = (bf16[256,2048]{1,0:T(8,128)(2,1)S(1)}) conditional(s32[]{:T(128)} %convert_element_type.92, () %tuple.22, (bf16[1,2304,2048]{2,1,0:T(8,128)(2,1)}, bf16[256,2304]{1,0:T(8,128)(2,1)}, f32[1,2048]{1,0:T(1,128)S(1)}, f32[256,2048]{1,0:T(8,128)}) %tuple.48), branch_computations={%region_3.4_spmd, %region_4.5_spmd} | conditional | flops 2418016256 | bytes 13770760 | solution.py:78
  168.1 7.5 %fusion.25 = bf16[256,2048]{1,0:T(8,128)(2,1)S(1)} fusion(f32[256,2048]{1,0:T(8,128)} %get-tuple-element.29, bf16[256,2304]{1,0:T(8,128)(2,1)} %get-tuple-element.26, bf16[1,2304,2048]{2,1,0:T(8,128)(2,1)} %get-tuple-element.27, f32[2048]{0:T(1024)S(1)} %bitcast.62), kind=kOutput, calls=%fused_computation.11 | convolution fusion | flops 2418016256 | bytes 13770752 | tf_op jit(solution)/shard_map/cond/branch_1_fun/dot_general | solution.py:55
  175.7 44.0 %all-gather.7.cloned.1.call-done = bf16[1,2048,2304]{1,2,0:T(8,128)(2,1)} async-done(((bf16[1,2048,72]{1,2,0:T(8,128)(2,1)}), bf16[1,2048,2304]{1,2,0:T(8,128)(2,1)}) %all-gather.7.cloned.1.call-update) | async-done | bytes 9437200 | tf_op jit(solution)/shard_map/all_gather | solution.py:73
  219.7 6.4 %fusion.40 = bf16[256,2304]{1,0:T(8,128)(2,1)S(1)} fusion(bf16[1,2048,2304]{1,2,0:T(8,128)(2,1)} %all-gather.7.cloned.1.call-done, bf16[256,2048]{1,0:T(8,128)(2,1)} %get-tuple-element.51, bf16[256,2048]{1,0:T(8,128)(2,1)S(1)} %get-tuple-element.52, pred[]{:T(512)S(6)} %eq.128), kind=kOutput, calls=%fused_computation.20 | convolution fusion | flops 2417033216 | bytes 12713985 | tf_op jit(solution)/shard_map/dot_general | solution.py:61
  226.5 1.3 collective-permute-start.13
  227.8 2.4 collective-permute-start.14
  230.2 1.2 collective-permute-start.15
  231.4 6.7 %fusion.37 = bf16[256,2304]{1,0:T(8,128)(2,1)S(1)} fusion(bf16[256,2048]{1,0:T(8,128)(2,1)} %copy-done.9, bf16[1,2048,2304]{1,2,0:T(8,128)(2,1)} %all-gather.5.cloned.1.call-done), kind=kOutput, calls=%fused_computation.19 | convolution fusion | flops 2416508928 | bytes 11665408 | tf_op jit(solution)/shard_map/dot_general | solution.py:61
  238.0 1.4 constant_dynamic-slice_fusion.5
  239.4 2.2 collective-permute-start.10
  241.6 2.8 %collective-permute-start.11 = (bf16[256,576]{1,0:T(8,128)(2,1)}, bf16[256,576]{1,0:T(8,128)(2,1)}, u32[]{:S(2)}, u32[]{:S(2)}) collective-permute-start(bf16[256,576]{1,0:T(8,128)(2,1)} %get-tuple-element.44), channel_id=1, source_target_pairs={{128,192},{160,224},{192,128},{224,160},{129,193},{161,225},{193,1... | collective-permute-start | bytes 884744 | tf_op jit(solution)/shard_map/ppermute | solution.py:18
  244.5 3.4 %collective-permute-start.12 = (bf16[256,576]{1,0:T(8,128)(2,1)}, bf16[256,576]{1,0:T(8,128)(2,1)}, u32[]{:S(2)}, u32[]{:S(2)}) collective-permute-start(bf16[256,576]{1,0:T(8,128)(2,1)} %get-tuple-element.43), channel_id=1, source_target_pairs={{128,224},{160,128},{192,160},{224,192},{129,225},{161,129},{193,1... | collective-permute-start | bytes 884744 | tf_op jit(solution)/shard_map/ppermute | solution.py:18
  248.2 1.3 collective-permute-start.16
  249.5 0.9 copy.34
  250.4 2.7 %collective-permute-done.10 = bf16[256,576]{1,0:T(8,128)(2,1)} collective-permute-done((bf16[256,576]{1,0:T(8,128)(2,1)}, bf16[256,576]{1,0:T(8,128)(2,1)}, u32[]{:S(2)}, u32[]{:S(2)}) %collective-permute-start.10) | collective-permute-done | bytes 294944 | tf_op jit(solution)/shard_map/ppermute | solution.py:18
  253.1 1.7 collective-permute-done.12
  254.8 2.0 fusion.47
  256.8 0.9 copy.33
  (47 shorter events, 4.4 us)
Async XLA Ops:
  7.2 109.7 %all-gather.5.cloned.1.call-start = ((), (), s32[]{:S(2)}) async-start(), calls=%async_computation | async-start | bytes 9732096 | tf_op jit(solution)/shard_map/all_gather | solution.py:72
  7.9 211.8 %all-gather.7.cloned.1.call-start = ((), (), s32[]{:S(2)}) async-start(), calls=%async_computation.1 | async-start | bytes 9732096 | tf_op jit(solution)/shard_map/all_gather | solution.py:73
  9.8 5.9 %collective-permute-start = (bf16[256,576]{1,0:T(8,128)(2,1)S(1)}, bf16[256,576]{1,0:T(8,128)(2,1)S(1)}, u32[]{:S(2)}, u32[]{:S(2)}) collective-permute-start(bf16[256,576]{1,0:T(8,128)(2,1)S(1)} %copy.23), channel_id=1, source_target_pairs={{0,96},{32,0},{64,32},{96,64},{1,97},{33,1},{65,33},{97,65},{2,98}... | collective-permute-start | bytes 884744 | tf_op jit(solution)/shard_map/ppermute | solution.py:18
  10.5 5.3 %collective-permute-start.1 = (bf16[256,576]{1,0:T(8,128)(2,1)S(1)}, bf16[256,576]{1,0:T(8,128)(2,1)S(1)}, u32[]{:S(2)}, u32[]{:S(2)}) collective-permute-start(bf16[256,576]{1,0:T(8,128)(2,1)S(1)} %copy.23), channel_id=1, source_target_pairs={{0,64},{32,96},{64,0},{96,32},{1,65},{33,97},{65,1},{97,33},{2,66}... | collective-permute-start | bytes 884744 | tf_op jit(solution)/shard_map/ppermute | solution.py:18
  11.2 4.6 %collective-permute-start.2 = (bf16[256,576]{1,0:T(8,128)(2,1)S(1)}, bf16[256,576]{1,0:T(8,128)(2,1)}, u32[]{:S(2)}, u32[]{:S(2)}) collective-permute-start(bf16[256,576]{1,0:T(8,128)(2,1)S(1)} %copy.23), channel_id=1, source_target_pairs={{0,32},{32,64},{64,96},{96,0},{1,33},{33,65},{65,97},{97,1},{2,34}... | collective-permute-start | bytes 884744 | tf_op jit(solution)/shard_map/ppermute | solution.py:18
  15.7 6.3 %copy-start = (f32[32,8,16,128]{3,1,2,0:T(8,128)}, f32[32,8,16,128]{3,1,2,0:T(8,128)S(1)}, u32[]{:S(2)}) copy-start(f32[32,8,16,128]{3,1,2,0:T(8,128)S(1)} %copy.37) | copy-start | bytes 6291460
  15.8 0.8 copy-start.1
  15.8 0.9 copy-start.2
  16.7 5.2 %copy-start.11 = (f32[1,2048]{1,0:T(1,128)S(1)}, f32[1,2048]{1,0:T(1,128)}, u32[]{:S(2)}) copy-start(f32[1,2048]{1,0:T(1,128)} %param.17) | copy-start | bytes 24580
  123.5 3.4 %copy-start.10 = (bf16[256,576]{0,1:T(8,128)(2,1)S(1)}, bf16[256,576]{0,1:T(8,128)(2,1)}, u32[]{:S(2)}) copy-start(bf16[256,576]{0,1:T(8,128)(2,1)} %param.15) | copy-start | bytes 884740
  124.8 3.4 %collective-permute-start.3 = (bf16[256,576]{1,0:T(8,128)(2,1)}, bf16[256,576]{1,0:T(8,128)(2,1)S(1)}, u32[]{:S(2)}, u32[]{:S(2)}) collective-permute-start(bf16[256,576]{1,0:T(8,128)(2,1)} %get-tuple-element.48), channel_id=1, source_target_pairs={{0,32},{32,64},{64,96},{96,0},{1,33},{33,65},{65,97},{97,1},{2,34}... | collective-permute-start | bytes 884744 | tf_op jit(solution)/shard_map/ppermute | solution.py:18
  125.5 2.8 %collective-permute-start.4 = (bf16[256,576]{1,0:T(8,128)(2,1)}, bf16[256,576]{1,0:T(8,128)(2,1)S(1)}, u32[]{:S(2)}, u32[]{:S(2)}) collective-permute-start(bf16[256,576]{1,0:T(8,128)(2,1)} %get-tuple-element.50), channel_id=1, source_target_pairs={{0,64},{32,96},{64,0},{96,32},{1,65},{33,97},{65,1},{97,33},{2,66}... | collective-permute-start | bytes 884744 | tf_op jit(solution)/shard_map/ppermute | solution.py:18
  126.2 2.1 collective-permute-start.5
  128.3 22.7 %copy-start.5 = (bf16[256,576]{1,0:T(8,128)(2,1)}, bf16[256,576]{1,0:T(8,128)(2,1)S(1)}, u32[]{:S(2)}) copy-start(bf16[256,576]{1,0:T(8,128)(2,1)S(1)} %collective-permute-done.3) | copy-start | bytes 884740
  128.3 35.5 %copy-start.7 = (bf16[256,576]{1,0:T(8,128)(2,1)}, bf16[256,576]{1,0:T(8,128)(2,1)S(1)}, u32[]{:S(2)}) copy-start(bf16[256,576]{1,0:T(8,128)(2,1)S(1)} %collective-permute-done.4) | copy-start | bytes 884740
  128.3 0.8 copy-start.8
  129.5 17.2 %collective-permute-start.6 = (bf16[256,576]{1,0:T(8,128)(2,1)S(1)}, bf16[256,576]{1,0:T(8,128)(2,1)S(1)}, u32[]{:S(2)}, u32[]{:S(2)}) collective-permute-start(bf16[256,576]{1,0:T(8,128)(2,1)S(1)} %fusion.46), channel_id=1, source_target_pairs={{0,128},{1,129},{2,130},{3,131},{4,132},{5,133},{6,134},{7,135},{8... | collective-permute-start | bytes 884744 | tf_op jit(solution)/shard_map/ppermute | solution.py:89
  146.6 11.8 %collective-permute-start.7 = (bf16[256,576]{1,0:T(8,128)(2,1)S(1)}, bf16[256,576]{1,0:T(8,128)(2,1)S(1)}, u32[]{:S(2)}, u32[]{:S(2)}) collective-permute-start(bf16[256,576]{1,0:T(8,128)(2,1)S(1)} %collective-permute-done.6), channel_id=1, source_target_pairs={{128,224},{160,128},{192,160},{224,192},{129,225},{161,129},{193,1... | collective-permute-start | bytes 884744 | tf_op jit(solution)/shard_map/ppermute | solution.py:18
  150.9 9.4 %collective-permute-start.8 = (bf16[256,576]{1,0:T(8,128)(2,1)S(1)}, bf16[256,576]{1,0:T(8,128)(2,1)S(1)}, u32[]{:S(2)}, u32[]{:S(2)}) collective-permute-start(bf16[256,576]{1,0:T(8,128)(2,1)S(1)} %collective-permute-done.6), channel_id=1, source_target_pairs={{128,192},{160,224},{192,128},{224,160},{129,193},{161,225},{193,1... | collective-permute-start | bytes 884744 | tf_op jit(solution)/shard_map/ppermute | solution.py:18
  154.1 9.7 %collective-permute-start.9 = (bf16[256,576]{1,0:T(8,128)(2,1)S(1)}, bf16[256,576]{1,0:T(8,128)(2,1)S(1)}, u32[]{:S(2)}, u32[]{:S(2)}) collective-permute-start(bf16[256,576]{1,0:T(8,128)(2,1)S(1)} %collective-permute-done.6), channel_id=1, source_target_pairs={{128,160},{160,192},{192,224},{224,128},{129,161},{161,193},{193,2... | collective-permute-start | bytes 884744 | tf_op jit(solution)/shard_map/ppermute | solution.py:18
  160.3 3.4 %copy-start.3 = (bf16[256,576]{1,0:T(8,128)(2,1)}, bf16[256,576]{1,0:T(8,128)(2,1)S(1)}, u32[]{:S(2)}) copy-start(bf16[256,576]{1,0:T(8,128)(2,1)S(1)} %collective-permute-done.8) | copy-start | bytes 884740
  163.8 0.7 copy-start.4
  175.6 50.4 %copy-start.9 = (bf16[256,2048]{1,0:T(8,128)(2,1)}, bf16[256,2048]{1,0:T(8,128)(2,1)S(1)}, u32[]{:S(2)}) copy-start(bf16[256,2048]{1,0:T(8,128)(2,1)S(1)} %get-tuple-element.52) | copy-start | bytes 3145732
  226.5 17.9 %collective-permute-start.13 = (bf16[256,576]{1,0:T(8,128)(2,1)S(1)}, bf16[256,576]{1,0:T(8,128)(2,1)S(1)}, u32[]{:S(2)}, u32[]{:S(2)}) collective-permute-start(bf16[256,576]{1,0:T(8,128)(2,1)S(1)} %get-tuple-element.45), channel_id=1, source_target_pairs={{0,32},{32,64},{64,96},{96,0},{1,33},{33,65},{65,97},{97,1},{2,34}... | collective-permute-start | bytes 884744 | tf_op jit(solution)/shard_map/ppermute | solution.py:14
  227.8 20.1 %collective-permute-start.14 = (bf16[256,576]{1,0:T(8,128)(2,1)S(1)}, bf16[256,576]{1,0:T(8,128)(2,1)S(1)}, u32[]{:S(2)}, u32[]{:S(2)}) collective-permute-start(bf16[256,576]{1,0:T(8,128)(2,1)S(1)} %get-tuple-element.47), channel_id=1, source_target_pairs={{0,64},{32,96},{64,0},{96,32},{1,65},{33,97},{65,1},{97,33},{2,66}... | collective-permute-start | bytes 884744 | tf_op jit(solution)/shard_map/ppermute | solution.py:14
  230.2 17.7 %collective-permute-start.15 = (bf16[256,576]{1,0:T(8,128)(2,1)S(1)}, bf16[256,576]{1,0:T(8,128)(2,1)S(1)}, u32[]{:S(2)}, u32[]{:S(2)}) collective-permute-start(bf16[256,576]{1,0:T(8,128)(2,1)S(1)} %get-tuple-element.46), channel_id=1, source_target_pairs={{0,96},{32,0},{64,32},{96,64},{1,97},{33,1},{65,33},{97,65},{2,98}... | collective-permute-start | bytes 884744 | tf_op jit(solution)/shard_map/ppermute | solution.py:14
  238.0 16.8 %copy-start.6 = (bf16[256,576]{1,0:T(8,128)(2,1)S(1)}, bf16[256,576]{1,0:T(8,128)(2,1)}, u32[]{:S(2)}) copy-start(bf16[256,576]{1,0:T(8,128)(2,1)} %copy-done.5) | copy-start | bytes 884740
  239.4 13.6 %collective-permute-start.10 = (bf16[256,576]{1,0:T(8,128)(2,1)}, bf16[256,576]{1,0:T(8,128)(2,1)}, u32[]{:S(2)}, u32[]{:S(2)}) collective-permute-start(bf16[256,576]{1,0:T(8,128)(2,1)} %get-tuple-element.42), channel_id=1, source_target_pairs={{128,160},{160,192},{192,224},{224,128},{129,161},{161,193},{193,2... | collective-permute-start | bytes 884744 | tf_op jit(solution)/shard_map/ppermute | solution.py:18
  241.6 11.4 %collective-permute-start.11 = (bf16[256,576]{1,0:T(8,128)(2,1)}, bf16[256,576]{1,0:T(8,128)(2,1)}, u32[]{:S(2)}, u32[]{:S(2)}) collective-permute-start(bf16[256,576]{1,0:T(8,128)(2,1)} %get-tuple-element.44), channel_id=1, source_target_pairs={{128,192},{160,224},{192,128},{224,160},{129,193},{161,225},{193,1... | collective-permute-start | bytes 884744 | tf_op jit(solution)/shard_map/ppermute | solution.py:18
  244.5 10.4 %collective-permute-start.12 = (bf16[256,576]{1,0:T(8,128)(2,1)}, bf16[256,576]{1,0:T(8,128)(2,1)}, u32[]{:S(2)}, u32[]{:S(2)}) collective-permute-start(bf16[256,576]{1,0:T(8,128)(2,1)} %get-tuple-element.43), channel_id=1, source_target_pairs={{128,224},{160,128},{192,160},{224,192},{129,225},{161,129},{193,1... | collective-permute-start | bytes 884744 | tf_op jit(solution)/shard_map/ppermute | solution.py:18
  248.2 6.6 %collective-permute-start.16 = (bf16[256,576]{1,0:T(8,128)(2,1)S(1)}, bf16[256,576]{1,0:T(8,128)(2,1)}, u32[]{:S(2)}, u32[]{:S(2)}) collective-permute-start(bf16[256,576]{1,0:T(8,128)(2,1)S(1)} %add_convert_fusion), channel_id=1, source_target_pairs={{0,128},{1,129},{2,130},{3,131},{4,132},{5,133},{6,134},{7,135},{8... | collective-permute-start | bytes 884744 | tf_op jit(solution)/shard_map/ppermute | solution.py:97
Sparse Core Ops, SparseCore 0:
  10.5 106.2 all-gather.4
  119.4 100.1 all-gather.6

commit v6 on v2

--- a/solution.py
+++ b/solution.py
@@ -40,6 +40,20 @@
     return total
 
 
+def decode_scatter(features, decoder, feat_index, n_feat):
+    cols = decoder.shape[1] // n_feat
+    total = None
+    for k in sorted(range(n_feat), key=lambda shift: (-min(shift, n_feat - shift), shift)):
+        target = (feat_index + k) % n_feat
+        chunk = lax.dynamic_slice_in_dim(decoder, target * cols, cols, 1)
+        piece = jnp.dot(features, chunk, preferred_element_type=jnp.float32).astype(jnp.bfloat16)
+        if k:
+            piece = within_layer(piece, None, k, n_feat)
+        piece = piece.astype(jnp.float32)
+        total = piece if total is None else total + piece
+    return total
+
+
 def feature_mask(block_list, block_count, feat_index, blocks_dev):
     listed = block_list[0]
     in_use = jnp.arange(listed.shape[1], dtype=jnp.int32)[None, :] < block_count[0][:, None]
@@ -64,8 +78,9 @@
     feat_index = lax.axis_index("feat")
     blocks_dev = enc_weight.shape[2] // BLOCK
     first_core = section_index == 0
-    first_dec = jnp.where(first_core, dec_own[0], lax.ppermute(dec_next[0], "layer", [(0, 1)]))
-    second_dec = jnp.where(first_core, lax.ppermute(dec_next[0], "layer", [(1, 0)]), dec_own[0])
+    swapped_next = lax.ppermute(dec_next[0], "layer", [(0, 1), (1, 0)])
+    first_dec = jnp.where(first_core, dec_own[0], swapped_next)
+    second_dec = jnp.where(first_core, swapped_next, dec_own[0])
     first_full = lax.all_gather(first_dec, "tok", axis=1, tiled=True)
     second_full = lax.all_gather(second_dec, "tok", axis=1, tiled=True)
     mask = feature_mask(block_list, block_count, feat_index, blocks_dev)
@@ -79,8 +94,7 @@
         gathered,
     )
     features = jnp.where(first_core, features, lax.ppermute(features, "layer", [(0, 1)]))
-    part = jnp.dot(features, first_full, preferred_element_type=jnp.float32).astype(jnp.bfloat16)
-    summed = feat_reduce_scatter(part, None, feat_index, n_feat)
+    summed = decode_scatter(features, first_full, feat_index, n_feat)
     recon_first = summed + carry_in.astype(jnp.float32)
     residual_next = (resid_in.astype(jnp.float32) + attention + recon_first).astype(jnp.bfloat16)
     outgoing_first = summed.astype(jnp.bfloat16)
@@ -96,8 +110,7 @@
         gathered,
     )
     features = jnp.where(first_core, lax.ppermute(features, "layer", [(1, 0)]), features)
-    part = jnp.dot(features, second_full, preferred_element_type=jnp.float32).astype(jnp.bfloat16)
-    summed = feat_reduce_scatter(part, None, feat_index, n_feat)
+    summed = decode_scatter(features, second_full, feat_index, n_feat)
     recon_second = summed + outgoing_first.astype(jnp.float32)
     outgoing_second = lax.ppermute(summed.astype(jnp.bfloat16), "layer", [(0, 1)])
 

time: 263 us -> 255 us (0.970)
  local copies, waits for them, and re-layouts: 15 us -> 2.13 us
  matrix products: 22.2 us -> 30.6 us
  starting transfers between devices: 36.8 us -> 33.4 us
    ppermute x6, waiting for transfers between devices: 24.1 us -> 10.3 us  [within_layer(): lax.ppermute(shard, 'feat', [(i, (i + shift) % n_feat) for i in range(n_f...]
    dot_general x2 -> x8, matrix products: 13.4 us -> 24.3 us  [decode_scatter(): jnp.dot(features, chunk, preferred_element_type=jnp.float32)]
    concatenate x2 -> x0, local copies, waits for them, and re-layouts: 6.35 us -> none  [feat_gather(): return jnp.concatenate(blocks, axis=-1)]
    all_gather x1, waiting for transfers between devices: 43.7 us -> 50 us  [shards(): second_full = lax.all_gather(second_dec, 'tok', axis=1, tiled=True)]
    all_gather x1, waiting for transfers between devices: 68.7 us -> 74 us  [shards(): first_full = lax.all_gather(first_dec, 'tok', axis=1, tiled=True)]
    unnamed x24 -> x11, local copies, waits for them, and re-layouts: 6.11 us -> 1.41 us
    ppermute x2 -> x1, starting transfers between devices: 6.55 us -> 3.29 us  [shards(): swapped_next = lax.ppermute(dec_next[0], 'layer', [(0, 1), (1, 0)])]
    select_n x4, other arithmetic: 3.25 us -> 0.37 us  [feat_gather(): block = jnp.where((feat_index - k) % n_feat == j, received[k], block)]
  transfers between devices with their start and end apart: 20 -> 19, of which waited for: 15 -> 12; matrix products, arithmetic and copies ran while one was open for 12% -> 12% of each run, Pallas kernels for 0% -> 0%
where the time goes in v6:
time: 255 us
  waiting for transfers between devices  168 us (66%)
  starting transfers between devices  33.4 us (13%)
  matrix products  30.6 us (12%)
  between operations  14.4 us (6%)
  other arithmetic  6.15 us (2%)
    all_gather x1, waiting for transfers between devices, shards(): first_full = lax.all_gather(first_dec, 'tok', axis=1, tiled=True)  74 us
    all_gather x1, waiting for transfers between devices, shards(): second_full = lax.all_gather(second_dec, 'tok', axis=1, tiled=True)  50 us
    dot_general x8, matrix products, decode_scatter(): jnp.dot(features, chunk, preferred_element_type=jnp.float32)  24.3 us
    ppermute x1, waiting for transfers between devices, shards(): lax.ppermute(features, 'layer', [(0, 1)])  20 us
    ppermute x6, starting transfers between devices, within_layer(): return lax.ppermute(shard, GROUP, pairs)  12.3 us
    ppermute x6, starting transfers between devices, within_layer(): lax.ppermute(shard, 'feat', [(i, (i + shift) % n_feat) for i in range(n_f...  11 us
    ppermute x6, waiting for transfers between devices, within_layer(): lax.ppermute(shard, 'feat', [(i, (i + shift) % n_feat) for i in range(n_f...  10.3 us
    dot_general x1, matrix products, encode(): jnp.dot(gathered, enc_weight[0], preferred_element_type=jnp.float32)  6.31 us
  transfers between devices with their start and end apart: 19, of which 12 were waited for; matrix products, arithmetic and copies ran while one was open for 12% of the time, Pallas kernels for 0%

profile of v6, /device:TPU:1, one launch (start us, length us, event | category | flops | bytes accessed | tf_op | source)
XLA Modules:
  0.0 254.6 jit_solution(10457294258935740177)
XLA Ops:
  7.2 3.3 %collective-permute-start.4 = (bf16[2048,72]{0,1:T(8,128)(2,1)}, bf16[2048,72]{0,1:T(8,128)(2,1)S(1)}, u32[]{:S(2)}, u32[]{:S(2)}) collective-permute-start(bf16[2048,72]{0,1:T(8,128)(2,1)} %bitcast.59), channel_id=1, source_target_pairs={{0,128},{128,0},{1,129},{129,1},{2,130},{130,2},{3,131},{131,3},{4... | collective-permute-start | bytes 884744 | tf_op jit(solution)/shard_map/ppermute | solution.py:81
  10.5 1.4 collective-permute-done.4
  11.9 1.8 bitcast_select_fusion
  13.8 0.7 all-gather.5.cloned.1.call-update
  14.5 0.7 collective-permute-start
  15.2 0.7 collective-permute-start.1
  15.9 0.7 collective-permute-start.2
  16.7 0.7 iota_compare_fusion
  17.4 0.9 and_reduce_fusion
  18.3 0.6 broadcast_in_dim.16
  18.9 0.9 copy.19
  20.2 0.5 copy-done.4
  20.8 1.3 collective-permute-start.3
  22.1 20.0 %collective-permute-done.3 = bf16[256,2048]{1,0:T(8,128)(2,1)} collective-permute-done((bf16[256,2048]{1,0:T(8,128)(2,1)S(1)}, bf16[256,2048]{1,0:T(8,128)(2,1)}, u32[]{:S(2)}, u32[]{:S(2)}) %collective-permute-start.3) | collective-permute-done | bytes 1048608 | tf_op jit(solution)/shard_map/ppermute | solution.py:96
  42.1 1.3 broadcast_select_fusion.1
  43.4 74.0 %all-gather.3.cloned.1.call-done = bf16[2048,2304]{0,1:T(8,128)(2,1)} async-done(((bf16[2048,72]{0,1:T(8,128)(2,1)}), bf16[2048,2304]{0,1:T(8,128)(2,1)}) %all-gather.3.cloned.1.call-update) | async-done | bytes 9437200 | tf_op jit(solution)/shard_map/all_gather | solution.py:84
  117.4 3.2 %fusion.44 = bf16[256,576]{0,1:T(8,128)(2,1)} fusion(bf16[256,2048]{1,0:T(8,128)(2,1)S(1)} %broadcast_select_fusion.1, bf16[2048,2304]{0,1:T(8,128)(2,1)} %all-gather.3.cloned.1.call-done, s32[]{:T(128)S(6)} %select_n.357), kind=kOutput, calls=%fused_computation.29 | convolution fusion | flops 604127232 | bytes 3702788 | tf_op jit(solution)/shard_map/dot_general | solution.py:49
  120.6 2.7 %collective-permute-start.5 = (bf16[256,576]{0,1:T(8,128)(2,1)}, bf16[256,576]{0,1:T(8,128)(2,1)}, u32[]{:S(2)}, u32[]{:S(2)}) collective-permute-start(bf16[256,576]{0,1:T(8,128)(2,1)} %fusion.44), channel_id=1, source_target_pairs={{0,64},{32,96},{64,0},{96,32},{1,65},{33,97},{65,1},{97,33},{2,66}... | collective-permute-start | bytes 884744 | tf_op jit(solution)/shard_map/ppermute | solution.py:13
  123.3 3.2 %fusion.47 = bf16[256,576]{0,1:T(8,128)(2,1)} fusion(bf16[256,2048]{1,0:T(8,128)(2,1)S(1)} %broadcast_select_fusion.1, bf16[2048,2304]{0,1:T(8,128)(2,1)} %all-gather.3.cloned.1.call-done, s32[]{:T(128)S(6)} %select_n.359), kind=kOutput, calls=%fused_computation.30 | convolution fusion | flops 604127232 | bytes 3702788 | tf_op jit(solution)/shard_map/dot_general | solution.py:49
  126.5 0.3 collective-permute-start.6
  126.8 3.2 %fusion.50 = bf16[256,576]{0,1:T(8,128)(2,1)} fusion(bf16[256,2048]{1,0:T(8,128)(2,1)S(1)} %broadcast_select_fusion.1, bf16[2048,2304]{0,1:T(8,128)(2,1)} %all-gather.3.cloned.1.call-done, s32[]{:T(128)S(6)} %select_n.361), kind=kOutput, calls=%fused_computation.31 | convolution fusion | flops 604127232 | bytes 3702788 | tf_op jit(solution)/shard_map/dot_general | solution.py:49
  130.0 2.4 collective-permute-start.7
  132.4 4.6 %collective-permute-done.6 = bf16[256,576]{0,1:T(8,128)(2,1)} collective-permute-done((bf16[256,576]{0,1:T(8,128)(2,1)}, bf16[256,576]{0,1:T(8,128)(2,1)}, u32[]{:S(2)}, u32[]{:S(2)}) %collective-permute-start.6) | collective-permute-done | bytes 294944 | tf_op jit(solution)/shard_map/ppermute | solution.py:13
  137.0 0.2 collective-permute-done.7
  137.1 3.8 %fusion.77 = (bf16[256,576]{0,1:T(8,128)(2,1)S(1)}, f32[256,576]{0,1:T(8,128)}) fusion(bf16[256,576]{0,1:T(8,128)(2,1)} %param.15, bf16[256,576]{0,1:T(8,128)(2,1)S(1)} %copy-done.1, bf16[1,256,576]{1,2,0:T(8,128)(2,1)} %param.14, pred[]{:T(512)S(6)} %eq.123, bf16[256,576]{0,1:T(8,128)(2,1)} %collective-permute-done.7, ...), kind=kOutput, calls=%fused_computation.51 | convolution fusion | flops 606486528 | bytes 6062085 | tf_op jit(solution)/shard_map/dot_general | solution.py:49
  140.9 2.8 %collective-permute-start.8 = (bf16[256,576]{0,1:T(8,128)(2,1)S(1)}, bf16[256,576]{0,1:T(8,128)(2,1)S(1)}, u32[]{:S(2)}, u32[]{:S(2)}) collective-permute-start(bf16[256,576]{0,1:T(8,128)(2,1)S(1)} %get-tuple-element.58), channel_id=1, source_target_pairs={{0,128},{128,0},{1,129},{129,1},{2,130},{130,2},{3,131},{131,3},{4... | collective-permute-start | bytes 884744 | tf_op jit(solution)/shard_map/ppermute | solution.py:101
  143.7 1.2 collective-permute-done.8
  144.9 3.8 %collective-permute-start.10 = (bf16[256,576]{0,1:T(8,128)(2,1)S(1)}, bf16[256,576]{0,1:T(8,128)(2,1)S(1)}, u32[]{:S(2)}, u32[]{:S(2)}) collective-permute-start(bf16[256,576]{0,1:T(8,128)(2,1)S(1)} %collective-permute-done.8), channel_id=1, source_target_pairs={{128,192},{160,224},{192,128},{224,160},{129,193},{161,225},{193,1... | collective-permute-start | bytes 884744 | tf_op jit(solution)/shard_map/ppermute | solution.py:17
  148.7 4.0 %collective-permute-start.11 = (bf16[256,576]{0,1:T(8,128)(2,1)S(1)}, bf16[256,576]{0,1:T(8,128)(2,1)S(1)}, u32[]{:S(2)}, u32[]{:S(2)}) collective-permute-start(bf16[256,576]{0,1:T(8,128)(2,1)S(1)} %collective-permute-done.8), channel_id=1, source_target_pairs={{128,160},{160,192},{192,224},{224,128},{129,161},{161,193},{193,2... | collective-permute-start | bytes 884744 | tf_op jit(solution)/shard_map/ppermute | solution.py:17
  152.7 2.5 collective-permute-start.9
  155.2 2.2 collective-permute-done.11
  157.4 3.0 %collective-permute-done.9 = bf16[256,576]{0,1:T(8,128)(2,1)S(1)} collective-permute-done((bf16[256,576]{0,1:T(8,128)(2,1)S(1)}, bf16[256,576]{0,1:T(8,128)(2,1)S(1)}, u32[]{:S(2)}, u32[]{:S(2)}) %collective-permute-start.9) | collective-permute-done | bytes 294944 | tf_op jit(solution)/shard_map/ppermute | solution.py:17
  160.7 6.5 %conditional.3 = (bf16[256,2048]{1,0:T(8,128)(2,1)S(1)}) conditional(s32[]{:T(128)} %convert_element_type.88, (bf16[1,2304,2048]{2,1,0:T(8,128)(2,1)}, bf16[256,2304]{0,1:T(8,128)(2,1)S(1)}, f32[1,2048]{1,0:T(1,128)S(1)}, f32[256,2048]{1,0:T(8,128)S(1)}) %tuple.47, () %tuple.23), branch_computations={%region_3.4_spmd, %region_4.5_spmd} | conditional | flops 2418016256 | bytes 13770760 | solution.py:106
  160.9 6.3 %fusion.25 = bf16[256,2048]{1,0:T(8,128)(2,1)S(1)} fusion(f32[256,2048]{1,0:T(8,128)S(1)} %get-tuple-element.29, bf16[256,2304]{0,1:T(8,128)(2,1)S(1)} %get-tuple-element.45, bf16[1,2304,2048]{2,1,0:T(8,128)(2,1)} %get-tuple-element.27, f32[2048]{0:T(1024)S(1)} %bitcast.57), kind=kOutput, calls=%fused_computation.11 | convolution fusion | flops 2418016256 | bytes 13770752 | tf_op jit(solution)/shard_map/cond/branch_0_fun/dot_general | solution.py:68
  167.2 1.4 collective-permute-start.12
  168.6 2.2 collective-permute-done.12
  170.9 50.0 %all-gather.5.cloned.1.call-done = bf16[2048,2304]{0,1:T(8,128)(2,1)} async-done(((bf16[2048,72]{0,1:T(8,128)(2,1)}), bf16[2048,2304]{0,1:T(8,128)(2,1)}) %all-gather.5.cloned.1.call-update) | async-done | bytes 9437200 | tf_op jit(solution)/shard_map/all_gather | solution.py:85
  220.9 2.5 fusion.59
  223.4 2.8 %collective-permute-start.13 = (bf16[256,576]{0,1:T(8,128)(2,1)S(1)}, bf16[256,576]{0,1:T(8,128)(2,1)S(1)}, u32[]{:S(2)}, u32[]{:S(2)}) collective-permute-start(bf16[256,576]{0,1:T(8,128)(2,1)S(1)} %fusion.59), channel_id=1, source_target_pairs={{0,64},{32,96},{64,0},{96,32},{1,65},{33,97},{65,1},{97,33},{2,66}... | collective-permute-start | bytes 884744 | tf_op jit(solution)/shard_map/ppermute | solution.py:13
  226.1 2.5 fusion.62
  228.6 0.4 collective-permute-start.14
  229.0 2.5 fusion.65
  231.5 2.5 collective-permute-start.15
  233.9 5.5 %collective-permute-done.14 = bf16[256,576]{0,1:T(8,128)(2,1)S(1)} collective-permute-done((bf16[256,576]{0,1:T(8,128)(2,1)S(1)}, bf16[256,576]{0,1:T(8,128)(2,1)S(1)}, u32[]{:S(2)}, u32[]{:S(2)}) %collective-permute-start.14) | collective-permute-done | bytes 294944 | tf_op jit(solution)/shard_map/ppermute | solution.py:13
  239.5 3.5 %fusion.78 = (bf16[256,576]{0,1:T(8,128)(2,1)S(1)}, bf16[1,256,576]{1,2,0:T(8,128)(2,1)}) fusion(bf16[256,576]{0,1:T(8,128)(2,1)S(1)} %collective-permute-done.15, bf16[256,576]{0,1:T(8,128)(2,1)S(1)} %collective-permute-done.14, bf16[256,576]{0,1:T(8,128)(2,1)S(1)} %collective-permute-done.13, bf16[256,576]{0,1:T(8,128)(2,1)S(1)} %copy-done.3, ...), kind=kOutput, calls=%fused_computation.63 | convolution fusion | flops 607223808 | bytes 6651909 | tf_op jit(solution)/shard_map/dot_general | solution.py:49
  243.0 1.3 collective-permute-start.16
  244.3 2.7 %collective-permute-done.16 = bf16[256,576]{0,1:T(8,128)(2,1)S(1)} collective-permute-done((bf16[256,576]{0,1:T(8,128)(2,1)S(1)}, bf16[256,576]{0,1:T(8,128)(2,1)S(1)}, u32[]{:S(2)}, u32[]{:S(2)}) %collective-permute-start.16) | collective-permute-done | bytes 294944 | tf_op jit(solution)/shard_map/ppermute | solution.py:115
  247.0 0.8 select_bitcast_fusion
  (31 shorter events, 1.1 us)
Async XLA Ops:
  7.2 110.3 %all-gather.3.cloned.1.call-start = ((), (), s32[]{:S(2)}) async-start(), calls=%async_computation | async-start | bytes 9732096 | tf_op jit(solution)/shard_map/all_gather | solution.py:84
  7.2 4.7 %collective-permute-start.4 = (bf16[2048,72]{0,1:T(8,128)(2,1)}, bf16[2048,72]{0,1:T(8,128)(2,1)S(1)}, u32[]{:S(2)}, u32[]{:S(2)}) collective-permute-start(bf16[2048,72]{0,1:T(8,128)(2,1)} %bitcast.59), channel_id=1, source_target_pairs={{0,128},{128,0},{1,129},{129,1},{2,130},{130,2},{3,131},{131,3},{4... | collective-permute-start | bytes 884744 | tf_op jit(solution)/shard_map/ppermute | solution.py:81
  13.8 207.1 %all-gather.5.cloned.1.call-start = ((), (), s32[]{:S(2)}) async-start(), calls=%async_computation.1 | async-start | bytes 9732096 | tf_op jit(solution)/shard_map/all_gather | solution.py:85
  14.5 5.3 %collective-permute-start = (bf16[256,576]{0,1:T(8,128)(2,1)}, bf16[256,576]{0,1:T(8,128)(2,1)S(1)}, u32[]{:S(2)}, u32[]{:S(2)}) collective-permute-start(bf16[256,576]{0,1:T(8,128)(2,1)} %param.13), channel_id=1, source_target_pairs={{0,96},{32,0},{64,32},{96,64},{1,97},{33,1},{65,33},{97,65},{2,98}... | collective-permute-start | bytes 884744 | tf_op jit(solution)/shard_map/ppermute | solution.py:17
  15.2 4.6 %collective-permute-start.1 = (bf16[256,576]{0,1:T(8,128)(2,1)}, bf16[256,576]{0,1:T(8,128)(2,1)S(1)}, u32[]{:S(2)}, u32[]{:S(2)}) collective-permute-start(bf16[256,576]{0,1:T(8,128)(2,1)} %param.13), channel_id=1, source_target_pairs={{0,64},{32,96},{64,0},{96,32},{1,65},{33,97},{65,1},{97,33},{2,66}... | collective-permute-start | bytes 884744 | tf_op jit(solution)/shard_map/ppermute | solution.py:17
  15.9 3.9 %collective-permute-start.2 = (bf16[256,576]{0,1:T(8,128)(2,1)}, bf16[256,576]{0,1:T(8,128)(2,1)S(1)}, u32[]{:S(2)}, u32[]{:S(2)}) collective-permute-start(bf16[256,576]{0,1:T(8,128)(2,1)} %param.13), channel_id=1, source_target_pairs={{0,32},{32,64},{64,96},{96,0},{1,33},{33,65},{65,97},{97,1},{2,34}... | collective-permute-start | bytes 884744 | tf_op jit(solution)/shard_map/ppermute | solution.py:17
  18.9 1.0 copy-start.1
  19.9 0.7 copy-start.4
  20.7 1.4 copy-start
  20.8 21.3 %collective-permute-start.3 = (bf16[256,2048]{1,0:T(8,128)(2,1)S(1)}, bf16[256,2048]{1,0:T(8,128)(2,1)}, u32[]{:S(2)}, u32[]{:S(2)}) collective-permute-start(bf16[256,2048]{1,0:T(8,128)(2,1)S(1)} %get-tuple-element.60), channel_id=1, source_target_pairs={{0,128},{1,129},{2,130},{3,131},{4,132},{5,133},{6,134},{7,135},{8... | collective-permute-start | bytes 3145736 | tf_op jit(solution)/shard_map/ppermute | solution.py:96
  120.6 11.8 %collective-permute-start.5 = (bf16[256,576]{0,1:T(8,128)(2,1)}, bf16[256,576]{0,1:T(8,128)(2,1)}, u32[]{:S(2)}, u32[]{:S(2)}) collective-permute-start(bf16[256,576]{0,1:T(8,128)(2,1)} %fusion.44), channel_id=1, source_target_pairs={{0,64},{32,96},{64,0},{96,32},{1,65},{33,97},{65,1},{97,33},{2,66}... | collective-permute-start | bytes 884744 | tf_op jit(solution)/shard_map/ppermute | solution.py:13
  126.5 10.4 %collective-permute-start.6 = (bf16[256,576]{0,1:T(8,128)(2,1)}, bf16[256,576]{0,1:T(8,128)(2,1)}, u32[]{:S(2)}, u32[]{:S(2)}) collective-permute-start(bf16[256,576]{0,1:T(8,128)(2,1)} %fusion.47), channel_id=1, source_target_pairs={{0,32},{32,64},{64,96},{96,0},{1,33},{33,65},{65,97},{97,1},{2,34}... | collective-permute-start | bytes 884744 | tf_op jit(solution)/shard_map/ppermute | solution.py:13
  130.0 7.1 %collective-permute-start.7 = (bf16[256,576]{0,1:T(8,128)(2,1)}, bf16[256,576]{0,1:T(8,128)(2,1)}, u32[]{:S(2)}, u32[]{:S(2)}) collective-permute-start(bf16[256,576]{0,1:T(8,128)(2,1)} %fusion.50), channel_id=1, source_target_pairs={{0,96},{32,0},{64,32},{96,64},{1,97},{33,1},{65,33},{97,65},{2,98}... | collective-permute-start | bytes 884744 | tf_op jit(solution)/shard_map/ppermute | solution.py:13
  140.9 4.0 %collective-permute-start.8 = (bf16[256,576]{0,1:T(8,128)(2,1)S(1)}, bf16[256,576]{0,1:T(8,128)(2,1)S(1)}, u32[]{:S(2)}, u32[]{:S(2)}) collective-permute-start(bf16[256,576]{0,1:T(8,128)(2,1)S(1)} %get-tuple-element.58), channel_id=1, source_target_pairs={{0,128},{128,0},{1,129},{129,1},{2,130},{130,2},{3,131},{131,3},{4... | collective-permute-start | bytes 884744 | tf_op jit(solution)/shard_map/ppermute | solution.py:101
  144.9 10.3 %collective-permute-start.10 = (bf16[256,576]{0,1:T(8,128)(2,1)S(1)}, bf16[256,576]{0,1:T(8,128)(2,1)S(1)}, u32[]{:S(2)}, u32[]{:S(2)}) collective-permute-start(bf16[256,576]{0,1:T(8,128)(2,1)S(1)} %collective-permute-done.8), channel_id=1, source_target_pairs={{128,192},{160,224},{192,128},{224,160},{129,193},{161,225},{193,1... | collective-permute-start | bytes 884744 | tf_op jit(solution)/shard_map/ppermute | solution.py:17
  148.7 8.7 %collective-permute-start.11 = (bf16[256,576]{0,1:T(8,128)(2,1)S(1)}, bf16[256,576]{0,1:T(8,128)(2,1)S(1)}, u32[]{:S(2)}, u32[]{:S(2)}) collective-permute-start(bf16[256,576]{0,1:T(8,128)(2,1)S(1)} %collective-permute-done.8), channel_id=1, source_target_pairs={{128,160},{160,192},{192,224},{224,128},{129,161},{161,193},{193,2... | collective-permute-start | bytes 884744 | tf_op jit(solution)/shard_map/ppermute | solution.py:17
  152.7 7.7 %collective-permute-start.9 = (bf16[256,576]{0,1:T(8,128)(2,1)S(1)}, bf16[256,576]{0,1:T(8,128)(2,1)S(1)}, u32[]{:S(2)}, u32[]{:S(2)}) collective-permute-start(bf16[256,576]{0,1:T(8,128)(2,1)S(1)} %collective-permute-done.8), channel_id=1, source_target_pairs={{128,224},{160,128},{192,160},{224,192},{129,225},{161,129},{193,1... | collective-permute-start | bytes 884744 | tf_op jit(solution)/shard_map/ppermute | solution.py:17
  167.2 3.6 %collective-permute-start.12 = (bf16[256,2048]{1,0:T(8,128)(2,1)S(1)}, bf16[256,2048]{1,0:T(8,128)(2,1)S(1)}, u32[]{:S(2)}, u32[]{:S(2)}) collective-permute-start(bf16[256,2048]{1,0:T(8,128)(2,1)S(1)} %get-tuple-element.61), channel_id=1, source_target_pairs={{128,0},{129,1},{130,2},{131,3},{132,4},{133,5},{134,6},{135,7},{1... | collective-permute-start | bytes 3145736 | tf_op jit(solution)/shard_map/ppermute | solution.py:112
  223.4 10.6 %collective-permute-start.13 = (bf16[256,576]{0,1:T(8,128)(2,1)S(1)}, bf16[256,576]{0,1:T(8,128)(2,1)S(1)}, u32[]{:S(2)}, u32[]{:S(2)}) collective-permute-start(bf16[256,576]{0,1:T(8,128)(2,1)S(1)} %fusion.59), channel_id=1, source_target_pairs={{0,64},{32,96},{64,0},{96,32},{1,65},{33,97},{65,1},{97,33},{2,66}... | collective-permute-start | bytes 884744 | tf_op jit(solution)/shard_map/ppermute | solution.py:13
  228.6 10.9 %copy-start.2 = (f32[256,576]{0,1:T(8,128)S(1)}, f32[256,576]{0,1:T(8,128)}, u32[]{:S(2)}) copy-start(f32[256,576]{0,1:T(8,128)} %get-tuple-element.59) | copy-start | bytes 1769476
  228.6 10.9 %copy-start.3 = (bf16[256,576]{0,1:T(8,128)(2,1)S(1)}, bf16[256,576]{0,1:T(8,128)(2,1)}, u32[]{:S(2)}) copy-start(bf16[256,576]{0,1:T(8,128)(2,1)} %param.15) | copy-start | bytes 884740
  228.6 10.8 %collective-permute-start.14 = (bf16[256,576]{0,1:T(8,128)(2,1)S(1)}, bf16[256,576]{0,1:T(8,128)(2,1)S(1)}, u32[]{:S(2)}, u32[]{:S(2)}) collective-permute-start(bf16[256,576]{0,1:T(8,128)(2,1)S(1)} %fusion.62), channel_id=1, source_target_pairs={{0,32},{32,64},{64,96},{96,0},{1,33},{33,65},{65,97},{97,1},{2,34}... | collective-permute-start | bytes 884744 | tf_op jit(solution)/shard_map/ppermute | solution.py:13
  231.5 8.0 %collective-permute-start.15 = (bf16[256,576]{0,1:T(8,128)(2,1)S(1)}, bf16[256,576]{0,1:T(8,128)(2,1)S(1)}, u32[]{:S(2)}, u32[]{:S(2)}) collective-permute-start(bf16[256,576]{0,1:T(8,128)(2,1)S(1)} %fusion.65), channel_id=1, source_target_pairs={{0,96},{32,0},{64,32},{96,64},{1,97},{33,1},{65,33},{97,65},{2,98}... | collective-permute-start | bytes 884744 | tf_op jit(solution)/shard_map/ppermute | solution.py:13
  243.0 4.0 %collective-permute-start.16 = (bf16[256,576]{0,1:T(8,128)(2,1)S(1)}, bf16[256,576]{0,1:T(8,128)(2,1)S(1)}, u32[]{:S(2)}, u32[]{:S(2)}) collective-permute-start(bf16[256,576]{0,1:T(8,128)(2,1)S(1)} %get-tuple-element.48), channel_id=1, source_target_pairs={{0,128},{1,129},{2,130},{3,131},{4,132},{5,133},{6,134},{7,135},{8... | collective-permute-start | bytes 884744 | tf_op jit(solution)/shard_map/ppermute | solution.py:115
Sparse Core Ops, SparseCore 0:
  13.9 103.4 all-gather.2
  120.6 100.2 all-gather.4

commit v7 on v6

--- a/solution.py
+++ b/solution.py
@@ -41,17 +41,11 @@
 
 
 def decode_scatter(features, decoder, feat_index, n_feat):
-    cols = decoder.shape[1] // n_feat
-    total = None
-    for k in sorted(range(n_feat), key=lambda shift: (-min(shift, n_feat - shift), shift)):
-        target = (feat_index + k) % n_feat
-        chunk = lax.dynamic_slice_in_dim(decoder, target * cols, cols, 1)
-        piece = jnp.dot(features, chunk, preferred_element_type=jnp.float32).astype(jnp.bfloat16)
-        if k:
-            piece = within_layer(piece, None, k, n_feat)
-        piece = piece.astype(jnp.float32)
-        total = piece if total is None else total + piece
-    return total
+    part = jnp.dot(features, decoder, preferred_element_type=jnp.float32).astype(jnp.bfloat16)
+    rows, columns = part.shape
+    chunks = part.reshape(rows, n_feat, columns // n_feat).transpose(1, 0, 2)
+    received = lax.all_to_all(chunks, "feat", 0, 0, tiled=True)
+    return jnp.sum(received.astype(jnp.float32), axis=0)
 
 
 def feature_mask(block_list, block_count, feat_index, blocks_dev):

time: 255 us -> 261 us (1.024)
  blocking collectives: 0 us -> 37 us
  matrix products: 30.6 us -> 17.7 us
  starting transfers between devices: 33.4 us -> 20.5 us
  waiting for transfers between devices: 168 us -> 159 us
  local copies, waits for them, and re-layouts: 2.13 us -> 5.31 us
    all_to_all x0 -> x2, blocking collectives: none -> 37 us  [decode_scatter(): received = lax.all_to_all(chunks, 'feat', 0, 0, tiled=True)]
    ppermute x6 -> x0, starting transfers between devices: 11 us -> none  [within_layer(): lax.ppermute(shard, 'feat', [(i, (i + shift) % n_feat) for i in range(n_f...]
    ppermute x6 -> x0, waiting for transfers between devices: 10.3 us -> none  [within_layer(): lax.ppermute(shard, 'feat', [(i, (i + shift) % n_feat) for i in range(n_f...]
    dot_general x8 -> x2, matrix products: 24.3 us -> 14.1 us  [decode_scatter(): jnp.dot(features, decoder, preferred_element_type=jnp.float32)]
    dot_general x1, matrix products: 6.31 us -> 3.63 us  [encode(): jnp.dot(gathered, enc_weight[0], preferred_element_type=jnp.float32)]
  transfers between devices with their start and end apart: 19 -> 13, of which waited for: 12 -> 8; matrix products, arithmetic and copies ran while one was open for 12% -> 7% of each run, Pallas kernels for 0% -> 0%
where the time goes in v7:
time: 261 us; the launch traced here: 260 us
  waiting for transfers between devices  159 us (61%)
  blocking collectives  37 us (14%)
  starting transfers between devices  20.5 us (8%)
  matrix products  17.7 us (7%)
  between operations  14.5 us (6%)
  other arithmetic  6.04 us (2%)
  local copies, waits for them, and re-layouts  5.31 us (2%)
    all_gather x1, waiting for transfers between devices, shards(): first_full = lax.all_gather(first_dec, 'tok', axis=1, tiled=True)  74.3 us
    all_gather x1, waiting for transfers between devices, shards(): second_full = lax.all_gather(second_dec, 'tok', axis=1, tiled=True)  51 us
    all_to_all x2, blocking collectives, decode_scatter(): received = lax.all_to_all(chunks, 'feat', 0, 0, tiled=True)  37 us
    ppermute x1, waiting for transfers between devices, shards(): lax.ppermute(features, 'layer', [(0, 1)])  20.1 us
    dot_general x2, matrix products, decode_scatter(): jnp.dot(features, decoder, preferred_element_type=jnp.float32)  14.1 us
    ppermute x6, starting transfers between devices, within_layer(): return lax.ppermute(shard, GROUP, pairs)  9.84 us
    ppermute x6, waiting for transfers between devices, within_layer(): return lax.ppermute(shard, GROUP, pairs)  7.1 us
  transfers between devices with their start and end apart: 13, of which 8 were waited for; matrix products, arithmetic and copies ran while one was open for 7% of the time, Pallas kernels for 0%

profile of v7, /device:TPU:1, one launch (start us, length us, event | category | flops | bytes accessed | tf_op | source)
XLA Modules:
  0.0 260.5 jit_solution(7296288444000258826)
XLA Ops:
  7.2 3.3 %collective-permute-start.4 = (bf16[2048,72]{0,1:T(8,128)(2,1)}, bf16[2048,72]{0,1:T(8,128)(2,1)S(1)}, u32[]{:S(2)}, u32[]{:S(2)}) collective-permute-start(bf16[2048,72]{0,1:T(8,128)(2,1)} %bitcast.61), channel_id=1, source_target_pairs={{0,128},{128,0},{1,129},{129,1},{2,130},{130,2},{3,131},{131,3},{4... | collective-permute-start | bytes 884744 | tf_op jit(solution)/shard_map/ppermute | solution.py:75
  10.5 1.4 collective-permute-done.4
  11.9 1.8 bitcast_select_fusion.1
  13.8 0.0 all-gather.5.cloned.1.call-start
  13.8 0.7 all-gather.5.cloned.1.call-update
  14.5 0.7 collective-permute-start
  15.2 0.7 collective-permute-start.1
  15.9 0.7 collective-permute-start.2
  16.7 0.7 iota_compare_fusion
  17.4 0.9 and_reduce_fusion
  18.3 0.6 broadcast_in_dim.16
  18.9 0.9 copy.25
  19.9 0.1 select_select_fusion.6
  20.0 0.1 select_select_fusion.7
  20.1 0.1 pad_maximum_fusion
  20.2 0.4 copy-done.10
  20.6 1.1 conditional.2
  20.7 1.1 broadcast.22
  21.7 1.3 collective-permute-start.3
  23.0 20.1 %collective-permute-done.3 = bf16[256,2048]{1,0:T(8,128)(2,1)S(1)} collective-permute-done((bf16[256,2048]{1,0:T(8,128)(2,1)}, bf16[256,2048]{1,0:T(8,128)(2,1)S(1)}, u32[]{:S(2)}, u32[]{:S(2)}) %collective-permute-start.3) | collective-permute-done | bytes 1048608 | tf_op jit(solution)/shard_map/ppermute | solution.py:90
  43.1 74.3 %all-gather.3.cloned.1.call-done = bf16[2048,2304]{0,1:T(8,128)(2,1)} async-done(((bf16[2048,72]{0,1:T(8,128)(2,1)}), bf16[2048,2304]{0,1:T(8,128)(2,1)}) %all-gather.3.cloned.1.call-update) | async-done | bytes 9437200 | tf_op jit(solution)/shard_map/all_gather | solution.py:78
  117.4 7.4 %convolution_convert_fusion.1 = bf16[256,2304]{1,0:T(8,128)(2,1)} fusion(bf16[2048,2304]{0,1:T(8,128)(2,1)} %all-gather.3.cloned.1.call-done, bf16[256,2048]{1,0:T(8,128)(2,1)} %get-tuple-element.66, bf16[256,2048]{1,0:T(8,128)(2,1)S(1)} %collective-permute-done.3, pred[]{:T(512)S(6)} %eq.115), kind=kOutput, calls=%fused_computation.13 | convolution fusion | flops 2417033216 | bytes 12713985 | tf_op jit(solution)/shard_map/dot_general | solution.py:44
  124.8 1.6 copy.18
  126.4 18.2 %all_to_all.10 = bf16[4,256,576]{1,2,0:T(8,128)(2,1)S(1)} all-to-all(bf16[4,256,576]{1,2,0:T(8,128)(2,1)S(1)} %bitcast.55), channel_id=1, replica_groups=mesh['layer'=2,'feat'=4,'tok'=32] {'feat'}, dimensions={0} | all-to-all | bytes 2359296 | tf_op jit(solution)/shard_map/all_to_all | solution.py:47
  144.6 0.2 convert_reduce_fusion.1
  144.8 0.1 fusion.35
  145.0 3.3 %collective-permute-start.5 = (bf16[256,576]{0,1:T(8,128)(2,1)S(1)}, bf16[256,576]{0,1:T(8,128)(2,1)S(1)}, u32[]{:S(2)}, u32[]{:S(2)}) collective-permute-start(bf16[256,576]{0,1:T(8,128)(2,1)S(1)} %fusion.35), channel_id=1, source_target_pairs={{0,128},{128,0},{1,129},{129,1},{2,130},{130,2},{3,131},{131,3},{4... | collective-permute-start | bytes 884744 | tf_op jit(solution)/shard_map/ppermute | solution.py:95
  148.2 1.2 collective-permute-done.5
  149.4 2.8 %collective-permute-start.6 = (bf16[256,576]{0,1:T(8,128)(2,1)S(1)}, bf16[256,576]{0,1:T(8,128)(2,1)S(1)}, u32[]{:S(2)}, u32[]{:S(2)}) collective-permute-start(bf16[256,576]{0,1:T(8,128)(2,1)S(1)} %collective-permute-done.5), channel_id=1, source_target_pairs={{128,224},{160,128},{192,160},{224,192},{129,225},{161,129},{193,1... | collective-permute-start | bytes 884744 | tf_op jit(solution)/shard_map/ppermute | solution.py:17
  152.2 3.1 %collective-permute-start.7 = (bf16[256,576]{0,1:T(8,128)(2,1)S(1)}, bf16[256,576]{0,1:T(8,128)(2,1)S(1)}, u32[]{:S(2)}, u32[]{:S(2)}) collective-permute-start(bf16[256,576]{0,1:T(8,128)(2,1)S(1)} %collective-permute-done.5), channel_id=1, source_target_pairs={{128,192},{160,224},{192,128},{224,160},{129,193},{161,225},{193,1... | collective-permute-start | bytes 884744 | tf_op jit(solution)/shard_map/ppermute | solution.py:17
  155.3 1.9 collective-permute-start.8
  157.3 4.0 %collective-permute-done.7 = bf16[256,576]{0,1:T(8,128)(2,1)S(1)} collective-permute-done((bf16[256,576]{0,1:T(8,128)(2,1)S(1)}, bf16[256,576]{0,1:T(8,128)(2,1)S(1)}, u32[]{:S(2)}, u32[]{:S(2)}) %collective-permute-start.7) | collective-permute-done | bytes 294944 | tf_op jit(solution)/shard_map/ppermute | solution.py:17
  161.2 3.1 %collective-permute-done.8 = bf16[256,576]{0,1:T(8,128)(2,1)S(1)} collective-permute-done((bf16[256,576]{0,1:T(8,128)(2,1)S(1)}, bf16[256,576]{0,1:T(8,128)(2,1)S(1)}, u32[]{:S(2)}, u32[]{:S(2)}) %collective-permute-start.8) | collective-permute-done | bytes 294944 | tf_op jit(solution)/shard_map/ppermute | solution.py:17
  164.4 0.1 select_select_fusion.2
  164.4 0.1 select_select_fusion.3
  164.6 0.1 pad_maximum_fusion.1
  164.7 3.6 %conditional.3 = (bf16[256,2048]{1,0:T(8,128)(2,1)}) conditional(s32[]{:T(128)} %convert_element_type.52, (bf16[1,2304,2048]{2,1,0:T(8,128)(2,1)S(1)}, bf16[256,2304]{0,1:T(8,128)(2,1)S(1)}, f32[1,2048]{1,0:T(1,128)S(1)}, f32[256,2048]{1,0:T(8,128)S(1)}) %tuple.49, () %tuple.23), branch_computations={%region_4.5_spmd, %region_5.6_spmd} | conditional | flops 2418016256 | bytes 13770760 | solution.py:100
  164.7 3.6 %fusion.25 = bf16[256,2048]{1,0:T(8,128)(2,1)} fusion(f32[256,2048]{1,0:T(8,128)S(1)} %get-tuple-element.29, bf16[256,2304]{0,1:T(8,128)(2,1)S(1)} %get-tuple-element.53, bf16[1,2304,2048]{2,1,0:T(8,128)(2,1)S(1)} %get-tuple-element.27, f32[2048]{0:T(1024)S(1)} %bitcast.59), kind=kOutput, calls=%fused_computation.11 | convolution fusion | flops 2418016256 | bytes 13770752 | tf_op jit(solution)/shard_map/cond/branch_0_fun/dot_general | solution.py:62
  168.3 1.5 collective-permute-start.9
  169.8 51.0 %all-gather.5.cloned.1.call-done = bf16[2048,2304]{0,1:T(8,128)(2,1)} async-done(((bf16[2048,72]{0,1:T(8,128)(2,1)}), bf16[2048,2304]{0,1:T(8,128)(2,1)}) %all-gather.5.cloned.1.call-update) | async-done | bytes 9437200 | tf_op jit(solution)/shard_map/all_gather | solution.py:79
  220.8 6.7 %convolution_convert_fusion = bf16[256,2304]{1,0:T(8,128)(2,1)S(1)} fusion(bf16[2048,2304]{0,1:T(8,128)(2,1)} %all-gather.5.cloned.1.call-done, bf16[256,2048]{1,0:T(8,128)(2,1)S(1)} %collective-permute-done.9, bf16[256,2048]{1,0:T(8,128)(2,1)} %get-tuple-element.67, pred[]{:T(512)S(6)} %eq.115), kind=kOutput, calls=%fused_computation.12 | convolution fusion | flops 2417033216 | bytes 12713985 | tf_op jit(solution)/shard_map/dot_general | solution.py:44
  227.5 0.6 copy.20
  228.2 18.9 %all_to_all.11 = bf16[4,256,576]{1,2,0:T(8,128)(2,1)S(1)} all-to-all(bf16[4,256,576]{1,2,0:T(8,128)(2,1)S(1)} %bitcast.56), channel_id=1, replica_groups=mesh['layer'=2,'feat'=4,'tok'=32] {'feat'}, dimensions={0} | all-to-all | bytes 2359296 | tf_op jit(solution)/shard_map/all_to_all | solution.py:47
  247.0 0.2 convert_reduce_fusion
  247.2 0.8 fusion.36
  248.0 1.3 collective-permute-start.10
  249.3 3.5 %collective-permute-done.10 = bf16[256,576]{0,1:T(8,128)(2,1)S(1)} collective-permute-done((bf16[256,576]{0,1:T(8,128)(2,1)S(1)}, bf16[256,576]{0,1:T(8,128)(2,1)S(1)}, u32[]{:S(2)}, u32[]{:S(2)}) %collective-permute-start.10) | collective-permute-done | bytes 294944 | tf_op jit(solution)/shard_map/ppermute | solution.py:109
  252.9 0.7 select_bitcast_fusion
  (31 shorter events, 0.2 us)
Async XLA Ops:
  7.2 110.3 %all-gather.3.cloned.1.call-start = ((), (), s32[]{:S(2)}) async-start(), calls=%async_computation.2 | async-start | bytes 9732096 | tf_op jit(solution)/shard_map/all_gather | solution.py:78
  7.2 4.7 %collective-permute-start.4 = (bf16[2048,72]{0,1:T(8,128)(2,1)}, bf16[2048,72]{0,1:T(8,128)(2,1)S(1)}, u32[]{:S(2)}, u32[]{:S(2)}) collective-permute-start(bf16[2048,72]{0,1:T(8,128)(2,1)} %bitcast.61), channel_id=1, source_target_pairs={{0,128},{128,0},{1,129},{129,1},{2,130},{130,2},{3,131},{131,3},{4... | collective-permute-start | bytes 884744 | tf_op jit(solution)/shard_map/ppermute | solution.py:75
  13.8 207.0 %all-gather.5.cloned.1.call-start = ((), (), s32[]{:S(2)}) async-start(), calls=%async_computation.3 | async-start | bytes 9732096 | tf_op jit(solution)/shard_map/all_gather | solution.py:79
  14.5 5.3 %collective-permute-start = (bf16[256,576]{0,1:T(8,128)(2,1)}, bf16[256,576]{0,1:T(8,128)(2,1)S(1)}, u32[]{:S(2)}, u32[]{:S(2)}) collective-permute-start(bf16[256,576]{0,1:T(8,128)(2,1)} %param.13), channel_id=1, source_target_pairs={{0,96},{32,0},{64,32},{96,64},{1,97},{33,1},{65,33},{97,65},{2,98}... | collective-permute-start | bytes 884744 | tf_op jit(solution)/shard_map/ppermute | solution.py:17
  15.2 4.6 %collective-permute-start.1 = (bf16[256,576]{0,1:T(8,128)(2,1)}, bf16[256,576]{0,1:T(8,128)(2,1)S(1)}, u32[]{:S(2)}, u32[]{:S(2)}) collective-permute-start(bf16[256,576]{0,1:T(8,128)(2,1)} %param.13), channel_id=1, source_target_pairs={{0,64},{32,96},{64,0},{96,32},{1,65},{33,97},{65,1},{97,33},{2,66}... | collective-permute-start | bytes 884744 | tf_op jit(solution)/shard_map/ppermute | solution.py:17
  15.9 3.9 %collective-permute-start.2 = (bf16[256,576]{0,1:T(8,128)(2,1)}, bf16[256,576]{0,1:T(8,128)(2,1)S(1)}, u32[]{:S(2)}, u32[]{:S(2)}) collective-permute-start(bf16[256,576]{0,1:T(8,128)(2,1)} %param.13), channel_id=1, source_target_pairs={{0,32},{32,64},{64,96},{96,0},{1,33},{33,65},{65,97},{97,1},{2,34}... | collective-permute-start | bytes 884744 | tf_op jit(solution)/shard_map/ppermute | solution.py:17
  18.9 1.0 copy-start.5
  20.0 0.7 copy-start.10
  21.7 21.4 %collective-permute-start.3 = (bf16[256,2048]{1,0:T(8,128)(2,1)}, bf16[256,2048]{1,0:T(8,128)(2,1)S(1)}, u32[]{:S(2)}, u32[]{:S(2)}) collective-permute-start(bf16[256,2048]{1,0:T(8,128)(2,1)} %get-tuple-element.66), channel_id=1, source_target_pairs={{0,128},{1,129},{2,130},{3,131},{4,132},{5,133},{6,134},{7,135},{8... | collective-permute-start | bytes 3145736 | tf_op jit(solution)/shard_map/ppermute | solution.py:90
  126.4 18.4 %copy-start.6 = (bf16[256,576]{0,1:T(8,128)(2,1)S(1)}, bf16[256,576]{0,1:T(8,128)(2,1)}, u32[]{:S(2)}) copy-start(bf16[256,576]{0,1:T(8,128)(2,1)} %param.13) | copy-start | bytes 884740
  126.4 18.4 %copy-start.7 = (bf16[256,576]{0,1:T(8,128)(2,1)S(1)}, bf16[256,576]{0,1:T(8,128)(2,1)}, u32[]{:S(2)}) copy-start(bf16[256,576]{0,1:T(8,128)(2,1)} %param.15) | copy-start | bytes 884740
  126.4 18.4 %copy-start.9 = (bf16[1,256,576]{1,2,0:T(8,128)(2,1)S(1)}, bf16[1,256,576]{1,2,0:T(8,128)(2,1)}, u32[]{:S(2)}) copy-start(bf16[1,256,576]{1,2,0:T(8,128)(2,1)} %param.14) | copy-start | bytes 884740
  144.6 20.1 %copy-start = (bf16[1,2304,2048]{2,1,0:T(8,128)(2,1)S(1)}, bf16[1,2304,2048]{2,1,0:T(8,128)(2,1)}, u32[]{:S(2)}) copy-start(bf16[1,2304,2048]{2,1,0:T(8,128)(2,1)} %param.16) | copy-start | bytes 28311556
  144.8 19.8 %copy-start.1 = (f32[256,576]{0,1:T(8,128)}, f32[256,576]{0,1:T(8,128)S(1)}, u32[]{:S(2)}) copy-start(f32[256,576]{0,1:T(8,128)S(1)} %convert_reduce_fusion.1) | copy-start | bytes 1769476
  145.0 4.5 %collective-permute-start.5 = (bf16[256,576]{0,1:T(8,128)(2,1)S(1)}, bf16[256,576]{0,1:T(8,128)(2,1)S(1)}, u32[]{:S(2)}, u32[]{:S(2)}) collective-permute-start(bf16[256,576]{0,1:T(8,128)(2,1)S(1)} %fusion.35), channel_id=1, source_target_pairs={{0,128},{128,0},{1,129},{129,1},{2,130},{130,2},{3,131},{131,3},{4... | collective-permute-start | bytes 884744 | tf_op jit(solution)/shard_map/ppermute | solution.py:95
  149.4 15.1 %copy-start.3 = (bf16[256,576]{0,1:T(8,128)(2,1)}, bf16[256,576]{0,1:T(8,128)(2,1)S(1)}, u32[]{:S(2)}) copy-start(bf16[256,576]{0,1:T(8,128)(2,1)S(1)} %collective-permute-done.5) | copy-start | bytes 884740
  149.4 7.8 %collective-permute-start.6 = (bf16[256,576]{0,1:T(8,128)(2,1)S(1)}, bf16[256,576]{0,1:T(8,128)(2,1)S(1)}, u32[]{:S(2)}, u32[]{:S(2)}) collective-permute-start(bf16[256,576]{0,1:T(8,128)(2,1)S(1)} %collective-permute-done.5), channel_id=1, source_target_pairs={{128,224},{160,128},{192,160},{224,192},{129,225},{161,129},{193,1... | collective-permute-start | bytes 884744 | tf_op jit(solution)/shard_map/ppermute | solution.py:17
  152.2 9.0 %collective-permute-start.7 = (bf16[256,576]{0,1:T(8,128)(2,1)S(1)}, bf16[256,576]{0,1:T(8,128)(2,1)S(1)}, u32[]{:S(2)}, u32[]{:S(2)}) collective-permute-start(bf16[256,576]{0,1:T(8,128)(2,1)S(1)} %collective-permute-done.5), channel_id=1, source_target_pairs={{128,192},{160,224},{192,128},{224,160},{129,193},{161,225},{193,1... | collective-permute-start | bytes 884744 | tf_op jit(solution)/shard_map/ppermute | solution.py:17
  155.3 9.0 %collective-permute-start.8 = (bf16[256,576]{0,1:T(8,128)(2,1)S(1)}, bf16[256,576]{0,1:T(8,128)(2,1)S(1)}, u32[]{:S(2)}, u32[]{:S(2)}) collective-permute-start(bf16[256,576]{0,1:T(8,128)(2,1)S(1)} %collective-permute-done.5), channel_id=1, source_target_pairs={{128,160},{160,192},{192,224},{224,128},{129,161},{161,193},{193,2... | collective-permute-start | bytes 884744 | tf_op jit(solution)/shard_map/ppermute | solution.py:17
  168.3 52.5 %collective-permute-start.9 = (bf16[256,2048]{1,0:T(8,128)(2,1)}, bf16[256,2048]{1,0:T(8,128)(2,1)S(1)}, u32[]{:S(2)}, u32[]{:S(2)}) collective-permute-start(bf16[256,2048]{1,0:T(8,128)(2,1)} %get-tuple-element.67), channel_id=1, source_target_pairs={{128,0},{129,1},{130,2},{131,3},{132,4},{133,5},{134,6},{135,7},{1... | collective-permute-start | bytes 3145736 | tf_op jit(solution)/shard_map/ppermute | solution.py:106
  228.1 19.1 %copy-start.2 = (f32[256,576]{0,1:T(8,128)S(1)}, f32[256,576]{0,1:T(8,128)}, u32[]{:S(2)}) copy-start(f32[256,576]{0,1:T(8,128)} %copy-done.1) | copy-start | bytes 1769476
  228.1 19.1 %copy-start.8 = (bf16[256,576]{0,1:T(8,128)(2,1)S(1)}, bf16[256,576]{0,1:T(8,128)(2,1)}, u32[]{:S(2)}) copy-start(bf16[256,576]{0,1:T(8,128)(2,1)} %param.15) | copy-start | bytes 884740
  247.0 5.8 %copy-start.4 = (bf16[256,576]{0,1:T(8,128)(2,1)S(1)}, bf16[256,576]{0,1:T(8,128)(2,1)}, u32[]{:S(2)}) copy-start(bf16[256,576]{0,1:T(8,128)(2,1)} %copy-done.3) | copy-start | bytes 884740
  248.0 4.8 %collective-permute-start.10 = (bf16[256,576]{0,1:T(8,128)(2,1)S(1)}, bf16[256,576]{0,1:T(8,128)(2,1)S(1)}, u32[]{:S(2)}, u32[]{:S(2)}) collective-permute-start(bf16[256,576]{0,1:T(8,128)(2,1)S(1)} %get-tuple-element.62), channel_id=1, source_target_pairs={{0,128},{1,129},{2,130},{3,131},{4,132},{5,133},{6,134},{7,135},{8... | collective-permute-start | bytes 884744 | tf_op jit(solution)/shard_map/ppermute | solution.py:109
Sparse Core Ops, SparseCore 0:
  13.9 103.4 all-gather.2
  120.6 100.1 all-gather.4

commit v8 on v6

--- a/solution.py
+++ b/solution.py
@@ -49,6 +49,8 @@
         piece = jnp.dot(features, chunk, preferred_element_type=jnp.float32).astype(jnp.bfloat16)
         if k:
             piece = within_layer(piece, None, k, n_feat)
+        else:
+            piece = lax.optimization_barrier(piece)
         piece = piece.astype(jnp.float32)
         total = piece if total is None else total + piece
     return total

time: 255 us -> 254 us (level)
  waiting for transfers between devices: 168 us -> 163 us
  other arithmetic: 6.15 us -> 10.4 us
    ppermute x6, waiting for transfers between devices: 10.3 us -> 4.87 us  [within_layer(): lax.ppermute(shard, 'feat', [(i, (i + shift) % n_feat) for i in range(n_f...]
  transfers between devices with their start and end apart: 19 -> 19, of which waited for: 12 -> 12; matrix products, arithmetic and copies ran while one was open for 12% -> 13% of each run, Pallas kernels for 0% -> 0%
where the time goes in v8:
time: 254 us; the launch traced here: 253 us
  waiting for transfers between devices  163 us (64%)
  starting transfers between devices  33.5 us (13%)
  matrix products  29.2 us (11%)
  between operations  14.5 us (6%)
  other arithmetic  10.4 us (4%)
    all_gather x1, waiting for transfers between devices, shards(): first_full = lax.all_gather(first_dec, 'tok', axis=1, tiled=True)  73 us
    all_gather x1, waiting for transfers between devices, shards(): second_full = lax.all_gather(second_dec, 'tok', axis=1, tiled=True)  52.1 us
    dot_general x8, matrix products, decode_scatter(): jnp.dot(features, chunk, preferred_element_type=jnp.float32)  22.8 us
    ppermute x1, waiting for transfers between devices, shards(): lax.ppermute(features, 'layer', [(0, 1)])  20 us
    ppermute x6, starting transfers between devices, within_layer(): return lax.ppermute(shard, GROUP, pairs)  12.3 us
    ppermute x6, starting transfers between devices, within_layer(): lax.ppermute(shard, 'feat', [(i, (i + shift) % n_feat) for i in range(n_f...  11 us
    dot_general x1, matrix products, encode(): jnp.dot(gathered, enc_weight[0], preferred_element_type=jnp.float32)  6.31 us
  transfers between devices with their start and end apart: 19, of which 12 were waited for; matrix products, arithmetic and copies ran while one was open for 13% of the time, Pallas kernels for 0%

profile of v8, /device:TPU:1, one launch (start us, length us, event | category | flops | bytes accessed | tf_op | source)
XLA Modules:
  0.0 253.2 jit_solution(8539006567864455377)
XLA Ops:
  7.2 3.3 %collective-permute-start.4 = (bf16[2048,72]{0,1:T(8,128)(2,1)}, bf16[2048,72]{0,1:T(8,128)(2,1)S(1)}, u32[]{:S(2)}, u32[]{:S(2)}) collective-permute-start(bf16[2048,72]{0,1:T(8,128)(2,1)} %bitcast.59), channel_id=1, source_target_pairs={{0,128},{128,0},{1,129},{129,1},{2,130},{130,2},{3,131},{131,3},{4... | collective-permute-start | bytes 884744 | tf_op jit(solution)/shard_map/ppermute | solution.py:83
  10.5 1.4 collective-permute-done.4
  11.9 1.8 bitcast_select_fusion
  13.8 0.7 all-gather.5.cloned.1.call-update
  14.5 0.7 collective-permute-start
  15.2 0.7 collective-permute-start.1
  15.9 0.7 collective-permute-start.2
  16.7 0.7 iota_compare_fusion
  17.4 0.9 and_reduce_fusion
  18.3 0.6 broadcast_in_dim.16
  18.9 0.9 copy.19
  20.2 0.5 copy-done.11
  20.7 1.3 collective-permute-start.3
  22.1 20.0 %collective-permute-done.3 = bf16[256,2048]{1,0:T(8,128)(2,1)} collective-permute-done((bf16[256,2048]{1,0:T(8,128)(2,1)S(1)}, bf16[256,2048]{1,0:T(8,128)(2,1)}, u32[]{:S(2)}, u32[]{:S(2)}) %collective-permute-start.3) | collective-permute-done | bytes 1048608 | tf_op jit(solution)/shard_map/ppermute | solution.py:98
  42.1 2.3 broadcast_select_fusion.1
  44.4 73.0 %all-gather.3.cloned.1.call-done = bf16[2048,2304]{0,1:T(8,128)(2,1)} async-done(((bf16[2048,72]{0,1:T(8,128)(2,1)}), bf16[2048,2304]{0,1:T(8,128)(2,1)}) %all-gather.3.cloned.1.call-update) | async-done | bytes 9437200 | tf_op jit(solution)/shard_map/all_gather | solution.py:86
  117.4 3.6 %fusion.44 = bf16[256,576]{0,1:T(8,128)(2,1)} fusion(bf16[256,2048]{1,0:T(8,128)(2,1)} %broadcast_select_fusion.1, bf16[2048,2304]{0,1:T(8,128)(2,1)} %all-gather.3.cloned.1.call-done, s32[]{:T(128)S(6)} %select_n.357), kind=kOutput, calls=%fused_computation.29 | convolution fusion | flops 604127232 | bytes 3702788 | tf_op jit(solution)/shard_map/dot_general | solution.py:49
  121.0 2.7 %collective-permute-start.5 = (bf16[256,576]{0,1:T(8,128)(2,1)}, bf16[256,576]{0,1:T(8,128)(2,1)S(1)}, u32[]{:S(2)}, u32[]{:S(2)}) collective-permute-start(bf16[256,576]{0,1:T(8,128)(2,1)} %fusion.44), channel_id=1, source_target_pairs={{0,64},{32,96},{64,0},{96,32},{1,65},{33,97},{65,1},{97,33},{2,66}... | collective-permute-start | bytes 884744 | tf_op jit(solution)/shard_map/ppermute | solution.py:13
  123.7 3.3 %fusion.47 = bf16[256,576]{0,1:T(8,128)(2,1)} fusion(bf16[256,2048]{1,0:T(8,128)(2,1)S(1)} %copy-done.9, bf16[2048,2304]{0,1:T(8,128)(2,1)} %all-gather.3.cloned.1.call-done, s32[]{:T(128)S(6)} %select_n.359), kind=kOutput, calls=%fused_computation.30 | convolution fusion | flops 604127232 | bytes 3702788 | tf_op jit(solution)/shard_map/dot_general | solution.py:49
  127.3 3.3 %fusion.50 = bf16[256,576]{0,1:T(8,128)(2,1)} fusion(bf16[256,2048]{1,0:T(8,128)(2,1)S(1)} %copy-done.9, bf16[2048,2304]{0,1:T(8,128)(2,1)} %all-gather.3.cloned.1.call-done, s32[]{:T(128)S(6)} %select_n.361), kind=kOutput, calls=%fused_computation.31 | convolution fusion | flops 604127232 | bytes 3702788 | tf_op jit(solution)/shard_map/dot_general | solution.py:49
  130.5 2.4 collective-permute-start.7
  132.9 2.8 %fusion.53 = bf16[256,576]{0,1:T(8,128)(2,1)S(1)} fusion(bf16[256,2048]{1,0:T(8,128)(2,1)} %broadcast_select_fusion.1, bf16[2048,2304]{0,1:T(8,128)(2,1)} %all-gather.3.cloned.1.call-done, s32[]{:T(128)S(6)} %select_n.362), kind=kOutput, calls=%fused_computation.32 | convolution fusion | flops 604127232 | bytes 3702788 | tf_op jit(solution)/shard_map/dot_general | solution.py:49
  135.8 1.5 collective-permute-done.6
  137.7 1.3 fusion.71
  138.9 2.9 %collective-permute-start.8 = (bf16[256,576]{0,1:T(8,128)(2,1)S(1)}, bf16[256,576]{0,1:T(8,128)(2,1)S(1)}, u32[]{:S(2)}, u32[]{:S(2)}) collective-permute-start(bf16[256,576]{0,1:T(8,128)(2,1)S(1)} %fusion.71), channel_id=1, source_target_pairs={{0,128},{128,0},{1,129},{129,1},{2,130},{130,2},{3,131},{131,3},{4... | collective-permute-start | bytes 884744 | tf_op jit(solution)/shard_map/ppermute | solution.py:103
  141.8 1.2 collective-permute-done.8
  143.0 3.8 %collective-permute-start.10 = (bf16[256,576]{0,1:T(8,128)(2,1)S(1)}, bf16[256,576]{0,1:T(8,128)(2,1)S(1)}, u32[]{:S(2)}, u32[]{:S(2)}) collective-permute-start(bf16[256,576]{0,1:T(8,128)(2,1)S(1)} %collective-permute-done.8), channel_id=1, source_target_pairs={{128,192},{160,224},{192,128},{224,160},{129,193},{161,225},{193,1... | collective-permute-start | bytes 884744 | tf_op jit(solution)/shard_map/ppermute | solution.py:17
  146.9 4.0 %collective-permute-start.11 = (bf16[256,576]{0,1:T(8,128)(2,1)S(1)}, bf16[256,576]{0,1:T(8,128)(2,1)S(1)}, u32[]{:S(2)}, u32[]{:S(2)}) collective-permute-start(bf16[256,576]{0,1:T(8,128)(2,1)S(1)} %collective-permute-done.8), channel_id=1, source_target_pairs={{128,160},{160,192},{192,224},{224,128},{129,161},{161,193},{193,2... | collective-permute-start | bytes 884744 | tf_op jit(solution)/shard_map/ppermute | solution.py:17
  150.8 2.5 collective-permute-start.9
  153.4 2.6 %collective-permute-done.11 = bf16[256,576]{0,1:T(8,128)(2,1)S(1)} collective-permute-done((bf16[256,576]{0,1:T(8,128)(2,1)S(1)}, bf16[256,576]{0,1:T(8,128)(2,1)S(1)}, u32[]{:S(2)}, u32[]{:S(2)}) %collective-permute-start.11) | collective-permute-done | bytes 294944 | tf_op jit(solution)/shard_map/ppermute | solution.py:17
  155.9 2.4 collective-permute-done.9
  158.6 6.5 %conditional.3 = (bf16[256,2048]{1,0:T(8,128)(2,1)S(1)}) conditional(s32[]{:T(128)} %convert_element_type.88, (bf16[1,2304,2048]{2,1,0:T(8,128)(2,1)}, bf16[256,2304]{0,1:T(8,128)(2,1)S(1)}, f32[1,2048]{1,0:T(1,128)S(1)}, f32[256,2048]{1,0:T(8,128)S(1)}) %tuple.46, () %tuple.23), branch_computations={%region_3.4_spmd, %region_4.5_spmd} | conditional | flops 2418016256 | bytes 13770760 | solution.py:108
  158.8 6.3 %fusion.25 = bf16[256,2048]{1,0:T(8,128)(2,1)S(1)} fusion(f32[256,2048]{1,0:T(8,128)S(1)} %get-tuple-element.29, bf16[256,2304]{0,1:T(8,128)(2,1)S(1)} %get-tuple-element.45, bf16[1,2304,2048]{2,1,0:T(8,128)(2,1)} %get-tuple-element.27, f32[2048]{0:T(1024)S(1)} %bitcast.57), kind=kOutput, calls=%fused_computation.11 | convolution fusion | flops 2418016256 | bytes 13770752 | tf_op jit(solution)/shard_map/cond/branch_0_fun/dot_general | solution.py:70
  165.1 1.4 collective-permute-start.12
  166.5 2.2 collective-permute-done.12
  168.8 52.1 %all-gather.5.cloned.1.call-done = bf16[2048,2304]{0,1:T(8,128)(2,1)} async-done(((bf16[2048,72]{0,1:T(8,128)(2,1)}), bf16[2048,2304]{0,1:T(8,128)(2,1)}) %all-gather.5.cloned.1.call-update) | async-done | bytes 9437200 | tf_op jit(solution)/shard_map/all_gather | solution.py:87
  220.9 2.5 fusion.56
  223.4 2.8 %collective-permute-start.13 = (bf16[256,576]{0,1:T(8,128)(2,1)S(1)}, bf16[256,576]{0,1:T(8,128)(2,1)S(1)}, u32[]{:S(2)}, u32[]{:S(2)}) collective-permute-start(bf16[256,576]{0,1:T(8,128)(2,1)S(1)} %fusion.56), channel_id=1, source_target_pairs={{0,64},{32,96},{64,0},{96,32},{1,65},{33,97},{65,1},{97,33},{2,66}... | collective-permute-start | bytes 884744 | tf_op jit(solution)/shard_map/ppermute | solution.py:13
  226.1 2.5 fusion.59
  228.6 0.4 collective-permute-start.14
  229.0 2.5 fusion.62
  231.5 2.5 collective-permute-start.15
  234.0 2.5 fusion.65
  236.5 3.0 %collective-permute-done.14 = bf16[256,576]{0,1:T(8,128)(2,1)S(1)} collective-permute-done((bf16[256,576]{0,1:T(8,128)(2,1)S(1)}, bf16[256,576]{0,1:T(8,128)(2,1)S(1)}, u32[]{:S(2)}, u32[]{:S(2)}) %collective-permute-start.14) | collective-permute-done | bytes 294944 | tf_op jit(solution)/shard_map/ppermute | solution.py:13
  239.5 2.1 fusion.72
  241.6 1.3 collective-permute-start.16
  242.9 2.8 %collective-permute-done.16 = bf16[256,576]{0,1:T(8,128)(2,1)S(1)} collective-permute-done((bf16[256,576]{0,1:T(8,128)(2,1)S(1)}, bf16[256,576]{0,1:T(8,128)(2,1)S(1)}, u32[]{:S(2)}, u32[]{:S(2)}) %collective-permute-start.16) | collective-permute-done | bytes 294944 | tf_op jit(solution)/shard_map/ppermute | solution.py:117
  245.6 0.8 select_bitcast_fusion
  (47 shorter events, 1.7 us)
Async XLA Ops:
  7.2 110.3 %all-gather.3.cloned.1.call-start = ((), (), s32[]{:S(2)}) async-start(), calls=%async_computation | async-start | bytes 9732096 | tf_op jit(solution)/shard_map/all_gather | solution.py:86
  7.2 4.7 %collective-permute-start.4 = (bf16[2048,72]{0,1:T(8,128)(2,1)}, bf16[2048,72]{0,1:T(8,128)(2,1)S(1)}, u32[]{:S(2)}, u32[]{:S(2)}) collective-permute-start(bf16[2048,72]{0,1:T(8,128)(2,1)} %bitcast.59), channel_id=1, source_target_pairs={{0,128},{128,0},{1,129},{129,1},{2,130},{130,2},{3,131},{131,3},{4... | collective-permute-start | bytes 884744 | tf_op jit(solution)/shard_map/ppermute | solution.py:83
  13.8 207.1 %all-gather.5.cloned.1.call-start = ((), (), s32[]{:S(2)}) async-start(), calls=%async_computation.1 | async-start | bytes 9732096 | tf_op jit(solution)/shard_map/all_gather | solution.py:87
  14.5 5.3 %collective-permute-start = (bf16[256,576]{0,1:T(8,128)(2,1)}, bf16[256,576]{0,1:T(8,128)(2,1)S(1)}, u32[]{:S(2)}, u32[]{:S(2)}) collective-permute-start(bf16[256,576]{0,1:T(8,128)(2,1)} %param.13), channel_id=1, source_target_pairs={{0,96},{32,0},{64,32},{96,64},{1,97},{33,1},{65,33},{97,65},{2,98}... | collective-permute-start | bytes 884744 | tf_op jit(solution)/shard_map/ppermute | solution.py:17
  15.2 4.6 %collective-permute-start.1 = (bf16[256,576]{0,1:T(8,128)(2,1)}, bf16[256,576]{0,1:T(8,128)(2,1)S(1)}, u32[]{:S(2)}, u32[]{:S(2)}) collective-permute-start(bf16[256,576]{0,1:T(8,128)(2,1)} %param.13), channel_id=1, source_target_pairs={{0,64},{32,96},{64,0},{96,32},{1,65},{33,97},{65,1},{97,33},{2,66}... | collective-permute-start | bytes 884744 | tf_op jit(solution)/shard_map/ppermute | solution.py:17
  15.9 3.9 %collective-permute-start.2 = (bf16[256,576]{0,1:T(8,128)(2,1)}, bf16[256,576]{0,1:T(8,128)(2,1)S(1)}, u32[]{:S(2)}, u32[]{:S(2)}) collective-permute-start(bf16[256,576]{0,1:T(8,128)(2,1)} %param.13), channel_id=1, source_target_pairs={{0,32},{32,64},{64,96},{96,0},{1,33},{33,65},{65,97},{97,1},{2,34}... | collective-permute-start | bytes 884744 | tf_op jit(solution)/shard_map/ppermute | solution.py:17
  18.9 1.0 copy-start
  19.9 0.7 copy-start.11
  20.7 21.3 %collective-permute-start.3 = (bf16[256,2048]{1,0:T(8,128)(2,1)S(1)}, bf16[256,2048]{1,0:T(8,128)(2,1)}, u32[]{:S(2)}, u32[]{:S(2)}) collective-permute-start(bf16[256,2048]{1,0:T(8,128)(2,1)S(1)} %get-tuple-element.58), channel_id=1, source_target_pairs={{0,128},{1,129},{2,130},{3,131},{4,132},{5,133},{6,134},{7,135},{8... | collective-permute-start | bytes 3145736 | tf_op jit(solution)/shard_map/ppermute | solution.py:98
  117.4 6.3 %copy-start.9 = (bf16[256,2048]{1,0:T(8,128)(2,1)S(1)}, bf16[256,2048]{1,0:T(8,128)(2,1)}, u32[]{:S(2)}) copy-start(bf16[256,2048]{1,0:T(8,128)(2,1)} %broadcast_select_fusion.1) | copy-start | bytes 3145732
  121.0 14.8 %collective-permute-start.5 = (bf16[256,576]{0,1:T(8,128)(2,1)}, bf16[256,576]{0,1:T(8,128)(2,1)S(1)}, u32[]{:S(2)}, u32[]{:S(2)}) collective-permute-start(bf16[256,576]{0,1:T(8,128)(2,1)} %fusion.44), channel_id=1, source_target_pairs={{0,64},{32,96},{64,0},{96,32},{1,65},{33,97},{65,1},{97,33},{2,66}... | collective-permute-start | bytes 884744 | tf_op jit(solution)/shard_map/ppermute | solution.py:13
  127.0 10.3 %collective-permute-start.6 = (bf16[256,576]{0,1:T(8,128)(2,1)}, bf16[256,576]{0,1:T(8,128)(2,1)S(1)}, u32[]{:S(2)}, u32[]{:S(2)}) collective-permute-start(bf16[256,576]{0,1:T(8,128)(2,1)} %fusion.47), channel_id=1, source_target_pairs={{0,32},{32,64},{64,96},{96,0},{1,33},{33,65},{65,97},{97,1},{2,34}... | collective-permute-start | bytes 884744 | tf_op jit(solution)/shard_map/ppermute | solution.py:13
  130.5 7.1 %copy-start.1 = (bf16[256,576]{0,1:T(8,128)(2,1)S(1)}, bf16[256,576]{0,1:T(8,128)(2,1)}, u32[]{:S(2)}) copy-start(bf16[256,576]{0,1:T(8,128)(2,1)} %param.15) | copy-start | bytes 884740
  130.5 7.1 %collective-permute-start.7 = (bf16[256,576]{0,1:T(8,128)(2,1)}, bf16[256,576]{0,1:T(8,128)(2,1)}, u32[]{:S(2)}, u32[]{:S(2)}) collective-permute-start(bf16[256,576]{0,1:T(8,128)(2,1)} %fusion.50), channel_id=1, source_target_pairs={{0,96},{32,0},{64,32},{96,64},{1,97},{33,1},{65,33},{97,65},{2,98}... | collective-permute-start | bytes 884744 | tf_op jit(solution)/shard_map/ppermute | solution.py:13
  132.9 4.7 %copy-start.10 = (bf16[1,256,576]{1,2,0:T(8,128)(2,1)S(1)}, bf16[1,256,576]{1,2,0:T(8,128)(2,1)}, u32[]{:S(2)}) copy-start(bf16[1,256,576]{1,2,0:T(8,128)(2,1)} %param.14) | copy-start | bytes 884740
  135.8 22.7 %copy-start.7 = (bf16[256,576]{0,1:T(8,128)(2,1)}, bf16[256,576]{0,1:T(8,128)(2,1)S(1)}, u32[]{:S(2)}) copy-start(bf16[256,576]{0,1:T(8,128)(2,1)S(1)} %fusion.53) | copy-start | bytes 884740
  135.8 22.5 %copy-start.3 = (bf16[256,576]{0,1:T(8,128)(2,1)}, bf16[256,576]{0,1:T(8,128)(2,1)S(1)}, u32[]{:S(2)}) copy-start(bf16[256,576]{0,1:T(8,128)(2,1)S(1)} %collective-permute-done.5) | copy-start | bytes 884740
  137.3 21.0 %copy-start.5 = (bf16[256,576]{0,1:T(8,128)(2,1)}, bf16[256,576]{0,1:T(8,128)(2,1)S(1)}, u32[]{:S(2)}) copy-start(bf16[256,576]{0,1:T(8,128)(2,1)S(1)} %collective-permute-done.6) | copy-start | bytes 884740
  138.9 4.1 %collective-permute-start.8 = (bf16[256,576]{0,1:T(8,128)(2,1)S(1)}, bf16[256,576]{0,1:T(8,128)(2,1)S(1)}, u32[]{:S(2)}, u32[]{:S(2)}) collective-permute-start(bf16[256,576]{0,1:T(8,128)(2,1)S(1)} %fusion.71), channel_id=1, source_target_pairs={{0,128},{128,0},{1,129},{129,1},{2,130},{130,2},{3,131},{131,3},{4... | collective-permute-start | bytes 884744 | tf_op jit(solution)/shard_map/ppermute | solution.py:103
  143.0 10.3 %collective-permute-start.10 = (bf16[256,576]{0,1:T(8,128)(2,1)S(1)}, bf16[256,576]{0,1:T(8,128)(2,1)S(1)}, u32[]{:S(2)}, u32[]{:S(2)}) collective-permute-start(bf16[256,576]{0,1:T(8,128)(2,1)S(1)} %collective-permute-done.8), channel_id=1, source_target_pairs={{128,192},{160,224},{192,128},{224,160},{129,193},{161,225},{193,1... | collective-permute-start | bytes 884744 | tf_op jit(solution)/shard_map/ppermute | solution.py:17
  146.9 9.1 %collective-permute-start.11 = (bf16[256,576]{0,1:T(8,128)(2,1)S(1)}, bf16[256,576]{0,1:T(8,128)(2,1)S(1)}, u32[]{:S(2)}, u32[]{:S(2)}) collective-permute-start(bf16[256,576]{0,1:T(8,128)(2,1)S(1)} %collective-permute-done.8), channel_id=1, source_target_pairs={{128,160},{160,192},{192,224},{224,128},{129,161},{161,193},{193,2... | collective-permute-start | bytes 884744 | tf_op jit(solution)/shard_map/ppermute | solution.py:17
  150.8 7.5 %collective-permute-start.9 = (bf16[256,576]{0,1:T(8,128)(2,1)S(1)}, bf16[256,576]{0,1:T(8,128)(2,1)S(1)}, u32[]{:S(2)}, u32[]{:S(2)}) collective-permute-start(bf16[256,576]{0,1:T(8,128)(2,1)S(1)} %collective-permute-done.8), channel_id=1, source_target_pairs={{128,224},{160,128},{192,160},{224,192},{129,225},{161,129},{193,1... | collective-permute-start | bytes 884744 | tf_op jit(solution)/shard_map/ppermute | solution.py:17
  165.1 3.6 %collective-permute-start.12 = (bf16[256,2048]{1,0:T(8,128)(2,1)S(1)}, bf16[256,2048]{1,0:T(8,128)(2,1)S(1)}, u32[]{:S(2)}, u32[]{:S(2)}) collective-permute-start(bf16[256,2048]{1,0:T(8,128)(2,1)S(1)} %get-tuple-element.59), channel_id=1, source_target_pairs={{128,0},{129,1},{130,2},{131,3},{132,4},{133,5},{134,6},{135,7},{1... | collective-permute-start | bytes 3145736 | tf_op jit(solution)/shard_map/ppermute | solution.py:114
  223.4 13.1 %collective-permute-start.13 = (bf16[256,576]{0,1:T(8,128)(2,1)S(1)}, bf16[256,576]{0,1:T(8,128)(2,1)S(1)}, u32[]{:S(2)}, u32[]{:S(2)}) collective-permute-start(bf16[256,576]{0,1:T(8,128)(2,1)S(1)} %fusion.56), channel_id=1, source_target_pairs={{0,64},{32,96},{64,0},{96,32},{1,65},{33,97},{65,1},{97,33},{2,66}... | collective-permute-start | bytes 884744 | tf_op jit(solution)/shard_map/ppermute | solution.py:13
  228.6 10.9 %collective-permute-start.14 = (bf16[256,576]{0,1:T(8,128)(2,1)S(1)}, bf16[256,576]{0,1:T(8,128)(2,1)S(1)}, u32[]{:S(2)}, u32[]{:S(2)}) collective-permute-start(bf16[256,576]{0,1:T(8,128)(2,1)S(1)} %fusion.59), channel_id=1, source_target_pairs={{0,32},{32,64},{64,96},{96,0},{1,33},{33,65},{65,97},{97,1},{2,34}... | collective-permute-start | bytes 884744 | tf_op jit(solution)/shard_map/ppermute | solution.py:13
  231.5 8.0 %copy-start.2 = (bf16[256,576]{0,1:T(8,128)(2,1)S(1)}, bf16[256,576]{0,1:T(8,128)(2,1)}, u32[]{:S(2)}) copy-start(bf16[256,576]{0,1:T(8,128)(2,1)} %param.15) | copy-start | bytes 884740
  231.5 8.0 %copy-start.4 = (bf16[256,576]{0,1:T(8,128)(2,1)S(1)}, bf16[256,576]{0,1:T(8,128)(2,1)}, u32[]{:S(2)}) copy-start(bf16[256,576]{0,1:T(8,128)(2,1)} %copy-done.3) | copy-start | bytes 884740
  231.5 8.0 %copy-start.6 = (bf16[256,576]{0,1:T(8,128)(2,1)S(1)}, bf16[256,576]{0,1:T(8,128)(2,1)}, u32[]{:S(2)}) copy-start(bf16[256,576]{0,1:T(8,128)(2,1)} %copy-done.5) | copy-start | bytes 884740
  231.5 8.0 %copy-start.8 = (bf16[256,576]{0,1:T(8,128)(2,1)S(1)}, bf16[256,576]{0,1:T(8,128)(2,1)}, u32[]{:S(2)}) copy-start(bf16[256,576]{0,1:T(8,128)(2,1)} %copy-done.7) | copy-start | bytes 884740
  231.5 8.0 %collective-permute-start.15 = (bf16[256,576]{0,1:T(8,128)(2,1)S(1)}, bf16[256,576]{0,1:T(8,128)(2,1)S(1)}, u32[]{:S(2)}, u32[]{:S(2)}) collective-permute-start(bf16[256,576]{0,1:T(8,128)(2,1)S(1)} %fusion.62), channel_id=1, source_target_pairs={{0,96},{32,0},{64,32},{96,64},{1,97},{33,1},{65,33},{97,65},{2,98}... | collective-permute-start | bytes 884744 | tf_op jit(solution)/shard_map/ppermute | solution.py:13
  241.6 4.0 %collective-permute-start.16 = (bf16[256,576]{0,1:T(8,128)(2,1)S(1)}, bf16[256,576]{0,1:T(8,128)(2,1)S(1)}, u32[]{:S(2)}, u32[]{:S(2)}) collective-permute-start(bf16[256,576]{0,1:T(8,128)(2,1)S(1)} %get-tuple-element.48), channel_id=1, source_target_pairs={{0,128},{1,129},{2,130},{3,131},{4,132},{5,133},{6,134},{7,135},{8... | collective-permute-start | bytes 884744 | tf_op jit(solution)/shard_map/ppermute | solution.py:117
Sparse Core Ops, SparseCore 0:
  13.9 103.4 all-gather.2
  120.6 100.2 all-gather.4

commit v9 on v8

--- a/solution.py
+++ b/solution.py
@@ -41,12 +41,21 @@
 
 
 def decode_scatter(features, decoder, feat_index, n_feat):
-    cols = decoder.shape[1] // n_feat
+    decoder = decoder if isinstance(decoder, tuple) else (decoder,)
+    cols = decoder[0].shape[1] // n_feat
     total = None
     for k in sorted(range(n_feat), key=lambda shift: (-min(shift, n_feat - shift), shift)):
         target = (feat_index + k) % n_feat
-        chunk = lax.dynamic_slice_in_dim(decoder, target * cols, cols, 1)
-        piece = jnp.dot(features, chunk, preferred_element_type=jnp.float32).astype(jnp.bfloat16)
+        piece = None
+        row = 0
+        for part in decoder:
+            chunk = lax.dynamic_slice_in_dim(part, target * cols, cols, 1)
+            product = jnp.dot(
+                features[:, row : row + part.shape[0]], chunk, preferred_element_type=jnp.float32
+            )
+            piece = product if piece is None else piece + product
+            row += part.shape[0]
+        piece = piece.astype(jnp.bfloat16)
         if k:
             piece = within_layer(piece, None, k, n_feat)
         else:
@@ -83,8 +92,12 @@
     swapped_next = lax.ppermute(dec_next[0], "layer", [(0, 1), (1, 0)])
     first_dec = jnp.where(first_core, dec_own[0], swapped_next)
     second_dec = jnp.where(first_core, swapped_next, dec_own[0])
-    first_full = lax.all_gather(first_dec, "tok", axis=1, tiled=True)
-    second_full = lax.all_gather(second_dec, "tok", axis=1, tiled=True)
+    half = second_dec.shape[0] // 2
+    early = lax.all_gather(
+        jnp.concatenate([first_dec, second_dec[:half]]), "tok", axis=1, tiled=True
+    )
+    first_full = early[: first_dec.shape[0]]
+    second_full = (early[first_dec.shape[0] :], lax.all_gather(second_dec[half:], "tok", axis=1, tiled=True))
     mask = feature_mask(block_list, block_count, feat_index, blocks_dev)
     attention = attn_out[0].astype(jnp.float32)
 

time: 254 us -> 258 us (1.016)
  local copies, waits for them, and re-layouts: 2.15 us -> 18.1 us
  waiting for transfers between devices: 163 us -> 152 us
    slice x0 -> x3, local copies, waits for them, and re-layouts: none -> 14.9 us  [the longest x1 9.18 us: shards(): first_full = early[:first_dec.shape[0]]]
    all_gather x2, waiting for transfers between devices: 125 us -> 113 us  [the longest x1 97.1 us: shards(): lax.all_gather(jnp.concatenate([first_dec, second_dec[:half]]), 'tok', ax...]
    dot_general x8 -> x12, matrix products: 22.8 us -> 23.3 us  [decode_scatter(): jnp.dot(features[:, row:row + part.shape[0]], chunk, preferred_element_ty...]
  transfers between devices with their start and end apart: 19 -> 19, of which waited for: 12 -> 11; matrix products, arithmetic and copies ran while one was open for 13% -> 18% of each run, Pallas kernels for 0% -> 0%
where the time goes in v9:
time: 258 us; the launch traced here: 257 us
  waiting for transfers between devices  152 us (59%)
  starting transfers between devices  33.9 us (13%)
  matrix products  30.5 us (12%)
  local copies, waits for them, and re-layouts  18.1 us (7%)
  between operations  14.6 us (6%)
  other arithmetic  7.95 us (3%)
    all_gather x1, waiting for transfers between devices, shards(): lax.all_gather(jnp.concatenate([first_dec, second_dec[:half]]), 'tok', ax...  97.1 us
    dot_general x12, matrix products, decode_scatter(): jnp.dot(features[:, row:row + part.shape[0]], chunk, preferred_element_ty...  23.3 us
    ppermute x1, waiting for transfers between devices, shards(): lax.ppermute(features, 'layer', [(0, 1)])  21.2 us
    all_gather x1, waiting for transfers between devices, shards(): lax.all_gather(second_dec[half:], 'tok', axis=1, tiled=True)  15.4 us
    ppermute x6, starting transfers between devices, within_layer(): return lax.ppermute(shard, GROUP, pairs)  12.4 us
    ppermute x6, starting transfers between devices, within_layer(): lax.ppermute(shard, 'feat', [(i, (i + shift) % n_feat) for i in range(n_f...  11 us
    slice x1, local copies, waits for them, and re-layouts, shards(): first_full = early[:first_dec.shape[0]]  9.18 us
    dot_general x1, matrix products, encode(): jnp.dot(gathered, enc_weight[0], preferred_element_type=jnp.float32)  7.28 us
  transfers between devices with their start and end apart: 19, of which 11 were waited for; matrix products, arithmetic and copies ran while one was open for 18% of the time, Pallas kernels for 0%

profile of v9, /device:TPU:1, one launch (start us, length us, event | category | flops | bytes accessed | tf_op | source)
XLA Modules:
  0.0 257.0 jit_solution(9318054193626236386)
XLA Ops:
  7.2 3.3 %collective-permute-start.4 = (bf16[2048,72]{0,1:T(8,128)(2,1)}, bf16[2048,72]{0,1:T(8,128)(2,1)S(1)}, u32[]{:S(2)}, u32[]{:S(2)}) collective-permute-start(bf16[2048,72]{0,1:T(8,128)(2,1)} %bitcast.55), channel_id=1, source_target_pairs={{0,128},{128,0},{1,129},{129,1},{2,130},{130,2},{3,131},{131,3},{4... | collective-permute-start | bytes 884744 | tf_op jit(solution)/shard_map/ppermute | solution.py:92
  10.5 1.4 collective-permute-done.4
  11.9 1.0 bitcast_select_fusion.1
  13.6 0.8 pad_maximum_fusion.2
  14.6 0.7 all-gather.5.cloned.1.call-update
  15.3 0.7 collective-permute-start
  16.0 0.7 collective-permute-start.1
  16.6 0.7 collective-permute-start.2
  18.3 0.9 copy.19
  20.0 1.1 conditional.2
  20.0 1.1 broadcast.25
  21.1 1.3 collective-permute-start.3
  22.5 21.2 %collective-permute-done.3 = bf16[256,2048]{1,0:T(8,128)(2,1)S(1)} collective-permute-done((bf16[256,2048]{1,0:T(8,128)(2,1)}, bf16[256,2048]{1,0:T(8,128)(2,1)S(1)}, u32[]{:S(2)}, u32[]{:S(2)}) %collective-permute-start.3) | collective-permute-done | bytes 1048608 | tf_op jit(solution)/shard_map/ppermute | solution.py:111
  43.6 1.1 broadcast_select_fusion.1
  44.8 97.1 %all-gather.3.cloned.1.call-done = bf16[3072,2304]{0,1:T(8,128)(2,1)} async-done(((bf16[3072,72]{0,1:T(8,128)(2,1)}), bf16[3072,2304]{0,1:T(8,128)(2,1)}) %all-gather.3.cloned.1.call-update) | async-done | bytes 14155792 | tf_op jit(solution)/shard_map/all_gather | solution.py:96
  141.8 9.2 %slice.31 = bf16[2048,2304]{0,1:T(8,128)(2,1)} slice(bf16[3072,2304]{0,1:T(8,128)(2,1)} %all-gather.3.cloned.1.call-done), slice={[0:2048], [0:2304]} | slice | bytes 18874368 | tf_op jit(solution)/shard_map/slice | solution.py:99
  151.0 3.3 %fusion.40 = bf16[256,576]{0,1:T(8,128)(2,1)} fusion(bf16[256,2048]{1,0:T(8,128)(2,1)S(1)} %copy-done.14, bf16[2048,2304]{0,1:T(8,128)(2,1)} %slice.31, s32[]{:T(128)S(6)} %select_n.362), kind=kOutput, calls=%fused_computation.29 | convolution fusion | flops 604127232 | bytes 3702788 | tf_op jit(solution)/shard_map/dot_general | solution.py:53
  154.3 2.7 %collective-permute-start.5 = (bf16[256,576]{0,1:T(8,128)(2,1)}, bf16[256,576]{0,1:T(8,128)(2,1)S(1)}, u32[]{:S(2)}, u32[]{:S(2)}) collective-permute-start(bf16[256,576]{0,1:T(8,128)(2,1)} %fusion.40), channel_id=1, source_target_pairs={{0,64},{32,96},{64,0},{96,32},{1,65},{33,97},{65,1},{97,33},{2,66}... | collective-permute-start | bytes 884744 | tf_op jit(solution)/shard_map/ppermute | solution.py:13
  157.0 3.3 %fusion.43 = bf16[256,576]{0,1:T(8,128)(2,1)} fusion(bf16[256,2048]{1,0:T(8,128)(2,1)S(1)} %copy-done.15, bf16[2048,2304]{0,1:T(8,128)(2,1)} %slice.31, s32[]{:T(128)S(6)} %select_n.364), kind=kOutput, calls=%fused_computation.30 | convolution fusion | flops 604127232 | bytes 3702788 | tf_op jit(solution)/shard_map/dot_general | solution.py:53
  160.6 3.3 %fusion.46 = bf16[256,576]{0,1:T(8,128)(2,1)} fusion(bf16[256,2048]{1,0:T(8,128)(2,1)S(1)} %copy-done.15, bf16[2048,2304]{0,1:T(8,128)(2,1)} %slice.31, s32[]{:T(128)S(6)} %select_n.366), kind=kOutput, calls=%fused_computation.31 | convolution fusion | flops 604127232 | bytes 3702788 | tf_op jit(solution)/shard_map/dot_general | solution.py:53
  163.8 2.4 collective-permute-start.7
  166.2 2.9 %fusion.49 = bf16[256,576]{0,1:T(8,128)(2,1)S(1)} fusion(bf16[256,2048]{1,0:T(8,128)(2,1)} %broadcast_select_fusion.1, bf16[2048,2304]{0,1:T(8,128)(2,1)} %slice.31, s32[]{:T(128)S(6)} %select_n.367), kind=kOutput, calls=%fused_computation.32 | convolution fusion | flops 604127232 | bytes 3702788 | tf_op jit(solution)/shard_map/dot_general | solution.py:53
  169.1 1.3 collective-permute-done.6
  170.9 1.3 fusion.75
  172.2 3.1 %collective-permute-start.8 = (bf16[256,576]{0,1:T(8,128)(2,1)S(1)}, bf16[256,576]{0,1:T(8,128)(2,1)S(1)}, u32[]{:S(2)}, u32[]{:S(2)}) collective-permute-start(bf16[256,576]{0,1:T(8,128)(2,1)S(1)} %fusion.75), channel_id=1, source_target_pairs={{0,128},{128,0},{1,129},{129,1},{2,130},{130,2},{3,131},{131,3},{4... | collective-permute-start | bytes 884744 | tf_op jit(solution)/shard_map/ppermute | solution.py:116
  175.3 1.2 collective-permute-done.8
  176.5 3.8 %collective-permute-start.10 = (bf16[256,576]{0,1:T(8,128)(2,1)S(1)}, bf16[256,576]{0,1:T(8,128)(2,1)S(1)}, u32[]{:S(2)}, u32[]{:S(2)}) collective-permute-start(bf16[256,576]{0,1:T(8,128)(2,1)S(1)} %collective-permute-done.8), channel_id=1, source_target_pairs={{128,192},{160,224},{192,128},{224,160},{129,193},{161,225},{193,1... | collective-permute-start | bytes 884744 | tf_op jit(solution)/shard_map/ppermute | solution.py:17
  180.3 4.0 %collective-permute-start.11 = (bf16[256,576]{0,1:T(8,128)(2,1)S(1)}, bf16[256,576]{0,1:T(8,128)(2,1)S(1)}, u32[]{:S(2)}, u32[]{:S(2)}) collective-permute-start(bf16[256,576]{0,1:T(8,128)(2,1)S(1)} %collective-permute-done.8), channel_id=1, source_target_pairs={{128,160},{160,192},{192,224},{224,128},{129,161},{161,193},{193,2... | collective-permute-start | bytes 884744 | tf_op jit(solution)/shard_map/ppermute | solution.py:17
  184.3 2.5 collective-permute-start.9
  186.9 2.2 collective-permute-done.11
  189.0 2.8 %collective-permute-done.9 = bf16[256,576]{0,1:T(8,128)(2,1)S(1)} collective-permute-done((bf16[256,576]{0,1:T(8,128)(2,1)S(1)}, bf16[256,576]{0,1:T(8,128)(2,1)S(1)}, u32[]{:S(2)}, u32[]{:S(2)}) %collective-permute-start.9) | collective-permute-done | bytes 294944 | tf_op jit(solution)/shard_map/ppermute | solution.py:17
  192.1 7.3 %conditional.3 = (bf16[256,2048]{1,0:T(8,128)(2,1)}) conditional(s32[]{:T(128)} %convert_element_type.88, (bf16[1,2304,2048]{2,1,0:T(8,128)(2,1)}, bf16[256,2304]{0,1:T(8,128)(2,1)S(1)}, f32[1,2048]{1,0:T(1,128)S(1)}, f32[256,2048]{1,0:T(8,128)S(1)}) %tuple.47, () %tuple.23), branch_computations={%region_3.4_spmd, %region_4.5_spmd} | conditional | flops 2418016256 | bytes 13770760 | solution.py:121
  192.1 7.3 %fusion.25 = bf16[256,2048]{1,0:T(8,128)(2,1)} fusion(f32[256,2048]{1,0:T(8,128)S(1)} %get-tuple-element.29, bf16[256,2304]{0,1:T(8,128)(2,1)S(1)} %get-tuple-element.45, bf16[1,2304,2048]{2,1,0:T(8,128)(2,1)} %get-tuple-element.27, f32[2048]{0:T(1024)S(1)} %bitcast.53), kind=kOutput, calls=%fused_computation.11 | convolution fusion | flops 2418016256 | bytes 13770752 | tf_op jit(solution)/shard_map/cond/branch_0_fun/dot_general | solution.py:79
  199.4 1.5 collective-permute-start.12
  200.9 5.1 %slice.33 = bf16[1024,2304]{0,1:T(8,128)(2,1)} slice(bf16[3072,2304]{0,1:T(8,128)(2,1)} %all-gather.3.cloned.1.call-done), slice={[2048:3072], [0:2304]} | slice | bytes 9437184 | tf_op jit(solution)/shard_map/slice | solution.py:100
  206.1 15.4 %all-gather.5.cloned.1.call-done = bf16[1024,2304]{0,1:T(8,128)(2,1)} async-done(((bf16[1024,72]{0,1:T(8,128)(2,1)}), bf16[1024,2304]{0,1:T(8,128)(2,1)}) %all-gather.5.cloned.1.call-update) | async-done | bytes 4718608 | tf_op jit(solution)/shard_map/all_gather | solution.py:100
  221.5 1.8 fusion.61
  223.3 1.9 fusion.36
  225.3 2.8 %collective-permute-start.13 = (bf16[256,576]{0,1:T(8,128)(2,1)S(1)}, bf16[256,576]{0,1:T(8,128)(2,1)S(1)}, u32[]{:S(2)}, u32[]{:S(2)}) collective-permute-start(bf16[256,576]{0,1:T(8,128)(2,1)S(1)} %fusion.36), channel_id=1, source_target_pairs={{0,64},{32,96},{64,0},{96,32},{1,65},{33,97},{65,1},{97,33},{2,66}... | collective-permute-start | bytes 884744 | tf_op jit(solution)/shard_map/ppermute | solution.py:13
  228.1 1.8 fusion.58
  230.8 1.8 fusion.55
  233.1 2.5 collective-permute-start.15
  235.6 1.8 fusion.52
  237.9 3.4 %collective-permute-done.14 = bf16[256,576]{0,1:T(8,128)(2,1)S(1)} collective-permute-done((bf16[256,576]{0,1:T(8,128)(2,1)S(1)}, bf16[256,576]{0,1:T(8,128)(2,1)S(1)}, u32[]{:S(2)}, u32[]{:S(2)}) %collective-permute-start.14) | collective-permute-done | bytes 294944 | tf_op jit(solution)/shard_map/ppermute | solution.py:13
  241.3 2.0 fusion.76
  243.3 1.3 collective-permute-start.16
  244.6 4.8 %collective-permute-done.16 = bf16[256,576]{0,1:T(8,128)(2,1)S(1)} collective-permute-done((bf16[256,576]{0,1:T(8,128)(2,1)S(1)}, bf16[256,576]{0,1:T(8,128)(2,1)S(1)}, u32[]{:S(2)}, u32[]{:S(2)}) %collective-permute-start.16) | collective-permute-done | bytes 294944 | tf_op jit(solution)/shard_map/ppermute | solution.py:130
  249.4 0.8 select_bitcast_fusion
  (71 shorter events, 5.5 us)
Async XLA Ops:
  7.2 8.1 %copy-start.2 = (bf16[256,576]{0,1:T(8,128)(2,1)S(1)}, bf16[256,576]{0,1:T(8,128)(2,1)}, u32[]{:S(2)}) copy-start(bf16[256,576]{0,1:T(8,128)(2,1)} %param.13) | copy-start | bytes 884740
  7.2 10.3 %copy-start.19 = (s32[1,2]{1,0:T(1,128)S(1)}, s32[1,2]{1,0:T(1,128)}, u32[]{:S(2)}) copy-start(s32[1,2]{1,0:T(1,128)} %param.21) | copy-start | bytes 28
  7.2 10.3 %copy-start.18 = (s32[1,2,32]{2,1,0:T(2,128)S(1)}, s32[1,2,32]{2,1,0:T(2,128)}, u32[]{:S(2)}) copy-start(s32[1,2,32]{2,1,0:T(2,128)} %param.20) | copy-start | bytes 772
  7.2 134.6 %all-gather.3.cloned.1.call-start = ((), (), s32[]{:S(2)}) async-start(), calls=%async_computation | async-start | bytes 14598144 | tf_op jit(solution)/shard_map/all_gather | solution.py:96
  7.2 4.7 %collective-permute-start.4 = (bf16[2048,72]{0,1:T(8,128)(2,1)}, bf16[2048,72]{0,1:T(8,128)(2,1)S(1)}, u32[]{:S(2)}, u32[]{:S(2)}) collective-permute-start(bf16[2048,72]{0,1:T(8,128)(2,1)} %bitcast.55), channel_id=1, source_target_pairs={{0,128},{128,0},{1,129},{129,1},{2,130},{130,2},{3,131},{131,3},{4... | collective-permute-start | bytes 884744 | tf_op jit(solution)/shard_map/ppermute | solution.py:92
  14.5 207.0 %all-gather.5.cloned.1.call-start = ((), (), s32[]{:S(2)}) async-start(), calls=%async_computation.1 | async-start | bytes 4866048 | tf_op jit(solution)/shard_map/all_gather | solution.py:100
  15.3 4.0 %collective-permute-start = (bf16[256,576]{0,1:T(8,128)(2,1)S(1)}, bf16[256,576]{0,1:T(8,128)(2,1)S(1)}, u32[]{:S(2)}, u32[]{:S(2)}) collective-permute-start(bf16[256,576]{0,1:T(8,128)(2,1)S(1)} %copy-done.2), channel_id=1, source_target_pairs={{0,96},{32,0},{64,32},{96,64},{1,97},{33,1},{65,33},{97,65},{2,98}... | collective-permute-start | bytes 884744 | tf_op jit(solution)/shard_map/ppermute | solution.py:17
  16.0 3.3 %collective-permute-start.1 = (bf16[256,576]{0,1:T(8,128)(2,1)S(1)}, bf16[256,576]{0,1:T(8,128)(2,1)S(1)}, u32[]{:S(2)}, u32[]{:S(2)}) collective-permute-start(bf16[256,576]{0,1:T(8,128)(2,1)S(1)} %copy-done.2), channel_id=1, source_target_pairs={{0,64},{32,96},{64,0},{96,32},{1,65},{33,97},{65,1},{97,33},{2,66}... | collective-permute-start | bytes 884744 | tf_op jit(solution)/shard_map/ppermute | solution.py:17
  16.6 2.6 %collective-permute-start.2 = (bf16[256,576]{0,1:T(8,128)(2,1)S(1)}, bf16[256,576]{0,1:T(8,128)(2,1)S(1)}, u32[]{:S(2)}, u32[]{:S(2)}) collective-permute-start(bf16[256,576]{0,1:T(8,128)(2,1)S(1)} %copy-done.2), channel_id=1, source_target_pairs={{0,32},{32,64},{64,96},{96,0},{1,33},{33,65},{65,97},{97,1},{2,34}... | collective-permute-start | bytes 884744 | tf_op jit(solution)/shard_map/ppermute | solution.py:17
  19.3 0.7 copy-start.17
  21.1 22.5 %collective-permute-start.3 = (bf16[256,2048]{1,0:T(8,128)(2,1)}, bf16[256,2048]{1,0:T(8,128)(2,1)S(1)}, u32[]{:S(2)}, u32[]{:S(2)}) collective-permute-start(bf16[256,2048]{1,0:T(8,128)(2,1)} %get-tuple-element.60), channel_id=1, source_target_pairs={{0,128},{1,129},{2,130},{3,131},{4,132},{5,133},{6,134},{7,135},{8... | collective-permute-start | bytes 3145736 | tf_op jit(solution)/shard_map/ppermute | solution.py:111
  44.8 106.3 %copy-start.14 = (bf16[256,2048]{1,0:T(8,128)(2,1)S(1)}, bf16[256,2048]{1,0:T(8,128)(2,1)}, u32[]{:S(2)}) copy-start(bf16[256,2048]{1,0:T(8,128)(2,1)} %broadcast_select_fusion.1) | copy-start | bytes 3145732
  151.0 6.0 %copy-start.15 = (bf16[256,2048]{1,0:T(8,128)(2,1)S(1)}, bf16[256,2048]{1,0:T(8,128)(2,1)}, u32[]{:S(2)}) copy-start(bf16[256,2048]{1,0:T(8,128)(2,1)} %broadcast_select_fusion.1) | copy-start | bytes 3145732
  154.3 14.8 %collective-permute-start.5 = (bf16[256,576]{0,1:T(8,128)(2,1)}, bf16[256,576]{0,1:T(8,128)(2,1)S(1)}, u32[]{:S(2)}, u32[]{:S(2)}) collective-permute-start(bf16[256,576]{0,1:T(8,128)(2,1)} %fusion.40), channel_id=1, source_target_pairs={{0,64},{32,96},{64,0},{96,32},{1,65},{33,97},{65,1},{97,33},{2,66}... | collective-permute-start | bytes 884744 | tf_op jit(solution)/shard_map/ppermute | solution.py:13
  160.3 10.2 %collective-permute-start.6 = (bf16[256,576]{0,1:T(8,128)(2,1)}, bf16[256,576]{0,1:T(8,128)(2,1)S(1)}, u32[]{:S(2)}, u32[]{:S(2)}) collective-permute-start(bf16[256,576]{0,1:T(8,128)(2,1)} %fusion.43), channel_id=1, source_target_pairs={{0,32},{32,64},{64,96},{96,0},{1,33},{33,65},{65,97},{97,1},{2,34}... | collective-permute-start | bytes 884744 | tf_op jit(solution)/shard_map/ppermute | solution.py:13
  163.8 7.1 %copy-start.3 = (bf16[256,576]{0,1:T(8,128)(2,1)S(1)}, bf16[256,576]{0,1:T(8,128)(2,1)}, u32[]{:S(2)}) copy-start(bf16[256,576]{0,1:T(8,128)(2,1)} %param.13) | copy-start | bytes 884740
  163.8 7.1 %copy-start.6 = (bf16[256,576]{0,1:T(8,128)(2,1)S(1)}, bf16[256,576]{0,1:T(8,128)(2,1)}, u32[]{:S(2)}) copy-start(bf16[256,576]{0,1:T(8,128)(2,1)} %param.15) | copy-start | bytes 884740
  163.8 7.1 %collective-permute-start.7 = (bf16[256,576]{0,1:T(8,128)(2,1)}, bf16[256,576]{0,1:T(8,128)(2,1)}, u32[]{:S(2)}, u32[]{:S(2)}) collective-permute-start(bf16[256,576]{0,1:T(8,128)(2,1)} %fusion.46), channel_id=1, source_target_pairs={{0,96},{32,0},{64,32},{96,64},{1,97},{33,1},{65,33},{97,65},{2,98}... | collective-permute-start | bytes 884744 | tf_op jit(solution)/shard_map/ppermute | solution.py:13
  166.2 4.7 %copy-start.16 = (bf16[1,256,576]{1,2,0:T(8,128)(2,1)S(1)}, bf16[1,256,576]{1,2,0:T(8,128)(2,1)}, u32[]{:S(2)}) copy-start(bf16[1,256,576]{1,2,0:T(8,128)(2,1)} %param.14) | copy-start | bytes 884740
  169.1 22.9 %copy-start.12 = (bf16[256,576]{0,1:T(8,128)(2,1)}, bf16[256,576]{0,1:T(8,128)(2,1)S(1)}, u32[]{:S(2)}) copy-start(bf16[256,576]{0,1:T(8,128)(2,1)S(1)} %fusion.49) | copy-start | bytes 884740
  169.1 22.9 %copy-start.8 = (bf16[256,576]{0,1:T(8,128)(2,1)}, bf16[256,576]{0,1:T(8,128)(2,1)S(1)}, u32[]{:S(2)}) copy-start(bf16[256,576]{0,1:T(8,128)(2,1)S(1)} %collective-permute-done.5) | copy-start | bytes 884740
  170.5 21.5 %copy-start.10 = (bf16[256,576]{0,1:T(8,128)(2,1)}, bf16[256,576]{0,1:T(8,128)(2,1)S(1)}, u32[]{:S(2)}) copy-start(bf16[256,576]{0,1:T(8,128)(2,1)S(1)} %collective-permute-done.6) | copy-start | bytes 884740
  172.2 4.3 %collective-permute-start.8 = (bf16[256,576]{0,1:T(8,128)(2,1)S(1)}, bf16[256,576]{0,1:T(8,128)(2,1)S(1)}, u32[]{:S(2)}, u32[]{:S(2)}) collective-permute-start(bf16[256,576]{0,1:T(8,128)(2,1)S(1)} %fusion.75), channel_id=1, source_target_pairs={{0,128},{128,0},{1,129},{129,1},{2,130},{130,2},{3,131},{131,3},{4... | collective-permute-start | bytes 884744 | tf_op jit(solution)/shard_map/ppermute | solution.py:116
  176.5 15.5 %copy-start.4 = (bf16[256,576]{0,1:T(8,128)(2,1)}, bf16[256,576]{0,1:T(8,128)(2,1)S(1)}, u32[]{:S(2)}) copy-start(bf16[256,576]{0,1:T(8,128)(2,1)S(1)} %collective-permute-done.8) | copy-start | bytes 884740
  176.5 10.3 %collective-permute-start.10 = (bf16[256,576]{0,1:T(8,128)(2,1)S(1)}, bf16[256,576]{0,1:T(8,128)(2,1)S(1)}, u32[]{:S(2)}, u32[]{:S(2)}) collective-permute-start(bf16[256,576]{0,1:T(8,128)(2,1)S(1)} %collective-permute-done.8), channel_id=1, source_target_pairs={{128,192},{160,224},{192,128},{224,160},{129,193},{161,225},{193,1... | collective-permute-start | bytes 884744 | tf_op jit(solution)/shard_map/ppermute | solution.py:17
  180.3 8.7 %collective-permute-start.11 = (bf16[256,576]{0,1:T(8,128)(2,1)S(1)}, bf16[256,576]{0,1:T(8,128)(2,1)S(1)}, u32[]{:S(2)}, u32[]{:S(2)}) collective-permute-start(bf16[256,576]{0,1:T(8,128)(2,1)S(1)} %collective-permute-done.8), channel_id=1, source_target_pairs={{128,160},{160,192},{192,224},{224,128},{129,161},{161,193},{193,2... | collective-permute-start | bytes 884744 | tf_op jit(solution)/shard_map/ppermute | solution.py:17
  184.3 7.5 %collective-permute-start.9 = (bf16[256,576]{0,1:T(8,128)(2,1)S(1)}, bf16[256,576]{0,1:T(8,128)(2,1)S(1)}, u32[]{:S(2)}, u32[]{:S(2)}) collective-permute-start(bf16[256,576]{0,1:T(8,128)(2,1)S(1)} %collective-permute-done.8), channel_id=1, source_target_pairs={{128,224},{160,128},{192,160},{224,192},{129,225},{161,129},{193,1... | collective-permute-start | bytes 884744 | tf_op jit(solution)/shard_map/ppermute | solution.py:17
  199.4 6.6 %copy-start.1 = (bf16[256,2048]{1,0:T(8,128)(2,1)S(1)}, bf16[256,2048]{1,0:T(8,128)(2,1)}, u32[]{:S(2)}) copy-start(bf16[256,2048]{1,0:T(8,128)(2,1)} %get-tuple-element.61) | copy-start | bytes 3145732
  199.4 6.6 %collective-permute-start.12 = (bf16[256,2048]{1,0:T(8,128)(2,1)}, bf16[256,2048]{1,0:T(8,128)(2,1)S(1)}, u32[]{:S(2)}, u32[]{:S(2)}) collective-permute-start(bf16[256,2048]{1,0:T(8,128)(2,1)} %get-tuple-element.61), channel_id=1, source_target_pairs={{128,0},{129,1},{130,2},{131,3},{132,4},{133,5},{134,6},{135,7},{1... | collective-permute-start | bytes 3145736 | tf_op jit(solution)/shard_map/ppermute | solution.py:127
  223.3 6.5 %copy-start = (bf16[1024,2304]{0,1:T(8,128)(2,1)S(1)}, bf16[1024,2304]{0,1:T(8,128)(2,1)}, u32[]{:S(2)}) copy-start(bf16[1024,2304]{0,1:T(8,128)(2,1)} %slice.33) | copy-start | bytes 14155780
  225.3 12.6 %collective-permute-start.13 = (bf16[256,576]{0,1:T(8,128)(2,1)S(1)}, bf16[256,576]{0,1:T(8,128)(2,1)S(1)}, u32[]{:S(2)}, u32[]{:S(2)}) collective-permute-start(bf16[256,576]{0,1:T(8,128)(2,1)S(1)} %fusion.36), channel_id=1, source_target_pairs={{0,64},{32,96},{64,0},{96,32},{1,65},{33,97},{65,1},{97,33},{2,66}... | collective-permute-start | bytes 884744 | tf_op jit(solution)/shard_map/ppermute | solution.py:13
  230.4 10.9 %collective-permute-start.14 = (bf16[256,576]{0,1:T(8,128)(2,1)S(1)}, bf16[256,576]{0,1:T(8,128)(2,1)S(1)}, u32[]{:S(2)}, u32[]{:S(2)}) collective-permute-start(bf16[256,576]{0,1:T(8,128)(2,1)S(1)} %fusion.37), channel_id=1, source_target_pairs={{0,32},{32,64},{64,96},{96,0},{1,33},{33,65},{65,97},{97,1},{2,34}... | collective-permute-start | bytes 884744 | tf_op jit(solution)/shard_map/ppermute | solution.py:13
  233.1 8.2 %copy-start.7 = (bf16[256,576]{0,1:T(8,128)(2,1)S(1)}, bf16[256,576]{0,1:T(8,128)(2,1)}, u32[]{:S(2)}) copy-start(bf16[256,576]{0,1:T(8,128)(2,1)} %param.15) | copy-start | bytes 884740
  233.1 8.2 %copy-start.9 = (bf16[256,576]{0,1:T(8,128)(2,1)S(1)}, bf16[256,576]{0,1:T(8,128)(2,1)}, u32[]{:S(2)}) copy-start(bf16[256,576]{0,1:T(8,128)(2,1)} %copy-done.8) | copy-start | bytes 884740
  233.1 8.2 %copy-start.11 = (bf16[256,576]{0,1:T(8,128)(2,1)S(1)}, bf16[256,576]{0,1:T(8,128)(2,1)}, u32[]{:S(2)}) copy-start(bf16[256,576]{0,1:T(8,128)(2,1)} %copy-done.10) | copy-start | bytes 884740
  233.1 8.2 %copy-start.13 = (bf16[256,576]{0,1:T(8,128)(2,1)S(1)}, bf16[256,576]{0,1:T(8,128)(2,1)}, u32[]{:S(2)}) copy-start(bf16[256,576]{0,1:T(8,128)(2,1)} %copy-done.12) | copy-start | bytes 884740
  233.1 8.2 %collective-permute-start.15 = (bf16[256,576]{0,1:T(8,128)(2,1)S(1)}, bf16[256,576]{0,1:T(8,128)(2,1)S(1)}, u32[]{:S(2)}, u32[]{:S(2)}) collective-permute-start(bf16[256,576]{0,1:T(8,128)(2,1)S(1)} %fusion.38), channel_id=1, source_target_pairs={{0,96},{32,0},{64,32},{96,64},{1,97},{33,1},{65,33},{97,65},{2,98}... | collective-permute-start | bytes 884744 | tf_op jit(solution)/shard_map/ppermute | solution.py:13
  237.4 12.0 %copy-start.5 = (bf16[256,576]{0,1:T(8,128)(2,1)S(1)}, bf16[256,576]{0,1:T(8,128)(2,1)}, u32[]{:S(2)}) copy-start(bf16[256,576]{0,1:T(8,128)(2,1)} %copy-done.4) | copy-start | bytes 884740
  243.3 6.1 %collective-permute-start.16 = (bf16[256,576]{0,1:T(8,128)(2,1)S(1)}, bf16[256,576]{0,1:T(8,128)(2,1)S(1)}, u32[]{:S(2)}, u32[]{:S(2)}) collective-permute-start(bf16[256,576]{0,1:T(8,128)(2,1)S(1)} %get-tuple-element.48), channel_id=1, source_target_pairs={{0,128},{1,129},{2,130},{3,131},{4,132},{5,133},{6,134},{7,135},{8... | collective-permute-start | bytes 884744 | tf_op jit(solution)/shard_map/ppermute | solution.py:130
Sparse Core Ops, SparseCore 0:
  14.6 127.1 all-gather.2
  144.4 77.0 all-gather.4

commit v10 on v8

--- a/solution.py
+++ b/solution.py
@@ -56,6 +56,27 @@
     return total
 
 
+def decode_scatter_across(features, decoder, feat_index, n_feat):
+    cols = decoder.shape[1] // n_feat
+    own_total = None
+    next_total = None
+    for k in sorted(range(n_feat), key=lambda shift: (-min(shift, n_feat - shift), shift)):
+        target = (feat_index + k) % n_feat
+        chunk = lax.dynamic_slice_in_dim(decoder, target * cols, cols, 1)
+        piece = jnp.dot(features, chunk, preferred_element_type=jnp.float32).astype(jnp.bfloat16)
+        cross = lax.ppermute(
+            piece, GROUP, [(i, n_feat + (i + k) % n_feat) for i in range(n_feat)]
+        ).astype(jnp.float32)
+        next_total = cross if next_total is None else next_total + cross
+        if k:
+            mine = within_layer(piece, 1, k, n_feat)
+        else:
+            mine = lax.optimization_barrier(piece)
+        mine = mine.astype(jnp.float32)
+        own_total = mine if own_total is None else own_total + mine
+    return own_total, next_total
+
+
 def feature_mask(block_list, block_count, feat_index, blocks_dev):
     listed = block_list[0]
     in_use = jnp.arange(listed.shape[1], dtype=jnp.int32)[None, :] < block_count[0][:, None]
@@ -112,9 +133,9 @@
         gathered,
     )
     features = jnp.where(first_core, lax.ppermute(features, "layer", [(1, 0)]), features)
-    summed = decode_scatter(features, second_full, feat_index, n_feat)
+    summed, next_second = decode_scatter_across(features, second_full, feat_index, n_feat)
     recon_second = summed + outgoing_first.astype(jnp.float32)
-    outgoing_second = lax.ppermute(summed.astype(jnp.bfloat16), "layer", [(0, 1)])
+    outgoing_second = next_second.astype(jnp.bfloat16)
 
     recon_out = jnp.where(first_core, recon_first, recon_second).astype(jnp.bfloat16)
     outgoing_out = jnp.where(first_core, swapped, outgoing_second)

time: 254 us -> 261 us (1.028)
  starting transfers between devices: 33.5 us -> 43 us
  waiting for transfers between devices: 163 us -> 160 us
    ppermute x6 -> x9, starting transfers between devices: 12.3 us -> 23.4 us  [within_layer(): return lax.ppermute(shard, GROUP, pairs)]
    dot_general x0 -> x4, matrix products: none -> 9.91 us  [decode_scatter_across(): jnp.dot(features, chunk, preferred_element_type=jnp.float32)]
    dot_general x8 -> x4, matrix products: 22.8 us -> 12.9 us  [decode_scatter(): jnp.dot(features, chunk, preferred_element_type=jnp.float32)]
    ppermute x6 -> x3, starting transfers between devices: 11 us -> 5.38 us  [within_layer(): lax.ppermute(shard, 'feat', [(i, (i + shift) % n_feat) for i in range(n_f...]
    ppermute x1 -> x4, starting transfers between devices: 1.28 us -> 5.3 us  [decode_scatter_across(): lax.ppermute(piece, GROUP, [(i, n_feat + (i + k) % n_feat) for i in range...]
    ppermute x6 -> x3, waiting for transfers between devices: 4.87 us -> 1.85 us  [within_layer(): lax.ppermute(shard, 'feat', [(i, (i + shift) % n_feat) for i in range(n_f...]
    ppermute x1 -> x4, waiting for transfers between devices: 2.75 us -> 0.01 us  [decode_scatter_across(): lax.ppermute(piece, GROUP, [(i, n_feat + (i + k) % n_feat) for i in range...]
    ppermute x6 -> x9, waiting for transfers between devices: 4.95 us -> 7.68 us  [within_layer(): return lax.ppermute(shard, GROUP, pairs)]
  transfers between devices with their start and end apart: 19 -> 22, of which waited for: 12 -> 12; matrix products, arithmetic and copies ran while one was open for 13% -> 13% of each run, Pallas kernels for 0% -> 0%
where the time goes in v10:
time: 261 us; the launch traced here: 260 us
  waiting for transfers between devices  160 us (61%)
  starting transfers between devices  43 us (16%)
  matrix products  29.2 us (11%)
  between operations  14.6 us (6%)
  other arithmetic  10.6 us (4%)
    all_gather x1, waiting for transfers between devices, shards(): first_full = lax.all_gather(first_dec, 'tok', axis=1, tiled=True)  73 us
    all_gather x1, waiting for transfers between devices, shards(): second_full = lax.all_gather(second_dec, 'tok', axis=1, tiled=True)  52 us
    ppermute x9, starting transfers between devices, within_layer(): return lax.ppermute(shard, GROUP, pairs)  23.4 us
    ppermute x1, waiting for transfers between devices, shards(): lax.ppermute(features, 'layer', [(0, 1)])  20 us
    dot_general x4, matrix products, decode_scatter(): jnp.dot(features, chunk, preferred_element_type=jnp.float32)  12.9 us
    dot_general x4, matrix products, decode_scatter_across(): jnp.dot(features, chunk, preferred_element_type=jnp.float32)  9.91 us
    ppermute x9, waiting for transfers between devices, within_layer(): return lax.ppermute(shard, GROUP, pairs)  7.68 us
    dot_general x1, matrix products, encode(): jnp.dot(gathered, enc_weight[0], preferred_element_type=jnp.float32)  6.31 us
  transfers between devices with their start and end apart: 22, of which 12 were waited for; matrix products, arithmetic and copies ran while one was open for 13% of the time, Pallas kernels for 0%

profile of v10, /device:TPU:1, one launch (start us, length us, event | category | flops | bytes accessed | tf_op | source)
XLA Modules:
  0.0 259.9 jit_solution(6782876499148224948)
XLA Ops:
  7.2 3.3 %collective-permute-start.4 = (bf16[2048,72]{0,1:T(8,128)(2,1)}, bf16[2048,72]{0,1:T(8,128)(2,1)S(1)}, u32[]{:S(2)}, u32[]{:S(2)}) collective-permute-start(bf16[2048,72]{0,1:T(8,128)(2,1)} %bitcast.59), channel_id=1, source_target_pairs={{0,128},{128,0},{1,129},{129,1},{2,130},{130,2},{3,131},{131,3},{4... | collective-permute-start | bytes 884744 | tf_op jit(solution)/shard_map/ppermute | solution.py:104
  10.5 1.4 collective-permute-done.4
  11.9 1.8 bitcast_select_fusion
  13.8 0.7 all-gather.5.cloned.1.call-update
  14.5 0.7 collective-permute-start
  15.2 0.7 collective-permute-start.1
  16.7 0.7 iota_compare_fusion
  17.4 0.9 and_reduce_fusion
  18.9 0.9 copy.19
  20.7 1.3 collective-permute-start.3
  22.1 20.0 %collective-permute-done.3 = bf16[256,2048]{1,0:T(8,128)(2,1)} collective-permute-done((bf16[256,2048]{1,0:T(8,128)(2,1)S(1)}, bf16[256,2048]{1,0:T(8,128)(2,1)}, u32[]{:S(2)}, u32[]{:S(2)}) %collective-permute-start.3) | collective-permute-done | bytes 1048608 | tf_op jit(solution)/shard_map/ppermute | solution.py:119
  42.1 2.3 broadcast_select_fusion.1
  44.4 73.0 %all-gather.3.cloned.1.call-done = bf16[2048,2304]{0,1:T(8,128)(2,1)} async-done(((bf16[2048,72]{0,1:T(8,128)(2,1)}), bf16[2048,2304]{0,1:T(8,128)(2,1)}) %all-gather.3.cloned.1.call-update) | async-done | bytes 9437200 | tf_op jit(solution)/shard_map/all_gather | solution.py:107
  117.4 3.6 %fusion.44 = bf16[256,576]{0,1:T(8,128)(2,1)} fusion(bf16[256,2048]{1,0:T(8,128)(2,1)} %broadcast_select_fusion.1, bf16[2048,2304]{0,1:T(8,128)(2,1)} %all-gather.3.cloned.1.call-done, s32[]{:T(128)S(6)} %select_n.357), kind=kOutput, calls=%fused_computation.29 | convolution fusion | flops 604127232 | bytes 3702788 | tf_op jit(solution)/shard_map/dot_general | solution.py:49
  121.0 2.7 %collective-permute-start.5 = (bf16[256,576]{0,1:T(8,128)(2,1)}, bf16[256,576]{0,1:T(8,128)(2,1)S(1)}, u32[]{:S(2)}, u32[]{:S(2)}) collective-permute-start(bf16[256,576]{0,1:T(8,128)(2,1)} %fusion.44), channel_id=1, source_target_pairs={{0,64},{32,96},{64,0},{96,32},{1,65},{33,97},{65,1},{97,33},{2,66}... | collective-permute-start | bytes 884744 | tf_op jit(solution)/shard_map/ppermute | solution.py:13
  123.7 3.2 %fusion.47 = bf16[256,576]{0,1:T(8,128)(2,1)} fusion(bf16[256,2048]{1,0:T(8,128)(2,1)S(1)} %copy-done.9, bf16[2048,2304]{0,1:T(8,128)(2,1)} %all-gather.3.cloned.1.call-done, s32[]{:T(128)S(6)} %select_n.359), kind=kOutput, calls=%fused_computation.30 | convolution fusion | flops 604127232 | bytes 3702788 | tf_op jit(solution)/shard_map/dot_general | solution.py:49
  127.3 3.3 %fusion.50 = bf16[256,576]{0,1:T(8,128)(2,1)} fusion(bf16[256,2048]{1,0:T(8,128)(2,1)S(1)} %copy-done.9, bf16[2048,2304]{0,1:T(8,128)(2,1)} %all-gather.3.cloned.1.call-done, s32[]{:T(128)S(6)} %select_n.361), kind=kOutput, calls=%fused_computation.31 | convolution fusion | flops 604127232 | bytes 3702788 | tf_op jit(solution)/shard_map/dot_general | solution.py:49
  130.5 2.4 collective-permute-start.7
  132.9 2.8 %fusion.53 = bf16[256,576]{0,1:T(8,128)(2,1)S(1)} fusion(bf16[256,2048]{1,0:T(8,128)(2,1)} %broadcast_select_fusion.1, bf16[2048,2304]{0,1:T(8,128)(2,1)} %all-gather.3.cloned.1.call-done, s32[]{:T(128)S(6)} %select_n.362), kind=kOutput, calls=%fused_computation.32 | convolution fusion | flops 604127232 | bytes 3702788 | tf_op jit(solution)/shard_map/dot_general | solution.py:49
  135.8 1.5 collective-permute-done.6
  137.6 1.3 fusion.73
  138.9 2.9 %collective-permute-start.8 = (bf16[256,576]{0,1:T(8,128)(2,1)S(1)}, bf16[256,576]{0,1:T(8,128)(2,1)S(1)}, u32[]{:S(2)}, u32[]{:S(2)}) collective-permute-start(bf16[256,576]{0,1:T(8,128)(2,1)S(1)} %fusion.73), channel_id=1, source_target_pairs={{0,128},{128,0},{1,129},{129,1},{2,130},{130,2},{3,131},{131,3},{4... | collective-permute-start | bytes 884744 | tf_op jit(solution)/shard_map/ppermute | solution.py:124
  141.8 1.2 collective-permute-done.8
  143.0 3.8 %collective-permute-start.10 = (bf16[256,576]{0,1:T(8,128)(2,1)S(1)}, bf16[256,576]{0,1:T(8,128)(2,1)S(1)}, u32[]{:S(2)}, u32[]{:S(2)}) collective-permute-start(bf16[256,576]{0,1:T(8,128)(2,1)S(1)} %collective-permute-done.8), channel_id=1, source_target_pairs={{128,192},{160,224},{192,128},{224,160},{129,193},{161,225},{193,1... | collective-permute-start | bytes 884744 | tf_op jit(solution)/shard_map/ppermute | solution.py:17
  146.8 4.0 %collective-permute-start.11 = (bf16[256,576]{0,1:T(8,128)(2,1)S(1)}, bf16[256,576]{0,1:T(8,128)(2,1)S(1)}, u32[]{:S(2)}, u32[]{:S(2)}) collective-permute-start(bf16[256,576]{0,1:T(8,128)(2,1)S(1)} %collective-permute-done.8), channel_id=1, source_target_pairs={{128,160},{160,192},{192,224},{224,128},{129,161},{161,193},{193,2... | collective-permute-start | bytes 884744 | tf_op jit(solution)/shard_map/ppermute | solution.py:17
  150.8 2.5 collective-permute-start.9
  153.3 2.6 collective-permute-done.11
  155.9 2.4 collective-permute-done.9
  158.6 6.5 %conditional.3 = (bf16[256,2048]{1,0:T(8,128)(2,1)S(1)}) conditional(s32[]{:T(128)} %convert_element_type.100, (bf16[1,2304,2048]{2,1,0:T(8,128)(2,1)}, bf16[256,2304]{0,1:T(8,128)(2,1)S(1)}, f32[1,2048]{1,0:T(1,128)S(1)}, f32[256,2048]{1,0:T(8,128)S(1)}) %tuple.45, () %tuple.23), branch_computations={%region_3.4_spmd, %region_4.5_spmd} | conditional | flops 2418016256 | bytes 13770760 | solution.py:129
  158.8 6.3 %fusion.25 = bf16[256,2048]{1,0:T(8,128)(2,1)S(1)} fusion(f32[256,2048]{1,0:T(8,128)S(1)} %get-tuple-element.29, bf16[256,2304]{0,1:T(8,128)(2,1)S(1)} %get-tuple-element.45, bf16[1,2304,2048]{2,1,0:T(8,128)(2,1)} %get-tuple-element.27, f32[2048]{0:T(1024)S(1)} %bitcast.57), kind=kOutput, calls=%fused_computation.11 | convolution fusion | flops 2418016256 | bytes 13770752 | tf_op jit(solution)/shard_map/cond/branch_0_fun/dot_general | solution.py:91
  165.1 1.4 collective-permute-start.12
  166.5 2.2 collective-permute-done.12
  168.8 52.0 %all-gather.5.cloned.1.call-done = bf16[2048,2304]{0,1:T(8,128)(2,1)} async-done(((bf16[2048,72]{0,1:T(8,128)(2,1)}), bf16[2048,2304]{0,1:T(8,128)(2,1)}) %all-gather.5.cloned.1.call-update) | async-done | bytes 9437200 | tf_op jit(solution)/shard_map/all_gather | solution.py:108
  220.9 2.5 fusion.56
  223.4 1.3 collective-permute-start.16
  224.7 2.5 fusion.59
  227.1 1.3 collective-permute-start.17
  228.4 2.5 fusion.62
  231.0 1.4 collective-permute-start.18
  232.4 2.5 fusion.65
  234.9 1.3 collective-permute-start.19
  236.2 4.6 %collective-permute-start.13 = (bf16[256,576]{0,1:T(8,128)(2,1)S(1)}, bf16[256,576]{0,1:T(8,128)(2,1)S(1)}, u32[]{:S(2)}, u32[]{:S(2)}) collective-permute-start(bf16[256,576]{0,1:T(8,128)(2,1)S(1)} %fusion.56), channel_id=1, source_target_pairs={{128,192},{160,224},{192,128},{224,160},{129,193},{161,225},{193,1... | collective-permute-start | bytes 884744 | tf_op jit(solution)/shard_map/ppermute | solution.py:17
  240.8 2.2 collective-permute-start.14
  243.0 4.3 %collective-permute-start.15 = (bf16[256,576]{0,1:T(8,128)(2,1)S(1)}, bf16[256,576]{0,1:T(8,128)(2,1)S(1)}, u32[]{:S(2)}, u32[]{:S(2)}) collective-permute-start(bf16[256,576]{0,1:T(8,128)(2,1)S(1)} %fusion.62), channel_id=1, source_target_pairs={{128,224},{160,128},{192,160},{224,192},{129,225},{161,129},{193,1... | collective-permute-start | bytes 884744 | tf_op jit(solution)/shard_map/ppermute | solution.py:17
  247.3 0.9 fusion.72
  248.3 1.2 collective-permute-done.14
  249.5 1.5 collective-permute-done.15
  251.0 2.1 fusion.70
  (53 shorter events, 3.4 us)
Async XLA Ops:
  7.2 110.3 %all-gather.3.cloned.1.call-start = ((), (), s32[]{:S(2)}) async-start(), calls=%async_computation | async-start | bytes 9732096 | tf_op jit(solution)/shard_map/all_gather | solution.py:107
  7.2 4.7 %collective-permute-start.4 = (bf16[2048,72]{0,1:T(8,128)(2,1)}, bf16[2048,72]{0,1:T(8,128)(2,1)S(1)}, u32[]{:S(2)}, u32[]{:S(2)}) collective-permute-start(bf16[2048,72]{0,1:T(8,128)(2,1)} %bitcast.59), channel_id=1, source_target_pairs={{0,128},{128,0},{1,129},{129,1},{2,130},{130,2},{3,131},{131,3},{4... | collective-permute-start | bytes 884744 | tf_op jit(solution)/shard_map/ppermute | solution.py:104
  13.8 207.1 %all-gather.5.cloned.1.call-start = ((), (), s32[]{:S(2)}) async-start(), calls=%async_computation.1 | async-start | bytes 9732096 | tf_op jit(solution)/shard_map/all_gather | solution.py:108
  14.5 5.3 %collective-permute-start = (bf16[256,576]{0,1:T(8,128)(2,1)}, bf16[256,576]{0,1:T(8,128)(2,1)S(1)}, u32[]{:S(2)}, u32[]{:S(2)}) collective-permute-start(bf16[256,576]{0,1:T(8,128)(2,1)} %param.13), channel_id=1, source_target_pairs={{0,96},{32,0},{64,32},{96,64},{1,97},{33,1},{65,33},{97,65},{2,98}... | collective-permute-start | bytes 884744 | tf_op jit(solution)/shard_map/ppermute | solution.py:17
  15.2 4.6 %collective-permute-start.1 = (bf16[256,576]{0,1:T(8,128)(2,1)}, bf16[256,576]{0,1:T(8,128)(2,1)S(1)}, u32[]{:S(2)}, u32[]{:S(2)}) collective-permute-start(bf16[256,576]{0,1:T(8,128)(2,1)} %param.13), channel_id=1, source_target_pairs={{0,64},{32,96},{64,0},{96,32},{1,65},{33,97},{65,1},{97,33},{2,66}... | collective-permute-start | bytes 884744 | tf_op jit(solution)/shard_map/ppermute | solution.py:17
  15.9 3.9 %collective-permute-start.2 = (bf16[256,576]{0,1:T(8,128)(2,1)}, bf16[256,576]{0,1:T(8,128)(2,1)S(1)}, u32[]{:S(2)}, u32[]{:S(2)}) collective-permute-start(bf16[256,576]{0,1:T(8,128)(2,1)} %param.13), channel_id=1, source_target_pairs={{0,32},{32,64},{64,96},{96,0},{1,33},{33,65},{65,97},{97,1},{2,34}... | collective-permute-start | bytes 884744 | tf_op jit(solution)/shard_map/ppermute | solution.py:17
  18.9 1.0 copy-start
  19.9 0.7 copy-start.11
  20.7 21.3 %collective-permute-start.3 = (bf16[256,2048]{1,0:T(8,128)(2,1)S(1)}, bf16[256,2048]{1,0:T(8,128)(2,1)}, u32[]{:S(2)}, u32[]{:S(2)}) collective-permute-start(bf16[256,2048]{1,0:T(8,128)(2,1)S(1)} %get-tuple-element.56), channel_id=1, source_target_pairs={{0,128},{1,129},{2,130},{3,131},{4,132},{5,133},{6,134},{7,135},{8... | collective-permute-start | bytes 3145736 | tf_op jit(solution)/shard_map/ppermute | solution.py:119
  117.4 6.3 %copy-start.9 = (bf16[256,2048]{1,0:T(8,128)(2,1)S(1)}, bf16[256,2048]{1,0:T(8,128)(2,1)}, u32[]{:S(2)}) copy-start(bf16[256,2048]{1,0:T(8,128)(2,1)} %broadcast_select_fusion.1) | copy-start | bytes 3145732
  121.0 14.8 %collective-permute-start.5 = (bf16[256,576]{0,1:T(8,128)(2,1)}, bf16[256,576]{0,1:T(8,128)(2,1)S(1)}, u32[]{:S(2)}, u32[]{:S(2)}) collective-permute-start(bf16[256,576]{0,1:T(8,128)(2,1)} %fusion.44), channel_id=1, source_target_pairs={{0,64},{32,96},{64,0},{96,32},{1,65},{33,97},{65,1},{97,33},{2,66}... | collective-permute-start | bytes 884744 | tf_op jit(solution)/shard_map/ppermute | solution.py:13
  127.0 10.3 %collective-permute-start.6 = (bf16[256,576]{0,1:T(8,128)(2,1)}, bf16[256,576]{0,1:T(8,128)(2,1)S(1)}, u32[]{:S(2)}, u32[]{:S(2)}) collective-permute-start(bf16[256,576]{0,1:T(8,128)(2,1)} %fusion.47), channel_id=1, source_target_pairs={{0,32},{32,64},{64,96},{96,0},{1,33},{33,65},{65,97},{97,1},{2,34}... | collective-permute-start | bytes 884744 | tf_op jit(solution)/shard_map/ppermute | solution.py:13
  130.5 7.1 %copy-start.1 = (bf16[256,576]{0,1:T(8,128)(2,1)S(1)}, bf16[256,576]{0,1:T(8,128)(2,1)}, u32[]{:S(2)}) copy-start(bf16[256,576]{0,1:T(8,128)(2,1)} %param.15) | copy-start | bytes 884740
  130.5 7.1 %collective-permute-start.7 = (bf16[256,576]{0,1:T(8,128)(2,1)}, bf16[256,576]{0,1:T(8,128)(2,1)}, u32[]{:S(2)}, u32[]{:S(2)}) collective-permute-start(bf16[256,576]{0,1:T(8,128)(2,1)} %fusion.50), channel_id=1, source_target_pairs={{0,96},{32,0},{64,32},{96,64},{1,97},{33,1},{65,33},{97,65},{2,98}... | collective-permute-start | bytes 884744 | tf_op jit(solution)/shard_map/ppermute | solution.py:13
  132.9 4.7 %copy-start.10 = (bf16[1,256,576]{1,2,0:T(8,128)(2,1)S(1)}, bf16[1,256,576]{1,2,0:T(8,128)(2,1)}, u32[]{:S(2)}) copy-start(bf16[1,256,576]{1,2,0:T(8,128)(2,1)} %param.14) | copy-start | bytes 884740
  135.8 22.8 %copy-start.7 = (bf16[256,576]{0,1:T(8,128)(2,1)}, bf16[256,576]{0,1:T(8,128)(2,1)S(1)}, u32[]{:S(2)}) copy-start(bf16[256,576]{0,1:T(8,128)(2,1)S(1)} %fusion.53) | copy-start | bytes 884740
  135.8 22.7 %copy-start.3 = (bf16[256,576]{0,1:T(8,128)(2,1)}, bf16[256,576]{0,1:T(8,128)(2,1)S(1)}, u32[]{:S(2)}) copy-start(bf16[256,576]{0,1:T(8,128)(2,1)S(1)} %collective-permute-done.5) | copy-start | bytes 884740
  137.3 21.2 %copy-start.5 = (bf16[256,576]{0,1:T(8,128)(2,1)}, bf16[256,576]{0,1:T(8,128)(2,1)S(1)}, u32[]{:S(2)}) copy-start(bf16[256,576]{0,1:T(8,128)(2,1)S(1)} %collective-permute-done.6) | copy-start | bytes 884740
  138.9 4.1 %collective-permute-start.8 = (bf16[256,576]{0,1:T(8,128)(2,1)S(1)}, bf16[256,576]{0,1:T(8,128)(2,1)S(1)}, u32[]{:S(2)}, u32[]{:S(2)}) collective-permute-start(bf16[256,576]{0,1:T(8,128)(2,1)S(1)} %fusion.73), channel_id=1, source_target_pairs={{0,128},{128,0},{1,129},{129,1},{2,130},{130,2},{3,131},{131,3},{4... | collective-permute-start | bytes 884744 | tf_op jit(solution)/shard_map/ppermute | solution.py:124
  143.0 10.3 %collective-permute-start.10 = (bf16[256,576]{0,1:T(8,128)(2,1)S(1)}, bf16[256,576]{0,1:T(8,128)(2,1)S(1)}, u32[]{:S(2)}, u32[]{:S(2)}) collective-permute-start(bf16[256,576]{0,1:T(8,128)(2,1)S(1)} %collective-permute-done.8), channel_id=1, source_target_pairs={{128,192},{160,224},{192,128},{224,160},{129,193},{161,225},{193,1... | collective-permute-start | bytes 884744 | tf_op jit(solution)/shard_map/ppermute | solution.py:17
  146.8 9.1 %collective-permute-start.11 = (bf16[256,576]{0,1:T(8,128)(2,1)S(1)}, bf16[256,576]{0,1:T(8,128)(2,1)S(1)}, u32[]{:S(2)}, u32[]{:S(2)}) collective-permute-start(bf16[256,576]{0,1:T(8,128)(2,1)S(1)} %collective-permute-done.8), channel_id=1, source_target_pairs={{128,160},{160,192},{192,224},{224,128},{129,161},{161,193},{193,2... | collective-permute-start | bytes 884744 | tf_op jit(solution)/shard_map/ppermute | solution.py:17
  150.8 7.5 %collective-permute-start.9 = (bf16[256,576]{0,1:T(8,128)(2,1)S(1)}, bf16[256,576]{0,1:T(8,128)(2,1)S(1)}, u32[]{:S(2)}, u32[]{:S(2)}) collective-permute-start(bf16[256,576]{0,1:T(8,128)(2,1)S(1)} %collective-permute-done.8), channel_id=1, source_target_pairs={{128,224},{160,128},{192,160},{224,192},{129,225},{161,129},{193,1... | collective-permute-start | bytes 884744 | tf_op jit(solution)/shard_map/ppermute | solution.py:17
  165.1 3.6 %collective-permute-start.12 = (bf16[256,2048]{1,0:T(8,128)(2,1)S(1)}, bf16[256,2048]{1,0:T(8,128)(2,1)S(1)}, u32[]{:S(2)}, u32[]{:S(2)}) collective-permute-start(bf16[256,2048]{1,0:T(8,128)(2,1)S(1)} %get-tuple-element.57), channel_id=1, source_target_pairs={{128,0},{129,1},{130,2},{131,3},{132,4},{133,5},{134,6},{135,7},{1... | collective-permute-start | bytes 3145736 | tf_op jit(solution)/shard_map/ppermute | solution.py:135
  223.4 17.4 %collective-permute-start.16 = (bf16[256,576]{0,1:T(8,128)(2,1)S(1)}, bf16[256,576]{0,1:T(8,128)(2,1)S(1)}, u32[]{:S(2)}, u32[]{:S(2)}) collective-permute-start(bf16[256,576]{0,1:T(8,128)(2,1)S(1)} %fusion.56), channel_id=1, source_target_pairs={{0,192},{32,224},{64,128},{96,160},{1,193},{33,225},{65,129},{97,1... | collective-permute-start | bytes 884744 | tf_op jit(solution)/shard_map/ppermute | solution.py:67
  227.1 15.9 %collective-permute-start.17 = (bf16[256,576]{0,1:T(8,128)(2,1)S(1)}, bf16[256,576]{0,1:T(8,128)(2,1)S(1)}, u32[]{:S(2)}, u32[]{:S(2)}) collective-permute-start(bf16[256,576]{0,1:T(8,128)(2,1)S(1)} %fusion.59), channel_id=1, source_target_pairs={{0,160},{32,192},{64,224},{96,128},{1,161},{33,193},{65,225},{97,1... | collective-permute-start | bytes 884744 | tf_op jit(solution)/shard_map/ppermute | solution.py:67
  230.9 20.0 %copy-start.2 = (bf16[256,576]{0,1:T(8,128)(2,1)S(1)}, bf16[256,576]{0,1:T(8,128)(2,1)}, u32[]{:S(2)}) copy-start(bf16[256,576]{0,1:T(8,128)(2,1)} %param.15) | copy-start | bytes 884740
  230.9 20.0 %copy-start.4 = (bf16[256,576]{0,1:T(8,128)(2,1)S(1)}, bf16[256,576]{0,1:T(8,128)(2,1)}, u32[]{:S(2)}) copy-start(bf16[256,576]{0,1:T(8,128)(2,1)} %copy-done.3) | copy-start | bytes 884740
  230.9 20.0 %copy-start.6 = (bf16[256,576]{0,1:T(8,128)(2,1)S(1)}, bf16[256,576]{0,1:T(8,128)(2,1)}, u32[]{:S(2)}) copy-start(bf16[256,576]{0,1:T(8,128)(2,1)} %copy-done.5) | copy-start | bytes 884740
  231.0 20.0 %copy-start.8 = (bf16[256,576]{0,1:T(8,128)(2,1)S(1)}, bf16[256,576]{0,1:T(8,128)(2,1)}, u32[]{:S(2)}) copy-start(bf16[256,576]{0,1:T(8,128)(2,1)} %copy-done.7) | copy-start | bytes 884740
  231.0 16.4 %collective-permute-start.18 = (bf16[256,576]{0,1:T(8,128)(2,1)S(1)}, bf16[256,576]{0,1:T(8,128)(2,1)S(1)}, u32[]{:S(2)}, u32[]{:S(2)}) collective-permute-start(bf16[256,576]{0,1:T(8,128)(2,1)S(1)} %fusion.62), channel_id=1, source_target_pairs={{0,224},{32,128},{64,160},{96,192},{1,225},{33,129},{65,161},{97,1... | collective-permute-start | bytes 884744 | tf_op jit(solution)/shard_map/ppermute | solution.py:67
  234.9 12.5 %collective-permute-start.19 = (bf16[256,576]{0,1:T(8,128)(2,1)S(1)}, bf16[256,576]{0,1:T(8,128)(2,1)S(1)}, u32[]{:S(2)}, u32[]{:S(2)}) collective-permute-start(bf16[256,576]{0,1:T(8,128)(2,1)S(1)} %fusion.65), channel_id=1, source_target_pairs={{0,128},{32,160},{64,192},{96,224},{1,129},{33,161},{65,193},{97,2... | collective-permute-start | bytes 884744 | tf_op jit(solution)/shard_map/ppermute | solution.py:67
  236.2 12.1 %collective-permute-start.13 = (bf16[256,576]{0,1:T(8,128)(2,1)S(1)}, bf16[256,576]{0,1:T(8,128)(2,1)S(1)}, u32[]{:S(2)}, u32[]{:S(2)}) collective-permute-start(bf16[256,576]{0,1:T(8,128)(2,1)S(1)} %fusion.56), channel_id=1, source_target_pairs={{128,192},{160,224},{192,128},{224,160},{129,193},{161,225},{193,1... | collective-permute-start | bytes 884744 | tf_op jit(solution)/shard_map/ppermute | solution.py:17
  240.8 8.7 %collective-permute-start.14 = (bf16[256,576]{0,1:T(8,128)(2,1)S(1)}, bf16[256,576]{0,1:T(8,128)(2,1)S(1)}, u32[]{:S(2)}, u32[]{:S(2)}) collective-permute-start(bf16[256,576]{0,1:T(8,128)(2,1)S(1)} %fusion.59), channel_id=1, source_target_pairs={{128,160},{160,192},{192,224},{224,128},{129,161},{161,193},{193,2... | collective-permute-start | bytes 884744 | tf_op jit(solution)/shard_map/ppermute | solution.py:17
  243.0 7.9 %collective-permute-start.15 = (bf16[256,576]{0,1:T(8,128)(2,1)S(1)}, bf16[256,576]{0,1:T(8,128)(2,1)S(1)}, u32[]{:S(2)}, u32[]{:S(2)}) collective-permute-start(bf16[256,576]{0,1:T(8,128)(2,1)S(1)} %fusion.62), channel_id=1, source_target_pairs={{128,224},{160,128},{192,160},{224,192},{129,225},{161,129},{193,1... | collective-permute-start | bytes 884744 | tf_op jit(solution)/shard_map/ppermute | solution.py:17
Sparse Core Ops, SparseCore 0:
  13.9 103.4 all-gather.2
  120.6 100.2 all-gather.4

commit v11 on v5

--- a/solution.py
+++ b/solution.py
@@ -39,6 +39,24 @@
         piece = lax.dynamic_slice_in_dim(terms, target * cols, cols, terms.ndim - 1)
         total = total + within_layer(piece, section, k, n_feat).astype(jnp.float32)
     return total
+
+
+def decode_scatter(features, decoder, feat_index, n_feat):
+    cols = decoder.shape[1] // n_feat
+    total = None
+    anchor = None
+    for k in sorted(range(n_feat), key=lambda shift: (-min(shift, n_feat - shift), shift)):
+        target = (feat_index + k) % n_feat
+        chunk = lax.dynamic_slice_in_dim(decoder, target * cols, cols, 1)
+        piece = jnp.dot(features, chunk, preferred_element_type=jnp.float32).astype(jnp.bfloat16)
+        anchor = piece[0, 0] if anchor is None else anchor + piece[0, 0]
+        if k:
+            piece = within_layer(piece, None, k, n_feat)
+        else:
+            piece = lax.optimization_barrier(piece)
+        piece = piece.astype(jnp.float32)
+        total = piece if total is None else total + piece
+    return total, anchor
 
 
 def feature_mask(block_list, block_count, feat_index, blocks_dev):
@@ -83,16 +101,17 @@
         )
 
     features_first = encoded(feat_gather(resid_in, 0, feat_index, n_feat), 0)
-    own_first = feat_reduce_scatter(decode(features_first, own_full), 0, feat_index, n_feat)
+    own_first, _ = decode_scatter(features_first, own_full, feat_index, n_feat)
     recon_first = own_first + carry_in.astype(jnp.float32)
     residual_next = (resid_in.astype(jnp.float32) + attention + recon_first).astype(jnp.bfloat16)
     residual_next = lax.ppermute(residual_next, "layer", [(0, 1)])
 
     features_second = encoded(feat_gather(residual_next, 1, feat_index, n_feat), 1)
-    own_second = feat_reduce_scatter(decode(features_second, own_full), 1, feat_index, n_feat)
+    own_second, own_piece = decode_scatter(features_second, own_full, feat_index, n_feat)
 
     features = jnp.where(first_core, features_first, features_second)
-    next_part = feat_reduce_scatter(decode(features, next_full), None, feat_index, n_feat)
+    features = features + (own_piece * 0).astype(features.dtype)
+    next_part, _ = decode_scatter(features, next_full, feat_index, n_feat)
     outgoing_now = next_part.astype(jnp.bfloat16)
     incoming = lax.ppermute(outgoing_now, "layer", [(0, 1)])
     recon_second = own_second + incoming.astype(jnp.float32)

time: 265 us -> 262 us (0.989); the launches traced: 265 us -> 259 us
  matrix products: 27.2 us -> 42 us
  local copies, waits for them, and re-layouts: 17.8 us -> 5.19 us
  waiting for transfers between devices: 167 us -> 158 us
    dot_general x3 -> x12, matrix products: 19.7 us -> 34.7 us  [decode_scatter(): jnp.dot(features, chunk, preferred_element_type=jnp.float32)]
    ppermute x3 -> x9, waiting for transfers between devices: 0.01 us -> 12.1 us  [within_layer(): lax.ppermute(shard, 'feat', [(i, (i + shift) % n_feat) for i in range(n_f...]
    all_gather x1, waiting for transfers between devices: 44 us -> 32 us  [shards(): next_full = lax.all_gather(dec_next[0], TOK, axis=1, tiled=True)]
    ppermute x1, waiting for transfers between devices: 15.9 us -> 4 us  [shards(): residual_next = lax.ppermute(residual_next, 'layer', [(0, 1)])]
    ppermute x12 -> x6, starting transfers between devices: 22.6 us -> 11.8 us  [within_layer(): return lax.ppermute(shard, GROUP, pairs)]
    ppermute x3 -> x9, starting transfers between devices: 4.85 us -> 13.8 us  [within_layer(): lax.ppermute(shard, 'feat', [(i, (i + shift) % n_feat) for i in range(n_f...]
    all_gather x1, waiting for transfers between devices: 93.8 us -> 101 us  [shards(): own_full = lax.all_gather(dec_own[0], TOK, axis=1, tiled=True)]
    unnamed x30 -> x27, local copies, waits for them, and re-layouts: 7.59 us -> 1.41 us
  transfers between devices with their start and end apart: 19 -> 19, of which waited for: 8 -> 11; matrix products, arithmetic and copies ran while one was open for 15% -> 19% of each run, Pallas kernels for 0% -> 0%
where the time goes in v11:
time: 262 us; the launch traced here: 259 us
  waiting for transfers between devices  158 us (60%)
  matrix products  42 us (16%)
  starting transfers between devices  28.2 us (11%)
  between operations  17 us (6%)
  other arithmetic  8.1 us (3%)
  local copies, waits for them, and re-layouts  5.19 us (2%)
    all_gather x1, waiting for transfers between devices, shards(): own_full = lax.all_gather(dec_own[0], TOK, axis=1, tiled=True)  101 us
    dot_general x12, matrix products, decode_scatter(): jnp.dot(features, chunk, preferred_element_type=jnp.float32)  34.7 us
    all_gather x1, waiting for transfers between devices, shards(): next_full = lax.all_gather(dec_next[0], TOK, axis=1, tiled=True)  32 us
    ppermute x9, starting transfers between devices, within_layer(): lax.ppermute(shard, 'feat', [(i, (i + shift) % n_feat) for i in range(n_f...  13.8 us
    ppermute x9, waiting for transfers between devices, within_layer(): lax.ppermute(shard, 'feat', [(i, (i + shift) % n_feat) for i in range(n_f...  12.1 us
    ppermute x6, starting transfers between devices, within_layer(): return lax.ppermute(shard, GROUP, pairs)  11.8 us
    ppermute x6, waiting for transfers between devices, within_layer(): return lax.ppermute(shard, GROUP, pairs)  7.82 us
    dot_general x1, matrix products, encode(): jnp.dot(gathered, enc_weight[0], preferred_element_type=jnp.float32)  7.3 us
  transfers between devices with their start and end apart: 19, of which 11 were waited for; matrix products, arithmetic and copies ran while one was open for 19% of the time, Pallas kernels for 0%

profile of v11, /device:TPU:1, one launch (start us, length us, event | category | flops | bytes accessed | tf_op | source)
XLA Modules:
  0.0 258.9 jit_solution(3915335885828446391)
XLA Ops:
  7.2 0.7 all-gather.5.cloned.1.call-update
  7.9 0.7 all-gather.7.cloned.1.call-update
  8.6 0.7 collective-permute-start
  9.3 0.7 collective-permute-start.1
  10.0 0.7 collective-permute-start.2
  10.9 0.7 iota_compare_fusion
  11.6 0.9 and_reduce_fusion
  13.1 0.9 copy.19
  14.8 1.1 conditional.2
  14.8 1.1 broadcast.25
  15.9 100.9 %all-gather.5.cloned.1.call-done = bf16[1,2048,2304]{1,2,0:T(8,128)(2,1)} async-done(((bf16[1,2048,72]{1,2,0:T(8,128)(2,1)}), bf16[1,2048,2304]{1,2,0:T(8,128)(2,1)}) %all-gather.5.cloned.1.call-update) | async-done | bytes 9437200 | tf_op jit(solution)/shard_map/all_gather | solution.py:90
  116.8 3.5 %fusion.64 = bf16[256,576]{0,1:T(8,128)(2,1)} fusion(bf16[256,2048]{1,0:T(8,128)(2,1)} %get-tuple-element.54, bf16[1,2048,2304]{1,2,0:T(8,128)(2,1)} %all-gather.5.cloned.1.call-done, s32[]{:T(128)S(6)} %select_n.341), kind=kOutput, calls=%fused_computation.49 | convolution fusion | flops 604127232 | bytes 3702788 | tf_op jit(solution)/shard_map/dot_general | solution.py:51
  120.4 2.7 %collective-permute-start.3 = (bf16[256,576]{0,1:T(8,128)(2,1)}, bf16[256,576]{0,1:T(8,128)(2,1)S(1)}, u32[]{:S(2)}, u32[]{:S(2)}) collective-permute-start(bf16[256,576]{0,1:T(8,128)(2,1)} %fusion.64), channel_id=1, source_target_pairs={{0,64},{32,96},{64,0},{96,32},{1,65},{33,97},{65,1},{97,33},{2,66}... | collective-permute-start | bytes 884744 | tf_op jit(solution)/shard_map/ppermute | solution.py:14
  123.1 3.5 %fusion.70 = bf16[256,576]{0,1:T(8,128)(2,1)} fusion(bf16[256,2048]{1,0:T(8,128)(2,1)} %get-tuple-element.54, bf16[1,2048,2304]{1,2,0:T(8,128)(2,1)} %all-gather.5.cloned.1.call-done, s32[]{:T(128)S(6)} %select_n.343), kind=kOutput, calls=%fused_computation.51 | convolution fusion | flops 604127232 | bytes 3702788 | tf_op jit(solution)/shard_map/dot_general | solution.py:51
  126.9 3.5 %fusion.76 = bf16[256,576]{0,1:T(8,128)(2,1)} fusion(bf16[256,2048]{1,0:T(8,128)(2,1)} %get-tuple-element.54, bf16[1,2048,2304]{1,2,0:T(8,128)(2,1)} %all-gather.5.cloned.1.call-done, s32[]{:T(128)S(6)} %select_n.345), kind=kOutput, calls=%fused_computation.53 | convolution fusion | flops 604127232 | bytes 3702788 | tf_op jit(solution)/shard_map/dot_general | solution.py:51
  130.4 2.4 collective-permute-start.5
  132.8 2.8 %fusion.82 = bf16[256,576]{0,1:T(8,128)(2,1)S(1)} fusion(bf16[256,2048]{1,0:T(8,128)(2,1)} %get-tuple-element.54, bf16[1,2048,2304]{1,2,0:T(8,128)(2,1)} %all-gather.5.cloned.1.call-done, s32[]{:T(128)S(6)} %select_n.346), kind=kOutput, calls=%fused_computation.55 | convolution fusion | flops 604127232 | bytes 3702788 | tf_op jit(solution)/shard_map/dot_general | solution.py:51
  135.6 0.7 collective-permute-done.4
  136.4 1.0 collective-permute-done.5
  137.4 1.3 fusion.101
  138.6 1.3 collective-permute-start.6
  139.9 4.0 %collective-permute-done.6 = bf16[256,576]{0,1:T(8,128)(2,1)S(1)} collective-permute-done((bf16[256,576]{0,1:T(8,128)(2,1)S(1)}, bf16[256,576]{0,1:T(8,128)(2,1)S(1)}, u32[]{:S(2)}, u32[]{:S(2)}) %collective-permute-start.6) | collective-permute-done | bytes 294944 | tf_op jit(solution)/shard_map/ppermute | solution.py:107
  143.9 5.3 %collective-permute-start.7 = (bf16[256,576]{0,1:T(8,128)(2,1)S(1)}, bf16[256,576]{0,1:T(8,128)(2,1)S(1)}, u32[]{:S(2)}, u32[]{:S(2)}) collective-permute-start(bf16[256,576]{0,1:T(8,128)(2,1)S(1)} %collective-permute-done.6), channel_id=1, source_target_pairs={{128,224},{160,128},{192,160},{224,192},{129,225},{161,129},{193,1... | collective-permute-start | bytes 884744 | tf_op jit(solution)/shard_map/ppermute | solution.py:18
  149.3 1.9 collective-permute-start.8
  151.2 2.5 collective-permute-start.9
  153.7 2.4 collective-permute-done.7
  156.1 2.4 collective-permute-done.8
  158.4 3.1 %collective-permute-done.9 = bf16[256,576]{0,1:T(8,128)(2,1)} collective-permute-done((bf16[256,576]{0,1:T(8,128)(2,1)S(1)}, bf16[256,576]{0,1:T(8,128)(2,1)}, u32[]{:S(2)}, u32[]{:S(2)}) %collective-permute-start.9) | collective-permute-done | bytes 294944 | tf_op jit(solution)/shard_map/ppermute | solution.py:18
  161.6 1.2 select_select_fusion.3
  162.9 7.5 %conditional.3 = (bf16[256,2048]{1,0:T(8,128)(2,1)}) conditional(s32[]{:T(128)} %convert_element_type.122, () %tuple.22, (bf16[1,2304,2048]{2,1,0:T(8,128)(2,1)}, bf16[256,2304]{0,1:T(8,128)(2,1)S(1)}, f32[1,2048]{1,0:T(1,128)S(1)}, f32[256,2048]{1,0:T(8,128)S(1)}) %tuple.44), branch_computations={%region_3.4_spmd, %region_4.5_spmd} | conditional | flops 2418016256 | bytes 13770760 | solution.py:96
  163.1 7.3 %fusion.25 = bf16[256,2048]{1,0:T(8,128)(2,1)} fusion(f32[256,2048]{1,0:T(8,128)S(1)} %get-tuple-element.29, bf16[256,2304]{0,1:T(8,128)(2,1)S(1)} %get-tuple-element.45, bf16[1,2304,2048]{2,1,0:T(8,128)(2,1)} %get-tuple-element.27, f32[2048]{0:T(1024)S(1)} %bitcast.114), kind=kOutput, calls=%fused_computation.11 | convolution fusion | flops 2418016256 | bytes 13770752 | tf_op jit(solution)/shard_map/cond/branch_1_fun/dot_general | solution.py:73
  170.4 2.8 %fusion.73 = bf16[256,576]{0,1:T(8,128)(2,1)S(1)} fusion(bf16[256,2048]{1,0:T(8,128)(2,1)} %get-tuple-element.55, bf16[1,2048,2304]{1,2,0:T(8,128)(2,1)} %all-gather.5.cloned.1.call-done, s32[]{:T(128)S(6)} %select_n.343), kind=kOutput, calls=%fused_computation.52 | convolution fusion | flops 604127232 | bytes 3702788 | tf_op jit(solution)/shard_map/dot_general | solution.py:51
  173.7 2.8 %fusion.67 = bf16[256,576]{0,1:T(8,128)(2,1)S(1)} fusion(bf16[256,2048]{1,0:T(8,128)(2,1)} %get-tuple-element.55, bf16[1,2048,2304]{1,2,0:T(8,128)(2,1)} %all-gather.5.cloned.1.call-done, s32[]{:T(128)S(6)} %select_n.341), kind=kOutput, calls=%fused_computation.50 | convolution fusion | flops 604127232 | bytes 3702788 | tf_op jit(solution)/shard_map/dot_general | solution.py:51
  177.1 2.9 %fusion.79 = bf16[256,576]{0,1:T(8,128)(2,1)S(1)} fusion(bf16[256,2048]{1,0:T(8,128)(2,1)} %get-tuple-element.55, bf16[1,2048,2304]{1,2,0:T(8,128)(2,1)} %all-gather.5.cloned.1.call-done, s32[]{:T(128)S(6)} %select_n.345), kind=kOutput, calls=%fused_computation.54 | convolution fusion | flops 604127232 | bytes 3702788 | tf_op jit(solution)/shard_map/dot_general | solution.py:51
  180.5 2.9 %fusion.85 = bf16[256,576]{0,1:T(8,128)(2,1)S(1)} fusion(bf16[256,2048]{1,0:T(8,128)(2,1)} %get-tuple-element.55, bf16[1,2048,2304]{1,2,0:T(8,128)(2,1)} %all-gather.5.cloned.1.call-done, s32[]{:T(128)S(6)} %select_n.346), kind=kOutput, calls=%fused_computation.56 | convolution fusion | flops 604127232 | bytes 3702788 | tf_op jit(solution)/shard_map/dot_general | solution.py:51
  186.4 1.4 select_add_fusion
  187.7 32.0 %all-gather.7.cloned.1.call-done = bf16[1,2048,2304]{1,2,0:T(8,128)(2,1)} async-done(((bf16[1,2048,72]{1,2,0:T(8,128)(2,1)}), bf16[1,2048,2304]{1,2,0:T(8,128)(2,1)}) %all-gather.7.cloned.1.call-update) | async-done | bytes 9437200 | tf_op jit(solution)/shard_map/all_gather | solution.py:91
  219.7 2.5 fusion.88
  222.2 2.8 %collective-permute-start.13 = (bf16[256,576]{0,1:T(8,128)(2,1)S(1)}, bf16[256,576]{0,1:T(8,128)(2,1)S(1)}, u32[]{:S(2)}, u32[]{:S(2)}) collective-permute-start(bf16[256,576]{0,1:T(8,128)(2,1)S(1)} %fusion.88), channel_id=1, source_target_pairs={{0,64},{32,96},{64,0},{96,32},{1,65},{33,97},{65,1},{97,33},{2,66}... | collective-permute-start | bytes 884744 | tf_op jit(solution)/shard_map/ppermute | solution.py:14
  225.0 2.5 fusion.91
  227.8 2.5 fusion.94
  230.4 2.5 collective-permute-start.15
  232.8 2.7 %collective-permute-start.12 = (bf16[256,576]{0,1:T(8,128)(2,1)S(1)}, bf16[256,576]{0,1:T(8,128)(2,1)S(1)}, u32[]{:S(2)}, u32[]{:S(2)}) collective-permute-start(bf16[256,576]{0,1:T(8,128)(2,1)S(1)} %fusion.79), channel_id=1, source_target_pairs={{0,96},{32,0},{64,32},{96,64},{1,97},{33,1},{65,33},{97,65},{2,98}... | collective-permute-start | bytes 884744 | tf_op jit(solution)/shard_map/ppermute | solution.py:14
  235.5 2.5 fusion.97
  238.5 1.3 collective-permute-start.16
  239.8 5.9 %collective-permute-done.11 = bf16[256,576]{0,1:T(8,128)(2,1)S(1)} collective-permute-done((bf16[256,576]{0,1:T(8,128)(2,1)S(1)}, bf16[256,576]{0,1:T(8,128)(2,1)S(1)}, u32[]{:S(2)}, u32[]{:S(2)}) %collective-permute-start.11) | collective-permute-done | bytes 294944 | tf_op jit(solution)/shard_map/ppermute | solution.py:14
  245.7 4.3 %collective-permute-done.10 = bf16[256,576]{0,1:T(8,128)(2,1)S(1)} collective-permute-done((bf16[256,576]{0,1:T(8,128)(2,1)S(1)}, bf16[256,576]{0,1:T(8,128)(2,1)S(1)}, u32[]{:S(2)}, u32[]{:S(2)}) %collective-permute-start.10) | collective-permute-done | bytes 294944 | tf_op jit(solution)/shard_map/ppermute | solution.py:14
  250.0 2.1 fusion.102
  (55 shorter events, 4.9 us)
Async XLA Ops:
  7.2 109.7 %all-gather.5.cloned.1.call-start = ((), (), s32[]{:S(2)}) async-start(), calls=%async_computation | async-start | bytes 9732096 | tf_op jit(solution)/shard_map/all_gather | solution.py:90
  7.9 211.8 %all-gather.7.cloned.1.call-start = ((), (), s32[]{:S(2)}) async-start(), calls=%async_computation.1 | async-start | bytes 9732096 | tf_op jit(solution)/shard_map/all_gather | solution.py:91
  8.6 5.3 %collective-permute-start = (bf16[256,576]{0,1:T(8,128)(2,1)}, bf16[256,576]{0,1:T(8,128)(2,1)S(1)}, u32[]{:S(2)}, u32[]{:S(2)}) collective-permute-start(bf16[256,576]{0,1:T(8,128)(2,1)} %param.13), channel_id=1, source_target_pairs={{0,96},{32,0},{64,32},{96,64},{1,97},{33,1},{65,33},{97,65},{2,98}... | collective-permute-start | bytes 884744 | tf_op jit(solution)/shard_map/ppermute | solution.py:18
  9.3 4.7 %collective-permute-start.1 = (bf16[256,576]{0,1:T(8,128)(2,1)}, bf16[256,576]{0,1:T(8,128)(2,1)S(1)}, u32[]{:S(2)}, u32[]{:S(2)}) collective-permute-start(bf16[256,576]{0,1:T(8,128)(2,1)} %param.13), channel_id=1, source_target_pairs={{0,64},{32,96},{64,0},{96,32},{1,65},{33,97},{65,1},{97,33},{2,66}... | collective-permute-start | bytes 884744 | tf_op jit(solution)/shard_map/ppermute | solution.py:18
  10.0 4.0 %collective-permute-start.2 = (bf16[256,576]{0,1:T(8,128)(2,1)}, bf16[256,576]{0,1:T(8,128)(2,1)S(1)}, u32[]{:S(2)}, u32[]{:S(2)}) collective-permute-start(bf16[256,576]{0,1:T(8,128)(2,1)} %param.13), channel_id=1, source_target_pairs={{0,32},{32,64},{64,96},{96,0},{1,33},{33,65},{65,97},{97,1},{2,34}... | collective-permute-start | bytes 884744 | tf_op jit(solution)/shard_map/ppermute | solution.py:18
  13.1 1.0 copy-start
  14.1 0.7 copy-start.12
  120.4 15.3 %collective-permute-start.3 = (bf16[256,576]{0,1:T(8,128)(2,1)}, bf16[256,576]{0,1:T(8,128)(2,1)S(1)}, u32[]{:S(2)}, u32[]{:S(2)}) collective-permute-start(bf16[256,576]{0,1:T(8,128)(2,1)} %fusion.64), channel_id=1, source_target_pairs={{0,64},{32,96},{64,0},{96,32},{1,65},{33,97},{65,1},{97,33},{2,66}... | collective-permute-start | bytes 884744 | tf_op jit(solution)/shard_map/ppermute | solution.py:14
  126.6 9.8 %collective-permute-start.4 = (bf16[256,576]{0,1:T(8,128)(2,1)}, bf16[256,576]{0,1:T(8,128)(2,1)S(1)}, u32[]{:S(2)}, u32[]{:S(2)}) collective-permute-start(bf16[256,576]{0,1:T(8,128)(2,1)} %fusion.70), channel_id=1, source_target_pairs={{0,32},{32,64},{64,96},{96,0},{1,33},{33,65},{65,97},{97,1},{2,34}... | collective-permute-start | bytes 884744 | tf_op jit(solution)/shard_map/ppermute | solution.py:14
  130.4 7.0 %copy-start.1 = (bf16[256,576]{0,1:T(8,128)(2,1)S(1)}, bf16[256,576]{0,1:T(8,128)(2,1)}, u32[]{:S(2)}) copy-start(bf16[256,576]{0,1:T(8,128)(2,1)} %param.13) | copy-start | bytes 884740
  130.4 7.0 %copy-start.2 = (bf16[256,576]{0,1:T(8,128)(2,1)S(1)}, bf16[256,576]{0,1:T(8,128)(2,1)}, u32[]{:S(2)}) copy-start(bf16[256,576]{0,1:T(8,128)(2,1)} %param.15) | copy-start | bytes 884740
  130.4 7.0 %collective-permute-start.5 = (bf16[256,576]{0,1:T(8,128)(2,1)}, bf16[256,576]{0,1:T(8,128)(2,1)}, u32[]{:S(2)}, u32[]{:S(2)}) collective-permute-start(bf16[256,576]{0,1:T(8,128)(2,1)} %fusion.76), channel_id=1, source_target_pairs={{0,96},{32,0},{64,32},{96,64},{1,97},{33,1},{65,33},{97,65},{2,98}... | collective-permute-start | bytes 884744 | tf_op jit(solution)/shard_map/ppermute | solution.py:14
  132.8 4.6 %copy-start.10 = (bf16[1,256,576]{1,2,0:T(8,128)(2,1)S(1)}, bf16[1,256,576]{1,2,0:T(8,128)(2,1)}, u32[]{:S(2)}) copy-start(bf16[1,256,576]{1,2,0:T(8,128)(2,1)} %param.14) | copy-start | bytes 884740
  135.6 3.0 %copy-start.8 = (bf16[256,576]{0,1:T(8,128)(2,1)}, bf16[256,576]{0,1:T(8,128)(2,1)S(1)}, u32[]{:S(2)}) copy-start(bf16[256,576]{0,1:T(8,128)(2,1)S(1)} %fusion.82) | copy-start | bytes 884740
  135.6 27.1 %copy-start.4 = (bf16[256,576]{0,1:T(8,128)(2,1)}, bf16[256,576]{0,1:T(8,128)(2,1)S(1)}, u32[]{:S(2)}) copy-start(bf16[256,576]{0,1:T(8,128)(2,1)S(1)} %collective-permute-done.3) | copy-start | bytes 884740
  136.4 26.4 %copy-start.6 = (bf16[256,576]{0,1:T(8,128)(2,1)}, bf16[256,576]{0,1:T(8,128)(2,1)S(1)}, u32[]{:S(2)}) copy-start(bf16[256,576]{0,1:T(8,128)(2,1)S(1)} %collective-permute-done.4) | copy-start | bytes 884740
  138.6 5.3 %collective-permute-start.6 = (bf16[256,576]{0,1:T(8,128)(2,1)S(1)}, bf16[256,576]{0,1:T(8,128)(2,1)S(1)}, u32[]{:S(2)}, u32[]{:S(2)}) collective-permute-start(bf16[256,576]{0,1:T(8,128)(2,1)S(1)} %fusion.101), channel_id=1, source_target_pairs={{0,128},{1,129},{2,130},{3,131},{4,132},{5,133},{6,134},{7,135},{8... | collective-permute-start | bytes 884744 | tf_op jit(solution)/shard_map/ppermute | solution.py:107
  143.9 12.1 %collective-permute-start.7 = (bf16[256,576]{0,1:T(8,128)(2,1)S(1)}, bf16[256,576]{0,1:T(8,128)(2,1)S(1)}, u32[]{:S(2)}, u32[]{:S(2)}) collective-permute-start(bf16[256,576]{0,1:T(8,128)(2,1)S(1)} %collective-permute-done.6), channel_id=1, source_target_pairs={{128,224},{160,128},{192,160},{224,192},{129,225},{161,129},{193,1... | collective-permute-start | bytes 884744 | tf_op jit(solution)/shard_map/ppermute | solution.py:18
  149.3 9.2 %collective-permute-start.8 = (bf16[256,576]{0,1:T(8,128)(2,1)S(1)}, bf16[256,576]{0,1:T(8,128)(2,1)}, u32[]{:S(2)}, u32[]{:S(2)}) collective-permute-start(bf16[256,576]{0,1:T(8,128)(2,1)S(1)} %collective-permute-done.6), channel_id=1, source_target_pairs={{128,192},{160,224},{192,128},{224,160},{129,193},{161,225},{193,1... | collective-permute-start | bytes 884744 | tf_op jit(solution)/shard_map/ppermute | solution.py:18
  151.2 10.3 %collective-permute-start.9 = (bf16[256,576]{0,1:T(8,128)(2,1)S(1)}, bf16[256,576]{0,1:T(8,128)(2,1)}, u32[]{:S(2)}, u32[]{:S(2)}) collective-permute-start(bf16[256,576]{0,1:T(8,128)(2,1)S(1)} %collective-permute-done.6), channel_id=1, source_target_pairs={{128,160},{160,192},{192,224},{224,128},{129,161},{161,193},{193,2... | collective-permute-start | bytes 884744 | tf_op jit(solution)/shard_map/ppermute | solution.py:18
  222.2 15.8 %collective-permute-start.13 = (bf16[256,576]{0,1:T(8,128)(2,1)S(1)}, bf16[256,576]{0,1:T(8,128)(2,1)S(1)}, u32[]{:S(2)}, u32[]{:S(2)}) collective-permute-start(bf16[256,576]{0,1:T(8,128)(2,1)S(1)} %fusion.88), channel_id=1, source_target_pairs={{0,64},{32,96},{64,0},{96,32},{1,65},{33,97},{65,1},{97,33},{2,66}... | collective-permute-start | bytes 884744 | tf_op jit(solution)/shard_map/ppermute | solution.py:14
  227.5 10.8 %collective-permute-start.14 = (bf16[256,576]{0,1:T(8,128)(2,1)S(1)}, bf16[256,576]{0,1:T(8,128)(2,1)S(1)}, u32[]{:S(2)}, u32[]{:S(2)}) collective-permute-start(bf16[256,576]{0,1:T(8,128)(2,1)S(1)} %fusion.91), channel_id=1, source_target_pairs={{0,32},{32,64},{64,96},{96,0},{1,33},{33,65},{65,97},{97,1},{2,34}... | collective-permute-start | bytes 884744 | tf_op jit(solution)/shard_map/ppermute | solution.py:14
  230.3 19.7 %copy-start.3 = (bf16[256,576]{0,1:T(8,128)(2,1)S(1)}, bf16[256,576]{0,1:T(8,128)(2,1)}, u32[]{:S(2)}) copy-start(bf16[256,576]{0,1:T(8,128)(2,1)} %param.15) | copy-start | bytes 884740
  230.3 19.6 %copy-start.5 = (bf16[256,576]{0,1:T(8,128)(2,1)S(1)}, bf16[256,576]{0,1:T(8,128)(2,1)}, u32[]{:S(2)}) copy-start(bf16[256,576]{0,1:T(8,128)(2,1)} %copy-done.4) | copy-start | bytes 884740
  230.3 19.6 %copy-start.7 = (bf16[256,576]{0,1:T(8,128)(2,1)S(1)}, bf16[256,576]{0,1:T(8,128)(2,1)}, u32[]{:S(2)}) copy-start(bf16[256,576]{0,1:T(8,128)(2,1)} %copy-done.6) | copy-start | bytes 884740
  230.3 19.6 %copy-start.9 = (bf16[256,576]{0,1:T(8,128)(2,1)S(1)}, bf16[256,576]{0,1:T(8,128)(2,1)}, u32[]{:S(2)}) copy-start(bf16[256,576]{0,1:T(8,128)(2,1)} %copy-done.8) | copy-start | bytes 884740
  230.4 8.0 %collective-permute-start.15 = (bf16[256,576]{0,1:T(8,128)(2,1)S(1)}, bf16[256,576]{0,1:T(8,128)(2,1)S(1)}, u32[]{:S(2)}, u32[]{:S(2)}) collective-permute-start(bf16[256,576]{0,1:T(8,128)(2,1)S(1)} %fusion.94), channel_id=1, source_target_pairs={{0,96},{32,0},{64,32},{96,64},{1,97},{33,1},{65,33},{97,65},{2,98}... | collective-permute-start | bytes 884744 | tf_op jit(solution)/shard_map/ppermute | solution.py:14
  232.8 12.8 %collective-permute-start.11 = (bf16[256,576]{0,1:T(8,128)(2,1)S(1)}, bf16[256,576]{0,1:T(8,128)(2,1)S(1)}, u32[]{:S(2)}, u32[]{:S(2)}) collective-permute-start(bf16[256,576]{0,1:T(8,128)(2,1)S(1)} %fusion.73), channel_id=1, source_target_pairs={{0,32},{32,64},{64,96},{96,0},{1,33},{33,65},{65,97},{97,1},{2,34}... | collective-permute-start | bytes 884744 | tf_op jit(solution)/shard_map/ppermute | solution.py:14
  232.8 12.8 %collective-permute-start.12 = (bf16[256,576]{0,1:T(8,128)(2,1)S(1)}, bf16[256,576]{0,1:T(8,128)(2,1)S(1)}, u32[]{:S(2)}, u32[]{:S(2)}) collective-permute-start(bf16[256,576]{0,1:T(8,128)(2,1)S(1)} %fusion.79), channel_id=1, source_target_pairs={{0,96},{32,0},{64,32},{96,64},{1,97},{33,1},{65,33},{97,65},{2,98}... | collective-permute-start | bytes 884744 | tf_op jit(solution)/shard_map/ppermute | solution.py:14
  238.0 12.0 %collective-permute-start.10 = (bf16[256,576]{0,1:T(8,128)(2,1)S(1)}, bf16[256,576]{0,1:T(8,128)(2,1)S(1)}, u32[]{:S(2)}, u32[]{:S(2)}) collective-permute-start(bf16[256,576]{0,1:T(8,128)(2,1)S(1)} %fusion.67), channel_id=1, source_target_pairs={{0,64},{32,96},{64,0},{96,32},{1,65},{33,97},{65,1},{97,33},{2,66}... | collective-permute-start | bytes 884744 | tf_op jit(solution)/shard_map/ppermute | solution.py:14
  238.5 13.6 %copy-start.11 = (bf16[256,576]{0,1:T(8,128)(2,1)}, bf16[256,576]{0,1:T(8,128)(2,1)S(1)}, u32[]{:S(2)}) copy-start(bf16[256,576]{0,1:T(8,128)(2,1)S(1)} %add_convert_fusion) | copy-start | bytes 884740
  238.5 11.5 %collective-permute-start.16 = (bf16[256,576]{0,1:T(8,128)(2,1)S(1)}, bf16[256,576]{0,1:T(8,128)(2,1)S(1)}, u32[]{:S(2)}, u32[]{:S(2)}) collective-permute-start(bf16[256,576]{0,1:T(8,128)(2,1)S(1)} %add_convert_fusion), channel_id=1, source_target_pairs={{0,128},{1,129},{2,130},{3,131},{4,132},{5,133},{6,134},{7,135},{8... | collective-permute-start | bytes 884744 | tf_op jit(solution)/shard_map/ppermute | solution.py:116
Sparse Core Ops, SparseCore 0:
  10.5 106.2 all-gather.4
  119.4 100.2 all-gather.6
